TPU v7x, 1024 devices: a whole 4x8x16 slice. The times are simulated.
1024 devices in a mesh: segment: 8 (over y), ctx: 16 (over z), tp: 8 (over x, core).
Axes of the slice: x: 4, y: 8, z: 16, core: 2. Of those that a mesh axis runs over, the one named last changes fastest.
Arguments:
- query: bfloat16 [8, 2048, 8192], P('segment', 'ctx', 'tp'), may hold values from -150 to 150
- keys: bfloat16 [8, 2048, 1024], P('segment', 'ctx', 'tp'), may hold values from -6 to 6
- values: bfloat16 [8, 2048, 1024], P('segment', 'ctx', 'tp'), may hold values from -6 to 6
- attn_out: bfloat16 [8, 2048, 8192], P('segment', 'ctx', 'tp'), may hold values from -4 to 4
- grad_out: bfloat16 [8, 2048, 8192], P('segment', ('ctx', 'tp')), may hold values from -6 to 6
- block_of: int32 [8, 32], P('segment'), may hold values from 0 to 31, each once within a row
Outputs:
- grad_query: bfloat16 [8, 2048, 8192], P('segment', 'ctx', 'tp')
- grad_keys: bfloat16 [8, 2048, 1024], P('segment', 'ctx', 'tp')
- grad_values: bfloat16 [8, 2048, 1024], P('segment', 'ctx', 'tp')
All inputs are finite; a program needn't handle non-finite values.
Results may differ from a plain program's by a relative error of at most 0.0055.
Values may be sent and summed in bfloat16 or wider, within the bound.
No kernel may reach another device: no remote copies, remote signals or barrier semaphores. Data moves between devices by JAX's collectives and lax.ppermute only.
A program may use at most 32 MiB of HBM per device.

v0:
```python
import jax
import jax.numpy as jnp
from jax import lax
from jax.sharding import PartitionSpec as P

HEAD_DIM = 128


def passed_along(value, axis, steps):
    count = lax.axis_size(axis)
    pairs = [(source, (source + steps) % count) for source in range(count)]
    return lax.ppermute(value, axis, pairs)


def body(query, keys, values, attn_out, grad_out, block_of):
    rows = query.shape[1]
    kv_width = keys.shape[2]
    head_dim = HEAD_DIM
    groups = kv_width // head_dim
    heads = query.shape[2] // head_dim
    per = heads // groups
    scale = head_dim ** (-0.5)
    half = rows // 2
    order = block_of[0]
    count = lax.axis_size("ctx")
    me = lax.axis_index("ctx")
    handed = passed_along(grad_out[0], "segment", -1)
    incoming = lax.all_to_all(handed, "tp", split_axis=1, concat_axis=0, tiled=True)
    q_local = query[0].reshape(rows, groups, per, head_dim)
    do_local = incoming.reshape(rows, groups, per, head_dim)
    delta = jnp.sum(
        attn_out[0].reshape(rows, groups, per, head_dim).astype(jnp.float32)
        * do_local.astype(jnp.float32),
        axis=-1,
    )
    delta = jnp.transpose(delta, (1, 2, 0))

    def place(first, length):
        index = first + jnp.arange(length, dtype=jnp.int32)
        table = (index // half)[:, None] == jnp.arange(order.shape[0], dtype=jnp.int32)[None, :]
        return jnp.sum(jnp.where(table, order[None, :], 0), axis=1) * half + index % half

    q_pos = place(me * rows, rows)

    def block_scores(k_block, k_pos):
        length = k_block.shape[0]
        k_three = k_block.reshape(length, groups, head_dim)
        scores = scale * jnp.einsum(
            "iged,jgd->geij", q_local, k_three, preferred_element_type=jnp.float32
        )
        allowed = k_pos[None, :] <= q_pos[:, None]
        return (scores, allowed)

    def block_grads(k_block, v_block, k_pos, lse):
        length = k_block.shape[0]
        scores, allowed = block_scores(k_block, k_pos)
        prob = jnp.where(allowed, jnp.exp(scores - lse[..., None]), 0.0)
        prob_b = prob.astype(jnp.bfloat16)
        v_three = v_block.reshape(length, groups, head_dim)
        k_three = k_block.reshape(length, groups, head_dim)
        dvalue = jnp.einsum("geij,iged->jgd", prob_b, do_local, preferred_element_type=jnp.float32)
        dprob = jnp.einsum("iged,jgd->geij", do_local, v_three, preferred_element_type=jnp.float32)
        dscore = (prob * (dprob - delta[..., None])).astype(jnp.bfloat16)
        dquery = jnp.einsum("geij,jgd->iged", dscore, k_three, preferred_element_type=jnp.float32)
        dkey = jnp.einsum("geij,iged->jgd", dscore, q_local, preferred_element_type=jnp.float32)
        return (dquery, dkey.reshape(length, kv_width), dvalue.reshape(length, kv_width))

    def guarded(k_block, v_block, k_pos, lse):
        length = k_block.shape[0]
        live = jnp.min(k_pos) <= jnp.max(q_pos)
        blank = (
            jnp.zeros((rows, groups, per, head_dim), jnp.float32),
            jnp.zeros((length, kv_width), jnp.float32),
            jnp.zeros((length, kv_width), jnp.float32),
        )
        return lax.cond(live, lambda: block_grads(k_block, v_block, k_pos, lse), lambda: blank)

    dq_zero = jnp.zeros((rows, groups, per, head_dim), jnp.float32)
    piece = lax.all_gather(keys[0], "ctx", axis=0, tiled=True)
    top_old = jnp.full((groups, per, rows), -1e30, jnp.float32)
    scores, allowed = block_scores(piece, place(jnp.int32(0), piece.shape[0]))
    top_new = jnp.maximum(top_old, jnp.max(jnp.where(allowed, scores, -1e30), axis=-1))
    terms = jnp.where(allowed, jnp.exp(scores - top_new[..., None]), 0.0)
    total_final = jnp.sum(terms, axis=-1)
    lse = top_new + jnp.log(total_final)

    def cycle_turn(step, state):
        k_block, v_block, dkey, dvalue, dquery = state
        source = (me - step) % count
        dq_add, dk_add, dv_add = guarded(k_block, v_block, place(source * rows, rows), lse)
        k_block, v_block = passed_along((k_block, v_block), "ctx", 1)
        dkey, dvalue = passed_along((dkey + dk_add, dvalue + dv_add), "ctx", 1)
        return (k_block, v_block, dkey, dvalue, dquery + dq_add)

    zero_kv = jnp.zeros((rows, kv_width), jnp.float32)
    state = lax.fori_loop(0, count, cycle_turn, (keys[0], values[0], zero_kv, zero_kv, dq_zero))
    dkey, dvalue, dquery = (state[2], state[3], state[4])
    grad_query = (scale * dquery).reshape(rows, heads * head_dim).astype(jnp.bfloat16)[None]
    grad_keys = (scale * dkey).astype(jnp.bfloat16)[None]
    grad_values = dvalue.astype(jnp.bfloat16)[None]
    return (grad_query, grad_keys, grad_values)


def solution(mesh):
    return jax.shard_map(
        body,
        mesh=mesh,
        in_specs=(
            P("segment", "ctx", "tp"),
            P("segment", "ctx", "tp"),
            P("segment", "ctx", "tp"),
            P("segment", "ctx", "tp"),
            P("segment", ("ctx", "tp"), None),
            P("segment", None),
        ),
        out_specs=(P("segment", "ctx", "tp"), P("segment", "ctx", "tp"), P("segment", "ctx", "tp")),
        check_vma=False,
    )
```

profile of v0, /device:TPU:6, one launch (start us, length us, event | category | flops | bytes accessed | tf_op | source)
XLA Modules:
  0.0 433.8 jit_solution(4099003233318565145)
XLA Ops:
  1.4 5.4 %collective-permute-start.4 = (bf16[16,8192]{1,0:T(8,128)(2,1)}, bf16[16,8192]{1,0:T(8,128)(2,1)S(1)}, u32[]{:S(2)}, u32[]{:S(2)}) collective-permute-start(bf16[16,8192]{1,0:T(8,128)(2,1)} %bitcast.130), channel_id=1, source_target_pairs={{0,896},{128,0},{256,128},{384,256},{512,384},{640,512},{768,640},... | collective-permute-start | bytes 786440 | tf_op jit(solution)/shard_map/ppermute | solution.py:12
  9.0 45.2 %all-gather = bf16[1,2048,128]{2,1,0:T(8,128)(2,1)S(1)} all-gather(bf16[1,128,128]{2,1,0:T(8,128)(2,1)S(1)} %copy.77), channel_id=2, replica_groups=mesh['segment'=8,'ctx'=16,'tp'=8] {'ctx'}, dimensions={1}, use_global_device_ids=true | all-gather | bytes 557056 | tf_op jit(solution)/shard_map/all_gather | solution.py:79
  55.5 4.6 %fusion.18 = (f32[8,128]{1,0:T(8,128)S(1)}, f32[2048,128,8]{1,0,2:T(8,128)}) fusion(pred[128,2048]{0,1:T(8,128)(4,1)S(1)} %broadcast_compare_fusion.1, bf16[128,8,128]{2,1,0:T(8,128)(2,1)S(1)} %bitcast.116, bf16[1,2048,128]{2,1,0:T(8,128)(2,1)S(1)} %all-gather), kind=kOutput, calls=%fused_computation.35 | convolution fusion | flops 543161344 | bytes 9441280 | tf_op jit(solution)/shard_map/iged,jgd->geij/dot_general | solution.py:48
  60.9 4.8 %all-to-all-start = ((bf16[16,8,1024]{2,0,1:T(8,128)(2,1)}), bf16[16,8,1024]{2,0,1:T(8,128)(2,1)S(1)}, u32[]{:S(2)}, u32[]{:S(2)}) async-start(bf16[16,8,1024]{2,0,1:T(8,128)(2,1)} %bitcast.111), calls=%async_computation | async-start | bytes 524288 | tf_op jit(solution)/shard_map/all_to_all | solution.py:28
  65.6 5.1 %fusion.21 = f32[8,128]{1,0:T(8,128)S(1)} fusion(f32[2048,128,8]{1,0,2:T(8,128)} %get-tuple-element.518, f32[8,128]{1,0:T(8,128)S(1)} %broadcast_maximum_fusion, pred[128,2048]{0,1:T(8,128)(4,1)S(1)} %broadcast_compare_fusion.1), kind=kLoop, calls=%fused_computation.38 | loop fusion | flops 8387584 | bytes 8658944 | tf_op jit(solution)/shard_map/reduce_sum | solution.py:84
  71.9 360.1 %while.25 = (s32[]{:T(128)}, bf16[128,128]{1,0:T(8,128)(2,1)S(1)}, bf16[128,128]{1,0:T(8,128)(2,1)S(1)}, f32[128,128]{1,0:T(8,128)S(1)}, f32[128,128]{1,0:T(8,12...) while((s32[]{:T(128)}, bf16[128,128]{1,0:T(8,128)(2,1)S(1)}, ...), condition=%wide.region_11.12_spmd.clone, body=%wide.region_6.11_spmd.clone.sunk | while | flops 169017104 | bytes 7090382 | solution.py:96
  75.1 2.7 collective-permute-start.1
  79.9 3.6 conditional.3
  85.4 3.9 collective-permute-start.3
  93.4 2.7 collective-permute-start
  100.8 6.2 %collective-permute-start.2 = (f32[128,128]{1,0:T(8,128)S(1)}, f32[128,128]{1,0:T(8,128)S(1)}, u32[]{:S(2)}, u32[]{:S(2)}) collective-permute-start(f32[128,128]{1,0:T(8,128)S(1)} %add.306), channel_id=1, source_target_pairs={{0,8},{8,16},{16,24},{24,32},{32,40},{40,48},{48,56},{56,64},{64,7... | collective-permute-start | bytes 196616 | tf_op jit(solution)/shard_map/while/body/eval_jaxpr/ppermute | solution.py:12
  107.1 3.4 collective-permute-start.3
  111.7 2.7 collective-permute-done.3
  117.9 3.2 collective-permute-start.1
  125.2 8.5 %collective-permute-start.3 = (f32[128,128]{1,0:T(8,128)S(1)}, f32[128,128]{1,0:T(8,128)S(1)}, u32[]{:S(2)}, u32[]{:S(2)}) collective-permute-start(f32[128,128]{1,0:T(8,128)S(1)} %add.307), channel_id=1, source_target_pairs={{0,8},{8,16},{16,24},{24,32},{32,40},{40,48},{48,56},{56,64},{64,7... | collective-permute-start | bytes 196616 | tf_op jit(solution)/shard_map/while/body/eval_jaxpr/ppermute | solution.py:12
  136.2 4.3 collective-permute-start
  141.1 3.5 collective-permute-start.1
  146.6 3.6 conditional.3
  154.3 3.3 collective-permute-done.2
  160.2 2.6 collective-permute-start
  163.4 4.4 %collective-permute-start.1 = (bf16[128,128]{1,0:T(8,128)(2,1)}, bf16[128,128]{1,0:T(8,128)(2,1)S(1)}, u32[]{:S(2)}, u32[]{:S(2)}) collective-permute-start(bf16[128,128]{1,0:T(8,128)(2,1)} %copy.65), channel_id=1, source_target_pairs={{0,8},{8,16},{16,24},{24,32},{32,40},{40,48},{48,56},{56,64},{64,7... | collective-permute-start | bytes 98312 | tf_op jit(solution)/shard_map/while/body/eval_jaxpr/ppermute | solution.py:12
  169.8 3.6 conditional.3
  173.5 3.0 collective-permute-start.2
  178.6 2.2 collective-permute-done.2
  180.8 3.1 collective-permute-done.3
  191.0 3.6 conditional.3
  194.7 2.6 collective-permute-start.2
  197.3 5.5 %collective-permute-start.3 = (f32[128,128]{1,0:T(8,128)S(1)}, f32[128,128]{1,0:T(8,128)S(1)}, u32[]{:S(2)}, u32[]{:S(2)}) collective-permute-start(f32[128,128]{1,0:T(8,128)S(1)} %add.307), channel_id=1, source_target_pairs={{0,8},{8,16},{16,24},{24,32},{32,40},{40,48},{48,56},{56,64},{64,7... | collective-permute-start | bytes 196616 | tf_op jit(solution)/shard_map/while/body/eval_jaxpr/ppermute | solution.py:12
  205.3 4.2 collective-permute-start
  214.1 3.6 conditional.3
  219.7 4.4 %collective-permute-start.3 = (f32[128,128]{1,0:T(8,128)S(1)}, f32[128,128]{1,0:T(8,128)S(1)}, u32[]{:S(2)}, u32[]{:S(2)}) collective-permute-start(f32[128,128]{1,0:T(8,128)S(1)} %add.307), channel_id=1, source_target_pairs={{0,8},{8,16},{16,24},{24,32},{32,40},{40,48},{48,56},{56,64},{64,7... | collective-permute-start | bytes 196616 | tf_op jit(solution)/shard_map/while/body/eval_jaxpr/ppermute | solution.py:12
  227.7 3.2 collective-permute-start
  235.7 3.6 conditional.3
  241.3 4.1 collective-permute-start.3
  249.3 3.0 collective-permute-start
  252.9 4.3 collective-permute-start.1
  259.2 3.6 conditional.3
  264.8 3.1 collective-permute-start.3
  275.3 4.0 collective-permute-start.1
  281.4 3.6 conditional.3
  285.0 3.3 collective-permute-start.2
  288.3 5.6 %collective-permute-start.3 = (f32[128,128]{1,0:T(8,128)S(1)}, f32[128,128]{1,0:T(8,128)S(1)}, u32[]{:S(2)}, u32[]{:S(2)}) collective-permute-start(f32[128,128]{1,0:T(8,128)S(1)} %add.307), channel_id=1, source_target_pairs={{0,8},{8,16},{16,24},{24,32},{32,40},{40,48},{48,56},{56,64},{64,7... | collective-permute-start | bytes 196616 | tf_op jit(solution)/shard_map/while/body/eval_jaxpr/ppermute | solution.py:12
  296.5 4.2 collective-permute-start
  301.3 2.2 collective-permute-start.1
  305.6 5.4 %collective-permute-start.2 = (f32[128,128]{1,0:T(8,128)S(1)}, f32[128,128]{1,0:T(8,128)S(1)}, u32[]{:S(2)}, u32[]{:S(2)}) collective-permute-start(f32[128,128]{1,0:T(8,128)S(1)} %add.306), channel_id=1, source_target_pairs={{0,8},{8,16},{16,24},{24,32},{32,40},{40,48},{48,56},{56,64},{64,7... | collective-permute-start | bytes 196616 | tf_op jit(solution)/shard_map/while/body/eval_jaxpr/ppermute | solution.py:12
  311.1 3.5 collective-permute-start.3
  316.4 2.5 collective-permute-done.3
  322.1 3.9 collective-permute-start.1
  328.0 3.6 conditional.3
  333.6 4.0 collective-permute-start.3
  341.6 2.8 collective-permute-start
  345.0 3.0 collective-permute-start.1
  350.1 3.6 conditional.3
  357.8 3.3 collective-permute-done.2
  366.2 2.6 collective-permute-start.1
  370.8 3.6 conditional.3
  376.4 5.5 %collective-permute-start.3 = (f32[128,128]{1,0:T(8,128)S(1)}, f32[128,128]{1,0:T(8,128)S(1)}, u32[]{:S(2)}, u32[]{:S(2)}) collective-permute-start(f32[128,128]{1,0:T(8,128)S(1)} %add.307), channel_id=1, source_target_pairs={{0,8},{8,16},{16,24},{24,32},{32,40},{40,48},{48,56},{56,64},{64,7... | collective-permute-start | bytes 196616 | tf_op jit(solution)/shard_map/while/body/eval_jaxpr/ppermute | solution.py:12
  384.3 4.2 collective-permute-start
  393.2 3.6 conditional.3
  398.8 7.2 %collective-permute-start.3 = (f32[128,128]{1,0:T(8,128)S(1)}, f32[128,128]{1,0:T(8,128)S(1)}, u32[]{:S(2)}, u32[]{:S(2)}) collective-permute-start(f32[128,128]{1,0:T(8,128)S(1)} %add.307), channel_id=1, source_target_pairs={{0,8},{8,16},{16,24},{24,32},{32,40},{40,48},{48,56},{56,64},{64,7... | collective-permute-start | bytes 196616 | tf_op jit(solution)/shard_map/while/body/eval_jaxpr/ppermute | solution.py:12
  408.5 4.3 collective-permute-start
  413.4 3.7 collective-permute-start.1
  419.1 3.6 conditional.3
  424.7 3.9 collective-permute-start.3
  (338 shorter events, 172.0 us)
Async XLA Ops:
  1.4 58.7 %collective-permute-start.4 = (bf16[16,8192]{1,0:T(8,128)(2,1)}, bf16[16,8192]{1,0:T(8,128)(2,1)S(1)}, u32[]{:S(2)}, u32[]{:S(2)}) collective-permute-start(bf16[16,8192]{1,0:T(8,128)(2,1)} %bitcast.130), channel_id=1, source_target_pairs={{0,896},{128,0},{256,128},{384,256},{512,384},{640,512},{768,640},... | collective-permute-start | bytes 786440 | tf_op jit(solution)/shard_map/ppermute | solution.py:12
  60.9 10.7 %all-to-all-start = ((bf16[16,8,1024]{2,0,1:T(8,128)(2,1)}), bf16[16,8,1024]{2,0,1:T(8,128)(2,1)S(1)}, u32[]{:S(2)}, u32[]{:S(2)}) async-start(bf16[16,8,1024]{2,0,1:T(8,128)(2,1)} %bitcast.111), calls=%async_computation | async-start | bytes 524288 | tf_op jit(solution)/shard_map/all_to_all | solution.py:28
  72.6 17.0 %collective-permute-start = (bf16[128,128]{1,0:T(8,128)(2,1)}, bf16[128,128]{1,0:T(8,128)(2,1)S(1)}, u32[]{:S(2)}, u32[]{:S(2)}) collective-permute-start(bf16[128,128]{1,0:T(8,128)(2,1)} %copy.64), channel_id=1, source_target_pairs={{0,8},{8,16},{16,24},{24,32},{32,40},{40,48},{48,56},{56,64},{64,7... | collective-permute-start | bytes 98312 | tf_op jit(solution)/shard_map/while/body/eval_jaxpr/ppermute | solution.py:12
  75.1 14.5 %collective-permute-start.1 = (bf16[128,128]{1,0:T(8,128)(2,1)}, bf16[128,128]{1,0:T(8,128)(2,1)S(1)}, u32[]{:S(2)}, u32[]{:S(2)}) collective-permute-start(bf16[128,128]{1,0:T(8,128)(2,1)} %copy.65), channel_id=1, source_target_pairs={{0,8},{8,16},{16,24},{24,32},{32,40},{40,48},{48,56},{56,64},{64,7... | collective-permute-start | bytes 98312 | tf_op jit(solution)/shard_map/while/body/eval_jaxpr/ppermute | solution.py:12
  83.5 7.5 %collective-permute-start.2 = (f32[128,128]{1,0:T(8,128)S(1)}, f32[128,128]{1,0:T(8,128)S(1)}, u32[]{:S(2)}, u32[]{:S(2)}) collective-permute-start(f32[128,128]{1,0:T(8,128)S(1)} %add.306), channel_id=1, source_target_pairs={{0,8},{8,16},{16,24},{24,32},{32,40},{40,48},{48,56},{56,64},{64,7... | collective-permute-start | bytes 196616 | tf_op jit(solution)/shard_map/while/body/eval_jaxpr/ppermute | solution.py:12
  85.4 7.4 %collective-permute-start.3 = (f32[128,128]{1,0:T(8,128)S(1)}, f32[128,128]{1,0:T(8,128)S(1)}, u32[]{:S(2)}, u32[]{:S(2)}) collective-permute-start(f32[128,128]{1,0:T(8,128)S(1)} %add.307), channel_id=1, source_target_pairs={{0,8},{8,16},{16,24},{24,32},{32,40},{40,48},{48,56},{56,64},{64,7... | collective-permute-start | bytes 196616 | tf_op jit(solution)/shard_map/while/body/eval_jaxpr/ppermute | solution.py:12
  93.4 17.2 %collective-permute-start = (bf16[128,128]{1,0:T(8,128)(2,1)}, bf16[128,128]{1,0:T(8,128)(2,1)S(1)}, u32[]{:S(2)}, u32[]{:S(2)}) collective-permute-start(bf16[128,128]{1,0:T(8,128)(2,1)} %copy.64), channel_id=1, source_target_pairs={{0,8},{8,16},{16,24},{24,32},{32,40},{40,48},{48,56},{56,64},{64,7... | collective-permute-start | bytes 98312 | tf_op jit(solution)/shard_map/while/body/eval_jaxpr/ppermute | solution.py:12
  96.8 13.9 %collective-permute-start.1 = (bf16[128,128]{1,0:T(8,128)(2,1)}, bf16[128,128]{1,0:T(8,128)(2,1)S(1)}, u32[]{:S(2)}, u32[]{:S(2)}) collective-permute-start(bf16[128,128]{1,0:T(8,128)(2,1)} %copy.65), channel_id=1, source_target_pairs={{0,8},{8,16},{16,24},{24,32},{32,40},{40,48},{48,56},{56,64},{64,7... | collective-permute-start | bytes 98312 | tf_op jit(solution)/shard_map/while/body/eval_jaxpr/ppermute | solution.py:12
  100.8 10.9 %collective-permute-start.2 = (f32[128,128]{1,0:T(8,128)S(1)}, f32[128,128]{1,0:T(8,128)S(1)}, u32[]{:S(2)}, u32[]{:S(2)}) collective-permute-start(f32[128,128]{1,0:T(8,128)S(1)} %add.306), channel_id=1, source_target_pairs={{0,8},{8,16},{16,24},{24,32},{32,40},{40,48},{48,56},{56,64},{64,7... | collective-permute-start | bytes 196616 | tf_op jit(solution)/shard_map/while/body/eval_jaxpr/ppermute | solution.py:12
  107.1 7.4 %collective-permute-start.3 = (f32[128,128]{1,0:T(8,128)S(1)}, f32[128,128]{1,0:T(8,128)S(1)}, u32[]{:S(2)}, u32[]{:S(2)}) collective-permute-start(f32[128,128]{1,0:T(8,128)S(1)} %add.307), channel_id=1, source_target_pairs={{0,8},{8,16},{16,24},{24,32},{32,40},{40,48},{48,56},{56,64},{64,7... | collective-permute-start | bytes 196616 | tf_op jit(solution)/shard_map/while/body/eval_jaxpr/ppermute | solution.py:12
  115.1 18.8 %collective-permute-start = (bf16[128,128]{1,0:T(8,128)(2,1)}, bf16[128,128]{1,0:T(8,128)(2,1)S(1)}, u32[]{:S(2)}, u32[]{:S(2)}) collective-permute-start(bf16[128,128]{1,0:T(8,128)(2,1)} %copy.64), channel_id=1, source_target_pairs={{0,8},{8,16},{16,24},{24,32},{32,40},{40,48},{48,56},{56,64},{64,7... | collective-permute-start | bytes 98312 | tf_op jit(solution)/shard_map/while/body/eval_jaxpr/ppermute | solution.py:12
  117.9 16.0 %collective-permute-start.1 = (bf16[128,128]{1,0:T(8,128)(2,1)}, bf16[128,128]{1,0:T(8,128)(2,1)S(1)}, u32[]{:S(2)}, u32[]{:S(2)}) collective-permute-start(bf16[128,128]{1,0:T(8,128)(2,1)} %copy.65), channel_id=1, source_target_pairs={{0,8},{8,16},{16,24},{24,32},{32,40},{40,48},{48,56},{56,64},{64,7... | collective-permute-start | bytes 98312 | tf_op jit(solution)/shard_map/while/body/eval_jaxpr/ppermute | solution.py:12
  123.2 10.7 %collective-permute-start.2 = (f32[128,128]{1,0:T(8,128)S(1)}, f32[128,128]{1,0:T(8,128)S(1)}, u32[]{:S(2)}, u32[]{:S(2)}) collective-permute-start(f32[128,128]{1,0:T(8,128)S(1)} %add.306), channel_id=1, source_target_pairs={{0,8},{8,16},{16,24},{24,32},{32,40},{40,48},{48,56},{56,64},{64,7... | collective-permute-start | bytes 196616 | tf_op jit(solution)/shard_map/while/body/eval_jaxpr/ppermute | solution.py:12
  125.2 10.4 %collective-permute-start.3 = (f32[128,128]{1,0:T(8,128)S(1)}, f32[128,128]{1,0:T(8,128)S(1)}, u32[]{:S(2)}, u32[]{:S(2)}) collective-permute-start(f32[128,128]{1,0:T(8,128)S(1)} %add.307), channel_id=1, source_target_pairs={{0,8},{8,16},{16,24},{24,32},{32,40},{40,48},{48,56},{56,64},{64,7... | collective-permute-start | bytes 196616 | tf_op jit(solution)/shard_map/while/body/eval_jaxpr/ppermute | solution.py:12
  136.2 18.1 %collective-permute-start = (bf16[128,128]{1,0:T(8,128)(2,1)}, bf16[128,128]{1,0:T(8,128)(2,1)S(1)}, u32[]{:S(2)}, u32[]{:S(2)}) collective-permute-start(bf16[128,128]{1,0:T(8,128)(2,1)} %copy.64), channel_id=1, source_target_pairs={{0,8},{8,16},{16,24},{24,32},{32,40},{40,48},{48,56},{56,64},{64,7... | collective-permute-start | bytes 98312 | tf_op jit(solution)/shard_map/while/body/eval_jaxpr/ppermute | solution.py:12
  141.1 13.2 %collective-permute-start.1 = (bf16[128,128]{1,0:T(8,128)(2,1)}, bf16[128,128]{1,0:T(8,128)(2,1)S(1)}, u32[]{:S(2)}, u32[]{:S(2)}) collective-permute-start(bf16[128,128]{1,0:T(8,128)(2,1)} %copy.65), channel_id=1, source_target_pairs={{0,8},{8,16},{16,24},{24,32},{32,40},{40,48},{48,56},{56,64},{64,7... | collective-permute-start | bytes 98312 | tf_op jit(solution)/shard_map/while/body/eval_jaxpr/ppermute | solution.py:12
  150.2 7.4 %collective-permute-start.2 = (f32[128,128]{1,0:T(8,128)S(1)}, f32[128,128]{1,0:T(8,128)S(1)}, u32[]{:S(2)}, u32[]{:S(2)}) collective-permute-start(f32[128,128]{1,0:T(8,128)S(1)} %add.306), channel_id=1, source_target_pairs={{0,8},{8,16},{16,24},{24,32},{32,40},{40,48},{48,56},{56,64},{64,7... | collective-permute-start | bytes 196616 | tf_op jit(solution)/shard_map/while/body/eval_jaxpr/ppermute | solution.py:12
  152.2 7.4 %collective-permute-start.3 = (f32[128,128]{1,0:T(8,128)S(1)}, f32[128,128]{1,0:T(8,128)S(1)}, u32[]{:S(2)}, u32[]{:S(2)}) collective-permute-start(f32[128,128]{1,0:T(8,128)S(1)} %add.307), channel_id=1, source_target_pairs={{0,8},{8,16},{16,24},{24,32},{32,40},{40,48},{48,56},{56,64},{64,7... | collective-permute-start | bytes 196616 | tf_op jit(solution)/shard_map/while/body/eval_jaxpr/ppermute | solution.py:12
  160.2 18.4 %collective-permute-start = (bf16[128,128]{1,0:T(8,128)(2,1)}, bf16[128,128]{1,0:T(8,128)(2,1)S(1)}, u32[]{:S(2)}, u32[]{:S(2)}) collective-permute-start(bf16[128,128]{1,0:T(8,128)(2,1)} %copy.64), channel_id=1, source_target_pairs={{0,8},{8,16},{16,24},{24,32},{32,40},{40,48},{48,56},{56,64},{64,7... | collective-permute-start | bytes 98312 | tf_op jit(solution)/shard_map/while/body/eval_jaxpr/ppermute | solution.py:12
  163.4 15.2 %collective-permute-start.1 = (bf16[128,128]{1,0:T(8,128)(2,1)}, bf16[128,128]{1,0:T(8,128)(2,1)S(1)}, u32[]{:S(2)}, u32[]{:S(2)}) collective-permute-start(bf16[128,128]{1,0:T(8,128)(2,1)} %copy.65), channel_id=1, source_target_pairs={{0,8},{8,16},{16,24},{24,32},{32,40},{40,48},{48,56},{56,64},{64,7... | collective-permute-start | bytes 98312 | tf_op jit(solution)/shard_map/while/body/eval_jaxpr/ppermute | solution.py:12
  173.5 7.4 %collective-permute-start.2 = (f32[128,128]{1,0:T(8,128)S(1)}, f32[128,128]{1,0:T(8,128)S(1)}, u32[]{:S(2)}, u32[]{:S(2)}) collective-permute-start(f32[128,128]{1,0:T(8,128)S(1)} %add.306), channel_id=1, source_target_pairs={{0,8},{8,16},{16,24},{24,32},{32,40},{40,48},{48,56},{56,64},{64,7... | collective-permute-start | bytes 196616 | tf_op jit(solution)/shard_map/while/body/eval_jaxpr/ppermute | solution.py:12
  176.5 7.5 %collective-permute-start.3 = (f32[128,128]{1,0:T(8,128)S(1)}, f32[128,128]{1,0:T(8,128)S(1)}, u32[]{:S(2)}, u32[]{:S(2)}) collective-permute-start(f32[128,128]{1,0:T(8,128)S(1)} %add.307), channel_id=1, source_target_pairs={{0,8},{8,16},{16,24},{24,32},{32,40},{40,48},{48,56},{56,64},{64,7... | collective-permute-start | bytes 196616 | tf_op jit(solution)/shard_map/while/body/eval_jaxpr/ppermute | solution.py:12
  184.5 18.4 %collective-permute-start = (bf16[128,128]{1,0:T(8,128)(2,1)}, bf16[128,128]{1,0:T(8,128)(2,1)S(1)}, u32[]{:S(2)}, u32[]{:S(2)}) collective-permute-start(bf16[128,128]{1,0:T(8,128)(2,1)} %copy.64), channel_id=1, source_target_pairs={{0,8},{8,16},{16,24},{24,32},{32,40},{40,48},{48,56},{56,64},{64,7... | collective-permute-start | bytes 98312 | tf_op jit(solution)/shard_map/while/body/eval_jaxpr/ppermute | solution.py:12
  187.1 15.9 %collective-permute-start.1 = (bf16[128,128]{1,0:T(8,128)(2,1)}, bf16[128,128]{1,0:T(8,128)(2,1)S(1)}, u32[]{:S(2)}, u32[]{:S(2)}) collective-permute-start(bf16[128,128]{1,0:T(8,128)(2,1)} %copy.65), channel_id=1, source_target_pairs={{0,8},{8,16},{16,24},{24,32},{32,40},{40,48},{48,56},{56,64},{64,7... | collective-permute-start | bytes 98312 | tf_op jit(solution)/shard_map/while/body/eval_jaxpr/ppermute | solution.py:12
  194.7 8.3 %collective-permute-start.2 = (f32[128,128]{1,0:T(8,128)S(1)}, f32[128,128]{1,0:T(8,128)S(1)}, u32[]{:S(2)}, u32[]{:S(2)}) collective-permute-start(f32[128,128]{1,0:T(8,128)S(1)} %add.306), channel_id=1, source_target_pairs={{0,8},{8,16},{16,24},{24,32},{32,40},{40,48},{48,56},{56,64},{64,7... | collective-permute-start | bytes 196616 | tf_op jit(solution)/shard_map/while/body/eval_jaxpr/ppermute | solution.py:12
  197.3 7.4 %collective-permute-start.3 = (f32[128,128]{1,0:T(8,128)S(1)}, f32[128,128]{1,0:T(8,128)S(1)}, u32[]{:S(2)}, u32[]{:S(2)}) collective-permute-start(f32[128,128]{1,0:T(8,128)S(1)} %add.307), channel_id=1, source_target_pairs={{0,8},{8,16},{16,24},{24,32},{32,40},{40,48},{48,56},{56,64},{64,7... | collective-permute-start | bytes 196616 | tf_op jit(solution)/shard_map/while/body/eval_jaxpr/ppermute | solution.py:12
  205.3 19.0 %collective-permute-start = (bf16[128,128]{1,0:T(8,128)(2,1)}, bf16[128,128]{1,0:T(8,128)(2,1)S(1)}, u32[]{:S(2)}, u32[]{:S(2)}) collective-permute-start(bf16[128,128]{1,0:T(8,128)(2,1)} %copy.64), channel_id=1, source_target_pairs={{0,8},{8,16},{16,24},{24,32},{32,40},{40,48},{48,56},{56,64},{64,7... | collective-permute-start | bytes 98312 | tf_op jit(solution)/shard_map/while/body/eval_jaxpr/ppermute | solution.py:12
  210.2 14.1 %collective-permute-start.1 = (bf16[128,128]{1,0:T(8,128)(2,1)}, bf16[128,128]{1,0:T(8,128)(2,1)S(1)}, u32[]{:S(2)}, u32[]{:S(2)}) collective-permute-start(bf16[128,128]{1,0:T(8,128)(2,1)} %copy.65), channel_id=1, source_target_pairs={{0,8},{8,16},{16,24},{24,32},{32,40},{40,48},{48,56},{56,64},{64,7... | collective-permute-start | bytes 98312 | tf_op jit(solution)/shard_map/while/body/eval_jaxpr/ppermute | solution.py:12
  217.8 7.4 %collective-permute-start.2 = (f32[128,128]{1,0:T(8,128)S(1)}, f32[128,128]{1,0:T(8,128)S(1)}, u32[]{:S(2)}, u32[]{:S(2)}) collective-permute-start(f32[128,128]{1,0:T(8,128)S(1)} %add.306), channel_id=1, source_target_pairs={{0,8},{8,16},{16,24},{24,32},{32,40},{40,48},{48,56},{56,64},{64,7... | collective-permute-start | bytes 196616 | tf_op jit(solution)/shard_map/while/body/eval_jaxpr/ppermute | solution.py:12
  219.7 7.4 %collective-permute-start.3 = (f32[128,128]{1,0:T(8,128)S(1)}, f32[128,128]{1,0:T(8,128)S(1)}, u32[]{:S(2)}, u32[]{:S(2)}) collective-permute-start(f32[128,128]{1,0:T(8,128)S(1)} %add.307), channel_id=1, source_target_pairs={{0,8},{8,16},{16,24},{24,32},{32,40},{40,48},{48,56},{56,64},{64,7... | collective-permute-start | bytes 196616 | tf_op jit(solution)/shard_map/while/body/eval_jaxpr/ppermute | solution.py:12
  227.7 17.9 %collective-permute-start = (bf16[128,128]{1,0:T(8,128)(2,1)}, bf16[128,128]{1,0:T(8,128)(2,1)S(1)}, u32[]{:S(2)}, u32[]{:S(2)}) collective-permute-start(bf16[128,128]{1,0:T(8,128)(2,1)} %copy.64), channel_id=1, source_target_pairs={{0,8},{8,16},{16,24},{24,32},{32,40},{40,48},{48,56},{56,64},{64,7... | collective-permute-start | bytes 98312 | tf_op jit(solution)/shard_map/while/body/eval_jaxpr/ppermute | solution.py:12
  231.5 14.1 %collective-permute-start.1 = (bf16[128,128]{1,0:T(8,128)(2,1)}, bf16[128,128]{1,0:T(8,128)(2,1)S(1)}, u32[]{:S(2)}, u32[]{:S(2)}) collective-permute-start(bf16[128,128]{1,0:T(8,128)(2,1)} %copy.65), channel_id=1, source_target_pairs={{0,8},{8,16},{16,24},{24,32},{32,40},{40,48},{48,56},{56,64},{64,7... | collective-permute-start | bytes 98312 | tf_op jit(solution)/shard_map/while/body/eval_jaxpr/ppermute | solution.py:12
  239.3 7.4 %collective-permute-start.2 = (f32[128,128]{1,0:T(8,128)S(1)}, f32[128,128]{1,0:T(8,128)S(1)}, u32[]{:S(2)}, u32[]{:S(2)}) collective-permute-start(f32[128,128]{1,0:T(8,128)S(1)} %add.306), channel_id=1, source_target_pairs={{0,8},{8,16},{16,24},{24,32},{32,40},{40,48},{48,56},{56,64},{64,7... | collective-permute-start | bytes 196616 | tf_op jit(solution)/shard_map/while/body/eval_jaxpr/ppermute | solution.py:12
  241.3 7.4 %collective-permute-start.3 = (f32[128,128]{1,0:T(8,128)S(1)}, f32[128,128]{1,0:T(8,128)S(1)}, u32[]{:S(2)}, u32[]{:S(2)}) collective-permute-start(f32[128,128]{1,0:T(8,128)S(1)} %add.307), channel_id=1, source_target_pairs={{0,8},{8,16},{16,24},{24,32},{32,40},{40,48},{48,56},{56,64},{64,7... | collective-permute-start | bytes 196616 | tf_op jit(solution)/shard_map/while/body/eval_jaxpr/ppermute | solution.py:12
  249.3 18.9 %collective-permute-start = (bf16[128,128]{1,0:T(8,128)(2,1)}, bf16[128,128]{1,0:T(8,128)(2,1)S(1)}, u32[]{:S(2)}, u32[]{:S(2)}) collective-permute-start(bf16[128,128]{1,0:T(8,128)(2,1)} %copy.64), channel_id=1, source_target_pairs={{0,8},{8,16},{16,24},{24,32},{32,40},{40,48},{48,56},{56,64},{64,7... | collective-permute-start | bytes 98312 | tf_op jit(solution)/shard_map/while/body/eval_jaxpr/ppermute | solution.py:12
  252.9 15.2 %collective-permute-start.1 = (bf16[128,128]{1,0:T(8,128)(2,1)}, bf16[128,128]{1,0:T(8,128)(2,1)S(1)}, u32[]{:S(2)}, u32[]{:S(2)}) collective-permute-start(bf16[128,128]{1,0:T(8,128)(2,1)} %copy.65), channel_id=1, source_target_pairs={{0,8},{8,16},{16,24},{24,32},{32,40},{40,48},{48,56},{56,64},{64,7... | collective-permute-start | bytes 98312 | tf_op jit(solution)/shard_map/while/body/eval_jaxpr/ppermute | solution.py:12
  262.9 7.4 %collective-permute-start.2 = (f32[128,128]{1,0:T(8,128)S(1)}, f32[128,128]{1,0:T(8,128)S(1)}, u32[]{:S(2)}, u32[]{:S(2)}) collective-permute-start(f32[128,128]{1,0:T(8,128)S(1)} %add.306), channel_id=1, source_target_pairs={{0,8},{8,16},{16,24},{24,32},{32,40},{40,48},{48,56},{56,64},{64,7... | collective-permute-start | bytes 196616 | tf_op jit(solution)/shard_map/while/body/eval_jaxpr/ppermute | solution.py:12
  264.8 7.4 %collective-permute-start.3 = (f32[128,128]{1,0:T(8,128)S(1)}, f32[128,128]{1,0:T(8,128)S(1)}, u32[]{:S(2)}, u32[]{:S(2)}) collective-permute-start(f32[128,128]{1,0:T(8,128)S(1)} %add.307), channel_id=1, source_target_pairs={{0,8},{8,16},{16,24},{24,32},{32,40},{40,48},{48,56},{56,64},{64,7... | collective-permute-start | bytes 196616 | tf_op jit(solution)/shard_map/while/body/eval_jaxpr/ppermute | solution.py:12
  272.8 21.3 %collective-permute-start = (bf16[128,128]{1,0:T(8,128)(2,1)}, bf16[128,128]{1,0:T(8,128)(2,1)S(1)}, u32[]{:S(2)}, u32[]{:S(2)}) collective-permute-start(bf16[128,128]{1,0:T(8,128)(2,1)} %copy.64), channel_id=1, source_target_pairs={{0,8},{8,16},{16,24},{24,32},{32,40},{40,48},{48,56},{56,64},{64,7... | collective-permute-start | bytes 98312 | tf_op jit(solution)/shard_map/while/body/eval_jaxpr/ppermute | solution.py:12
  275.3 18.8 %collective-permute-start.1 = (bf16[128,128]{1,0:T(8,128)(2,1)}, bf16[128,128]{1,0:T(8,128)(2,1)S(1)}, u32[]{:S(2)}, u32[]{:S(2)}) collective-permute-start(bf16[128,128]{1,0:T(8,128)(2,1)} %copy.65), channel_id=1, source_target_pairs={{0,8},{8,16},{16,24},{24,32},{32,40},{40,48},{48,56},{56,64},{64,7... | collective-permute-start | bytes 98312 | tf_op jit(solution)/shard_map/while/body/eval_jaxpr/ppermute | solution.py:12
  285.0 9.1 %collective-permute-start.2 = (f32[128,128]{1,0:T(8,128)S(1)}, f32[128,128]{1,0:T(8,128)S(1)}, u32[]{:S(2)}, u32[]{:S(2)}) collective-permute-start(f32[128,128]{1,0:T(8,128)S(1)} %add.306), channel_id=1, source_target_pairs={{0,8},{8,16},{16,24},{24,32},{32,40},{40,48},{48,56},{56,64},{64,7... | collective-permute-start | bytes 196616 | tf_op jit(solution)/shard_map/while/body/eval_jaxpr/ppermute | solution.py:12
  288.3 7.6 %collective-permute-start.3 = (f32[128,128]{1,0:T(8,128)S(1)}, f32[128,128]{1,0:T(8,128)S(1)}, u32[]{:S(2)}, u32[]{:S(2)}) collective-permute-start(f32[128,128]{1,0:T(8,128)S(1)} %add.307), channel_id=1, source_target_pairs={{0,8},{8,16},{16,24},{24,32},{32,40},{40,48},{48,56},{56,64},{64,7... | collective-permute-start | bytes 196616 | tf_op jit(solution)/shard_map/while/body/eval_jaxpr/ppermute | solution.py:12
  296.5 18.3 %collective-permute-start = (bf16[128,128]{1,0:T(8,128)(2,1)}, bf16[128,128]{1,0:T(8,128)(2,1)S(1)}, u32[]{:S(2)}, u32[]{:S(2)}) collective-permute-start(bf16[128,128]{1,0:T(8,128)(2,1)} %copy.64), channel_id=1, source_target_pairs={{0,8},{8,16},{16,24},{24,32},{32,40},{40,48},{48,56},{56,64},{64,7... | collective-permute-start | bytes 98312 | tf_op jit(solution)/shard_map/while/body/eval_jaxpr/ppermute | solution.py:12
  301.3 13.5 %collective-permute-start.1 = (bf16[128,128]{1,0:T(8,128)(2,1)}, bf16[128,128]{1,0:T(8,128)(2,1)S(1)}, u32[]{:S(2)}, u32[]{:S(2)}) collective-permute-start(bf16[128,128]{1,0:T(8,128)(2,1)} %copy.65), channel_id=1, source_target_pairs={{0,8},{8,16},{16,24},{24,32},{32,40},{40,48},{48,56},{56,64},{64,7... | collective-permute-start | bytes 98312 | tf_op jit(solution)/shard_map/while/body/eval_jaxpr/ppermute | solution.py:12
  305.6 10.8 %collective-permute-start.2 = (f32[128,128]{1,0:T(8,128)S(1)}, f32[128,128]{1,0:T(8,128)S(1)}, u32[]{:S(2)}, u32[]{:S(2)}) collective-permute-start(f32[128,128]{1,0:T(8,128)S(1)} %add.306), channel_id=1, source_target_pairs={{0,8},{8,16},{16,24},{24,32},{32,40},{40,48},{48,56},{56,64},{64,7... | collective-permute-start | bytes 196616 | tf_op jit(solution)/shard_map/while/body/eval_jaxpr/ppermute | solution.py:12
  311.1 7.8 %collective-permute-start.3 = (f32[128,128]{1,0:T(8,128)S(1)}, f32[128,128]{1,0:T(8,128)S(1)}, u32[]{:S(2)}, u32[]{:S(2)}) collective-permute-start(f32[128,128]{1,0:T(8,128)S(1)} %add.307), channel_id=1, source_target_pairs={{0,8},{8,16},{16,24},{24,32},{32,40},{40,48},{48,56},{56,64},{64,7... | collective-permute-start | bytes 196616 | tf_op jit(solution)/shard_map/while/body/eval_jaxpr/ppermute | solution.py:12
  319.6 18.3 %collective-permute-start = (bf16[128,128]{1,0:T(8,128)(2,1)}, bf16[128,128]{1,0:T(8,128)(2,1)S(1)}, u32[]{:S(2)}, u32[]{:S(2)}) collective-permute-start(bf16[128,128]{1,0:T(8,128)(2,1)} %copy.64), channel_id=1, source_target_pairs={{0,8},{8,16},{16,24},{24,32},{32,40},{40,48},{48,56},{56,64},{64,7... | collective-permute-start | bytes 98312 | tf_op jit(solution)/shard_map/while/body/eval_jaxpr/ppermute | solution.py:12
  322.1 15.8 %collective-permute-start.1 = (bf16[128,128]{1,0:T(8,128)(2,1)}, bf16[128,128]{1,0:T(8,128)(2,1)S(1)}, u32[]{:S(2)}, u32[]{:S(2)}) collective-permute-start(bf16[128,128]{1,0:T(8,128)(2,1)} %copy.65), channel_id=1, source_target_pairs={{0,8},{8,16},{16,24},{24,32},{32,40},{40,48},{48,56},{56,64},{64,7... | collective-permute-start | bytes 98312 | tf_op jit(solution)/shard_map/while/body/eval_jaxpr/ppermute | solution.py:12
  331.7 7.4 %collective-permute-start.2 = (f32[128,128]{1,0:T(8,128)S(1)}, f32[128,128]{1,0:T(8,128)S(1)}, u32[]{:S(2)}, u32[]{:S(2)}) collective-permute-start(f32[128,128]{1,0:T(8,128)S(1)} %add.306), channel_id=1, source_target_pairs={{0,8},{8,16},{16,24},{24,32},{32,40},{40,48},{48,56},{56,64},{64,7... | collective-permute-start | bytes 196616 | tf_op jit(solution)/shard_map/while/body/eval_jaxpr/ppermute | solution.py:12
  333.6 7.4 %collective-permute-start.3 = (f32[128,128]{1,0:T(8,128)S(1)}, f32[128,128]{1,0:T(8,128)S(1)}, u32[]{:S(2)}, u32[]{:S(2)}) collective-permute-start(f32[128,128]{1,0:T(8,128)S(1)} %add.307), channel_id=1, source_target_pairs={{0,8},{8,16},{16,24},{24,32},{32,40},{40,48},{48,56},{56,64},{64,7... | collective-permute-start | bytes 196616 | tf_op jit(solution)/shard_map/while/body/eval_jaxpr/ppermute | solution.py:12
  341.6 16.2 %collective-permute-start = (bf16[128,128]{1,0:T(8,128)(2,1)}, bf16[128,128]{1,0:T(8,128)(2,1)S(1)}, u32[]{:S(2)}, u32[]{:S(2)}) collective-permute-start(bf16[128,128]{1,0:T(8,128)(2,1)} %copy.64), channel_id=1, source_target_pairs={{0,8},{8,16},{16,24},{24,32},{32,40},{40,48},{48,56},{56,64},{64,7... | collective-permute-start | bytes 98312 | tf_op jit(solution)/shard_map/while/body/eval_jaxpr/ppermute | solution.py:12
  345.0 12.7 %collective-permute-start.1 = (bf16[128,128]{1,0:T(8,128)(2,1)}, bf16[128,128]{1,0:T(8,128)(2,1)S(1)}, u32[]{:S(2)}, u32[]{:S(2)}) collective-permute-start(bf16[128,128]{1,0:T(8,128)(2,1)} %copy.65), channel_id=1, source_target_pairs={{0,8},{8,16},{16,24},{24,32},{32,40},{40,48},{48,56},{56,64},{64,7... | collective-permute-start | bytes 98312 | tf_op jit(solution)/shard_map/while/body/eval_jaxpr/ppermute | solution.py:12
  353.7 7.4 %collective-permute-start.2 = (f32[128,128]{1,0:T(8,128)S(1)}, f32[128,128]{1,0:T(8,128)S(1)}, u32[]{:S(2)}, u32[]{:S(2)}) collective-permute-start(f32[128,128]{1,0:T(8,128)S(1)} %add.306), channel_id=1, source_target_pairs={{0,8},{8,16},{16,24},{24,32},{32,40},{40,48},{48,56},{56,64},{64,7... | collective-permute-start | bytes 196616 | tf_op jit(solution)/shard_map/while/body/eval_jaxpr/ppermute | solution.py:12
  355.7 7.4 %collective-permute-start.3 = (f32[128,128]{1,0:T(8,128)S(1)}, f32[128,128]{1,0:T(8,128)S(1)}, u32[]{:S(2)}, u32[]{:S(2)}) collective-permute-start(f32[128,128]{1,0:T(8,128)S(1)} %add.307), channel_id=1, source_target_pairs={{0,8},{8,16},{16,24},{24,32},{32,40},{40,48},{48,56},{56,64},{64,7... | collective-permute-start | bytes 196616 | tf_op jit(solution)/shard_map/while/body/eval_jaxpr/ppermute | solution.py:12
  363.6 18.4 %collective-permute-start = (bf16[128,128]{1,0:T(8,128)(2,1)}, bf16[128,128]{1,0:T(8,128)(2,1)S(1)}, u32[]{:S(2)}, u32[]{:S(2)}) collective-permute-start(bf16[128,128]{1,0:T(8,128)(2,1)} %copy.64), channel_id=1, source_target_pairs={{0,8},{8,16},{16,24},{24,32},{32,40},{40,48},{48,56},{56,64},{64,7... | collective-permute-start | bytes 98312 | tf_op jit(solution)/shard_map/while/body/eval_jaxpr/ppermute | solution.py:12
  366.2 15.9 %collective-permute-start.1 = (bf16[128,128]{1,0:T(8,128)(2,1)}, bf16[128,128]{1,0:T(8,128)(2,1)S(1)}, u32[]{:S(2)}, u32[]{:S(2)}) collective-permute-start(bf16[128,128]{1,0:T(8,128)(2,1)} %copy.65), channel_id=1, source_target_pairs={{0,8},{8,16},{16,24},{24,32},{32,40},{40,48},{48,56},{56,64},{64,7... | collective-permute-start | bytes 98312 | tf_op jit(solution)/shard_map/while/body/eval_jaxpr/ppermute | solution.py:12
  374.4 7.6 %collective-permute-start.2 = (f32[128,128]{1,0:T(8,128)S(1)}, f32[128,128]{1,0:T(8,128)S(1)}, u32[]{:S(2)}, u32[]{:S(2)}) collective-permute-start(f32[128,128]{1,0:T(8,128)S(1)} %add.306), channel_id=1, source_target_pairs={{0,8},{8,16},{16,24},{24,32},{32,40},{40,48},{48,56},{56,64},{64,7... | collective-permute-start | bytes 196616 | tf_op jit(solution)/shard_map/while/body/eval_jaxpr/ppermute | solution.py:12
  376.4 7.4 %collective-permute-start.3 = (f32[128,128]{1,0:T(8,128)S(1)}, f32[128,128]{1,0:T(8,128)S(1)}, u32[]{:S(2)}, u32[]{:S(2)}) collective-permute-start(f32[128,128]{1,0:T(8,128)S(1)} %add.307), channel_id=1, source_target_pairs={{0,8},{8,16},{16,24},{24,32},{32,40},{40,48},{48,56},{56,64},{64,7... | collective-permute-start | bytes 196616 | tf_op jit(solution)/shard_map/while/body/eval_jaxpr/ppermute | solution.py:12
  384.3 21.8 %collective-permute-start = (bf16[128,128]{1,0:T(8,128)(2,1)}, bf16[128,128]{1,0:T(8,128)(2,1)S(1)}, u32[]{:S(2)}, u32[]{:S(2)}) collective-permute-start(bf16[128,128]{1,0:T(8,128)(2,1)} %copy.64), channel_id=1, source_target_pairs={{0,8},{8,16},{16,24},{24,32},{32,40},{40,48},{48,56},{56,64},{64,7... | collective-permute-start | bytes 98312 | tf_op jit(solution)/shard_map/while/body/eval_jaxpr/ppermute | solution.py:12
  389.2 17.0 %collective-permute-start.1 = (bf16[128,128]{1,0:T(8,128)(2,1)}, bf16[128,128]{1,0:T(8,128)(2,1)S(1)}, u32[]{:S(2)}, u32[]{:S(2)}) collective-permute-start(bf16[128,128]{1,0:T(8,128)(2,1)} %copy.65), channel_id=1, source_target_pairs={{0,8},{8,16},{16,24},{24,32},{32,40},{40,48},{48,56},{56,64},{64,7... | collective-permute-start | bytes 98312 | tf_op jit(solution)/shard_map/while/body/eval_jaxpr/ppermute | solution.py:12
  396.8 9.4 %collective-permute-start.2 = (f32[128,128]{1,0:T(8,128)S(1)}, f32[128,128]{1,0:T(8,128)S(1)}, u32[]{:S(2)}, u32[]{:S(2)}) collective-permute-start(f32[128,128]{1,0:T(8,128)S(1)} %add.306), channel_id=1, source_target_pairs={{0,8},{8,16},{16,24},{24,32},{32,40},{40,48},{48,56},{56,64},{64,7... | collective-permute-start | bytes 196616 | tf_op jit(solution)/shard_map/while/body/eval_jaxpr/ppermute | solution.py:12
  398.8 9.1 %collective-permute-start.3 = (f32[128,128]{1,0:T(8,128)S(1)}, f32[128,128]{1,0:T(8,128)S(1)}, u32[]{:S(2)}, u32[]{:S(2)}) collective-permute-start(f32[128,128]{1,0:T(8,128)S(1)} %add.307), channel_id=1, source_target_pairs={{0,8},{8,16},{16,24},{24,32},{32,40},{40,48},{48,56},{56,64},{64,7... | collective-permute-start | bytes 196616 | tf_op jit(solution)/shard_map/while/body/eval_jaxpr/ppermute | solution.py:12
  408.5 20.3 %collective-permute-start = (bf16[128,128]{1,0:T(8,128)(2,1)}, bf16[128,128]{1,0:T(8,128)(2,1)S(1)}, u32[]{:S(2)}, u32[]{:S(2)}) collective-permute-start(bf16[128,128]{1,0:T(8,128)(2,1)} %copy.64), channel_id=1, source_target_pairs={{0,8},{8,16},{16,24},{24,32},{32,40},{40,48},{48,56},{56,64},{64,7... | collective-permute-start | bytes 98312 | tf_op jit(solution)/shard_map/while/body/eval_jaxpr/ppermute | solution.py:12
  413.4 15.4 %collective-permute-start.1 = (bf16[128,128]{1,0:T(8,128)(2,1)}, bf16[128,128]{1,0:T(8,128)(2,1)S(1)}, u32[]{:S(2)}, u32[]{:S(2)}) collective-permute-start(bf16[128,128]{1,0:T(8,128)(2,1)} %copy.65), channel_id=1, source_target_pairs={{0,8},{8,16},{16,24},{24,32},{32,40},{40,48},{48,56},{56,64},{64,7... | collective-permute-start | bytes 98312 | tf_op jit(solution)/shard_map/while/body/eval_jaxpr/ppermute | solution.py:12
  (6 other events, 64.3 us)
where the time goes:
time: 440 us; the launch traced here: 434 us
  starting transfers between devices  215 us (49%)
  waiting for transfers between devices  51.7 us (12%)
  matrix products  49.6 us (11%)
  blocking collectives  45.2 us (10%)
  other arithmetic  24.5 us (6%)
  local copies, waits for them, and re-layouts  24.2 us (6%)
  loops' own time  23.1 us (5%)
    ppermute x65, starting transfers between devices, passed_along(): return lax.ppermute(value, axis, pairs)  210 us
    ppermute x65, waiting for transfers between devices, passed_along(): return lax.ppermute(value, axis, pairs)  51.7 us
    all_gather x1, blocking collectives, body(): piece = lax.all_gather(keys[0], 'ctx', axis=0, tiled=True)  45.2 us
    another operation x1, loops' own time, body(): lax.fori_loop(0, count, cycle_turn, (keys[0], values[0], zero_kv, zero_kv...  22.3 us
    while x32, local copies, waits for them, and re-layouts  19.7 us
    dot_general x14, matrix products, block_scores(): jnp.einsum('iged,jgd->geij', q_local, k_three, preferred_element_type=jnp...  17.8 us
    dot_general x13, matrix products, block_grads(): jnp.einsum('geij,jgd->iged', dscore, k_three, preferred_element_type=jnp....  13.2 us
    dot_general x13, matrix products, block_grads(): jnp.einsum('iged,jgd->geij', do_local, v_three, preferred_element_type=jn...  12.9 us
  transfers between devices with their start and end apart: 66, of which 27 were waited for; matrix products, arithmetic and copies ran while one was open for 20% of the time, Pallas kernels for 0%

commit v1 on v0

v1 whole, which is shorter than its diff:
```python
import jax
import jax.numpy as jnp
from jax import lax
from jax.sharding import PartitionSpec as P

HEAD_DIM = 128
CHUNKS = 4


def passed_along(value, axis, steps):
    count = lax.axis_size(axis)
    pairs = [(source, (source + steps) % count) for source in range(count)]
    return lax.ppermute(value, axis, pairs)


def body(query, keys, values, attn_out, grad_out, block_of):
    rows = query.shape[1]
    kv_width = keys.shape[2]
    head_dim = HEAD_DIM
    groups = kv_width // head_dim
    heads = query.shape[2] // head_dim
    per = heads // groups
    scale = head_dim ** (-0.5)
    half = rows // 2
    order = block_of[0]
    me = lax.axis_index("ctx")
    handed = passed_along(grad_out[0], "segment", -1)
    incoming = lax.all_to_all(handed, "tp", split_axis=1, concat_axis=0, tiled=True)
    q_local = query[0].reshape(rows, groups, per, head_dim)
    do_local = incoming.reshape(rows, groups, per, head_dim)
    delta = jnp.sum(
        attn_out[0].reshape(rows, groups, per, head_dim).astype(jnp.float32)
        * do_local.astype(jnp.float32),
        axis=-1,
    )
    delta = jnp.transpose(delta, (1, 2, 0))

    def place(first, length):
        index = first + jnp.arange(length, dtype=jnp.int32)
        table = (index // half)[:, None] == jnp.arange(order.shape[0], dtype=jnp.int32)[None, :]
        return jnp.sum(jnp.where(table, order[None, :], 0), axis=1) * half + index % half

    q_pos = place(me * rows, rows)

    kv = jnp.concatenate([keys[0], values[0]], axis=1)
    kv_all = lax.all_gather(kv, "ctx", axis=0, tiled=True)
    seq = kv_all.shape[0]
    k_all = kv_all[:, :kv_width].reshape(seq, groups, head_dim)
    v_all = kv_all[:, kv_width:].reshape(seq, groups, head_dim)
    k_pos_all = place(jnp.int32(0), seq)
    width = seq // CHUNKS

    def chunk_scores(c):
        k_c = k_all[c * width:(c + 1) * width]
        scores = scale * jnp.einsum(
            "iged,jgd->geij", q_local, k_c, preferred_element_type=jnp.float32
        )
        allowed = k_pos_all[c * width:(c + 1) * width][None, :] <= q_pos[:, None]
        return scores, allowed

    tops = []
    for c in range(CHUNKS):
        scores, allowed = chunk_scores(c)
        tops.append(jnp.max(jnp.where(allowed, scores, -1e30), axis=-1))
    top = tops[0]
    for t in tops[1:]:
        top = jnp.maximum(top, t)
    total = jnp.zeros_like(top)
    for c in range(CHUNKS):
        scores, allowed = chunk_scores(c)
        total = total + jnp.sum(jnp.where(allowed, jnp.exp(scores - top[..., None]), 0.0), axis=-1)
    lse = top + jnp.log(total)

    dquery = jnp.zeros((rows, groups, per, head_dim), jnp.float32)
    dks = []
    dvs = []
    for c in range(CHUNKS):
        scores, allowed = chunk_scores(c)
        k_c = k_all[c * width:(c + 1) * width]
        v_c = v_all[c * width:(c + 1) * width]
        prob = jnp.where(allowed, jnp.exp(scores - lse[..., None]), 0.0)
        prob_b = prob.astype(jnp.bfloat16)
        dvalue = jnp.einsum("geij,iged->jgd", prob_b, do_local, preferred_element_type=jnp.float32)
        dprob = jnp.einsum("iged,jgd->geij", do_local, v_c, preferred_element_type=jnp.float32)
        dscore = (prob * (dprob - delta[..., None])).astype(jnp.bfloat16)
        dquery = dquery + jnp.einsum("geij,jgd->iged", dscore, k_c, preferred_element_type=jnp.float32)
        dkey = jnp.einsum("geij,iged->jgd", dscore, q_local, preferred_element_type=jnp.float32)
        dks.append(dkey.reshape(width, kv_width))
        dvs.append(dvalue.reshape(width, kv_width))
    dkv = jnp.concatenate([jnp.concatenate(dks, axis=0), jnp.concatenate(dvs, axis=0)], axis=1)
    dkv = lax.psum_scatter(dkv, "ctx", scatter_dimension=0, tiled=True)
    dkey = dkv[:, :kv_width]
    dvalue = dkv[:, kv_width:]
    grad_query = (scale * dquery).reshape(rows, heads * head_dim).astype(jnp.bfloat16)[None]
    grad_keys = (scale * dkey).astype(jnp.bfloat16)[None]
    grad_values = dvalue.astype(jnp.bfloat16)[None]
    return (grad_query, grad_keys, grad_values)


def solution(mesh):
    return jax.shard_map(
        body,
        mesh=mesh,
        in_specs=(
            P("segment", "ctx", "tp"),
            P("segment", "ctx", "tp"),
            P("segment", "ctx", "tp"),
            P("segment", "ctx", "tp"),
            P("segment", ("ctx", "tp"), None),
            P("segment", None),
        ),
        out_specs=(P("segment", "ctx", "tp"), P("segment", "ctx", "tp"), P("segment", "ctx", "tp")),
        check_vma=False,
    )
```

time: 440 us -> 193 us (0.44); the launches traced: 434 us -> 192 us
  starting transfers between devices: 215 us -> 19.1 us
  waiting for transfers between devices: 51.7 us -> 129 us
  blocking collectives: 45.2 us -> 0 us
  matrix products: 49.6 us -> 15.6 us
  loops' own time: 23.1 us -> 0 us
  local copies, waits for them, and re-layouts: 24.2 us -> 5.3 us
  other arithmetic: 24.5 us -> 9.23 us
  between operations: 0.83 us -> 14.3 us
    ppermute x65 -> x1, starting transfers between devices: 210 us -> 5.38 us  [passed_along(): return lax.ppermute(value, axis, pairs)]
    reduce_scatter x0 -> x1, waiting for transfers between devices: none -> 68.8 us  [body(): dkv = lax.psum_scatter(dkv, 'ctx', scatter_dimension=0, tiled=True)]
    all_gather x0 -> x1, waiting for transfers between devices: none -> 52.6 us  [body(): kv_all = lax.all_gather(kv, 'ctx', axis=0, tiled=True)]
    ppermute x65 -> x1, waiting for transfers between devices: 51.7 us -> 2.16 us  [passed_along(): return lax.ppermute(value, axis, pairs)]
    all_gather x1 -> x0, blocking collectives: 45.2 us -> none  [body(): piece = lax.all_gather(keys[0], 'ctx', axis=0, tiled=True)]
    dot_general x66 -> x20, matrix products: 49.6 us -> 15.6 us  [the longest x4 5.03 us: body(): jnp.einsum('geij,jgd->iged', dscore, k_c, preferred_element_type=jnp.floa...]
    another operation x17 -> x0, loops' own time: 23.1 us -> none  [the longest x1 22.3 us: body(): lax.fori_loop(0, count, cycle_turn, (keys[0], values[0], zero_kv, zero_kv...]
    while x32 -> x0, local copies, waits for them, and re-layouts: 19.7 us -> none
  transfers between devices with their start and end apart: 66 -> 4, of which waited for: 27 -> 4; matrix products, arithmetic and copies ran while one was open for 20% -> 6% of each run, Pallas kernels for 0% -> 0%
where the time goes in v1:
time: 193 us; the launch traced here: 192 us
  waiting for transfers between devices  129 us (67%)
  starting transfers between devices  19.1 us (10%)
  matrix products  15.6 us (8%)
  between operations  14.3 us (7%)
  other arithmetic  9.23 us (5%)
  local copies, waits for them, and re-layouts  5.3 us (3%)
    reduce_scatter x1, waiting for transfers between devices, body(): dkv = lax.psum_scatter(dkv, 'ctx', scatter_dimension=0, tiled=True)  68.8 us
    all_gather x1, waiting for transfers between devices, body(): kv_all = lax.all_gather(kv, 'ctx', axis=0, tiled=True)  52.6 us
    all_to_all x1, starting transfers between devices, body(): lax.all_to_all(handed, 'tp', split_axis=1, concat_axis=0, tiled=True)  13.7 us
    ppermute x1, starting transfers between devices, passed_along(): return lax.ppermute(value, axis, pairs)  5.38 us
    all_to_all x1, waiting for transfers between devices, body(): lax.all_to_all(handed, 'tp', split_axis=1, concat_axis=0, tiled=True)  5.07 us
    dot_general x4, matrix products, body(): jnp.einsum('geij,jgd->iged', dscore, k_c, preferred_element_type=jnp.floa...  5.03 us
    dot_general x4, matrix products, body(): jnp.einsum('iged,jgd->geij', do_local, v_c, preferred_element_type=jnp.fl...  3.99 us
  transfers between devices with their start and end apart: 4, of which 4 were waited for; matrix products, arithmetic and copies ran while one was open for 6% of the time, Pallas kernels for 0%

profile of v1, /device:TPU:6, one launch (start us, length us, event | category | flops | bytes accessed | tf_op | source)
XLA Modules:
  0.0 192.3 jit_solution(11662003906191972715)
XLA Ops:
  7.2 0.0 all-gather.2.cloned.1.call-start
  7.2 1.4 pad_maximum_fusion
  8.6 0.0 all-gather.2.cloned.1.call-update
  8.6 5.4 %collective-permute-start = (bf16[16,8192]{1,0:T(8,128)(2,1)}, bf16[16,8192]{1,0:T(8,128)(2,1)S(1)}, u32[]{:S(2)}, u32[]{:S(2)}) collective-permute-start(bf16[16,8192]{1,0:T(8,128)(2,1)} %bitcast.301), channel_id=1, source_target_pairs={{0,896},{128,0},{256,128},{384,256},{512,384},{640,512},{768,640},... | collective-permute-start | bytes 786440 | tf_op jit(solution)/shard_map/ppermute | solution.py:13
  14.1 0.7 select_reduce_fusion.1
  14.8 0.8 select_reduce_fusion
  15.6 1.0 convert_bitcast_fusion
  16.6 1.0 copy.119
  17.6 0.1 copy.121
  17.7 2.2 %collective-permute-done = bf16[16,8192]{1,0:T(8,128)(2,1)S(1)} collective-permute-done((bf16[16,8192]{1,0:T(8,128)(2,1)}, bf16[16,8192]{1,0:T(8,128)(2,1)S(1)}, u32[]{:S(2)}, u32[]{:S(2)}) %collective-permute-start) | collective-permute-done | bytes 262176 | tf_op jit(solution)/shard_map/ppermute | solution.py:13
  19.9 0.7 copy.164
  20.6 13.7 %all-to-all-start = ((bf16[16,8,1024]{2,0,1:T(8,128)(2,1)}), bf16[16,8,1024]{2,0,1:T(8,128)(2,1)S(1)}, u32[]{:S(2)}, u32[]{:S(2)}) async-start(bf16[16,8,1024]{2,0,1:T(8,128)(2,1)} %bitcast.272), calls=%async_computation | async-start | bytes 524288 | tf_op jit(solution)/shard_map/all_to_all | solution.py:28
  34.3 0.0 reduce-scatter.2.cloned.1.call-start
  34.3 0.3 broadcast_compare_fusion.2
  34.6 5.1 %all-to-all-done = bf16[16,8,1024]{2,0,1:T(8,128)(2,1)S(1)} async-done(((bf16[16,8,1024]{2,0,1:T(8,128)(2,1)}), bf16[16,8,1024]{2,0,1:T(8,128)(2,1)S(1)}, u32[]{:S(2)}, u32[]{:S(2)}) %all-to-all-start) | async-done | bytes 262176 | tf_op jit(solution)/shard_map/all_to_all | solution.py:28
  39.8 0.0 copy-start.3
  39.8 0.1 copy.122
  39.9 0.2 multiply_reduce_fusion
  40.2 52.6 %all-gather.2.cloned.1.call-done = bf16[2048,256]{1,0:T(8,128)(2,1)} async-done(((bf16[128,256]{1,0:T(8,128)(2,1)}), bf16[2048,256]{1,0:T(8,128)(2,1)}) %all-gather.2.cloned.1.call-update) | async-done | bytes 1048592 | tf_op jit(solution)/shard_map/all_gather | solution.py:46
  92.8 0.0 copy-start.2
  92.8 1.4 fusion.20
  94.2 0.0 copy-done.2
  94.2 0.5 fusion.14
  94.7 0.5 fusion.8
  95.2 0.5 fusion.26
  95.7 1.7 fusion.23
  97.4 0.5 convolution_bitcast_fusion.3
  97.9 0.5 convolution_bitcast_fusion.2
  98.4 0.5 convolution_bitcast_fusion.1
  99.0 0.5 convolution_bitcast_fusion
  99.5 0.7 fusion.36
  100.2 0.4 convolution_bitcast_fusion.7
  100.6 0.0 copy-done.3
  100.7 0.7 fusion.37
  101.4 0.4 convolution_bitcast_fusion.6
  101.8 0.0 copy-start.4
  101.9 1.8 fusion.38
  103.6 0.4 convolution_bitcast_fusion.5
  104.1 0.0 copy-done.4
  104.1 0.7 fusion.39
  104.8 0.0 copy-start
  104.8 1.0 copy-done
  105.8 0.4 convolution_bitcast_fusion.4
  106.2 1.5 maximum_maximum_fusion
  107.7 0.0 reduce-scatter.2.cloned.1.call-update
  107.8 1.2 fusion.67
  109.0 0.0 copy-start.1
  109.0 1.3 convolution_add_fusion.2
  110.3 1.2 convolution_add_fusion.1
  111.6 0.0 copy-done.1
  111.6 1.2 fusion.41
  112.8 0.9 copy.105
  113.7 68.8 %reduce-scatter.2.cloned.1.call-done = f32[128,256]{1,0:T(8,128)} async-done(((f32[2048,256]{1,0:T(8,128)}), f32[128,256]{1,0:T(8,128)}) %reduce-scatter.2.cloned.1.call-update) | async-done | bytes 131088 | tf_op jit(solution)/shard_map/reduce_scatter | solution.py:91
  182.5 1.5 fusion.89
  184.0 1.5 fusion.88
  (10 shorter events, 0.2 us)
Async XLA Ops:
  7.2 85.6 %all-gather.2.cloned.1.call-start = ((), (), s32[]{:S(2)}) async-start(), calls=%async_computation.2 | async-start | bytes 1114112 | tf_op jit(solution)/shard_map/all_gather | solution.py:46
  8.6 11.2 %collective-permute-start = (bf16[16,8192]{1,0:T(8,128)(2,1)}, bf16[16,8192]{1,0:T(8,128)(2,1)S(1)}, u32[]{:S(2)}, u32[]{:S(2)}) collective-permute-start(bf16[16,8192]{1,0:T(8,128)(2,1)} %bitcast.301), channel_id=1, source_target_pairs={{0,896},{128,0},{256,128},{384,256},{512,384},{640,512},{768,640},... | collective-permute-start | bytes 786440 | tf_op jit(solution)/shard_map/ppermute | solution.py:13
  20.6 19.1 %all-to-all-start = ((bf16[16,8,1024]{2,0,1:T(8,128)(2,1)}), bf16[16,8,1024]{2,0,1:T(8,128)(2,1)S(1)}, u32[]{:S(2)}, u32[]{:S(2)}) async-start(bf16[16,8,1024]{2,0,1:T(8,128)(2,1)} %bitcast.272), calls=%async_computation | async-start | bytes 524288 | tf_op jit(solution)/shard_map/all_to_all | solution.py:28
  34.3 148.2 %reduce-scatter.2.cloned.1.call-start = ((), (), s32[]{:S(2)}) async-start(), calls=%async_computation.3 | async-start | bytes 2228224 | tf_op jit(solution)/shard_map/reduce_scatter | solution.py:91
  39.8 60.9 %copy-start.3 = (bf16[16,8,8,128]{3,2,1,0:T(8,128)(2,1)}, bf16[16,8,8,128]{3,2,1,0:T(8,128)(2,1)S(1)}, u32[]{:S(2)}) copy-start(bf16[16,8,8,128]{3,2,1,0:T(8,128)(2,1)S(1)} %copy.120) | copy-start | bytes 786436
  92.8 1.4 copy-start.2
  101.8 2.2 %copy-start.4 = (bf16[16,8,8,128]{3,2,1,0:T(8,128)(2,1)S(1)}, bf16[16,8,8,128]{3,2,1,0:T(8,128)(2,1)}, u32[]{:S(2)}) copy-start(bf16[16,8,8,128]{3,2,1,0:T(8,128)(2,1)} %copy-done.3) | copy-start | bytes 786436
  104.8 1.0 copy-start
  109.0 2.6 %copy-start.1 = (bf16[8,128,512]{1,2,0:T(8,128)(2,1)S(1)}, bf16[8,128,512]{1,2,0:T(8,128)(2,1)}, u32[]{:S(2)}) copy-start(bf16[8,128,512]{1,2,0:T(8,128)(2,1)} %copy-done) | copy-start | bytes 3145732
Sparse Core Ops, SparseCore 0:
  10.6 82.1 all-gather.1
  107.9 74.5 reduce-scatter.1

commit v2 on v1

--- a/solution.py
+++ b/solution.py
@@ -43,11 +43,25 @@
     q_pos = place(me * rows, rows)
 
     kv = jnp.concatenate([keys[0], values[0]], axis=1)
-    kv_all = lax.all_gather(kv, "ctx", axis=0, tiled=True)
+    count = lax.axis_size("ctx")
+    reach = count // 2
+    slots = [None] * count
+    slots[reach] = kv
+    right = kv
+    left = kv
+    for step in range(1, reach + 1):
+        right = passed_along(right, "ctx", 1)
+        slots[reach - step] = right
+        if step < count - reach:
+            left = passed_along(left, "ctx", -1)
+            slots[reach + step] = left
+    kv_all = jnp.concatenate(slots, axis=0)
     seq = kv_all.shape[0]
     k_all = kv_all[:, :kv_width].reshape(seq, groups, head_dim)
     v_all = kv_all[:, kv_width:].reshape(seq, groups, head_dim)
-    k_pos_all = place(jnp.int32(0), seq)
+    slot_rows = jnp.arange(seq, dtype=jnp.int32)
+    global_rows = ((me + slot_rows // rows - reach) % count) * rows + slot_rows % rows
+    k_pos_all = jnp.take(order, global_rows // half) * half + global_rows % half
     width = seq // CHUNKS
 
     def chunk_scores(c):
@@ -87,8 +101,18 @@
         dkey = jnp.einsum("geij,iged->jgd", dscore, q_local, preferred_element_type=jnp.float32)
         dks.append(dkey.reshape(width, kv_width))
         dvs.append(dvalue.reshape(width, kv_width))
-    dkv = jnp.concatenate([jnp.concatenate(dks, axis=0), jnp.concatenate(dvs, axis=0)], axis=1)
-    dkv = lax.psum_scatter(dkv, "ctx", scatter_dimension=0, tiled=True)
+    parts = [jnp.concatenate([dk_c, dv_c], axis=1) for dk_c, dv_c in zip(dks, dvs)]
+    parts = jnp.concatenate(parts, axis=0).reshape(count, rows, 2 * kv_width)
+    going_left = parts[0]
+    for step in range(1, reach):
+        going_left = passed_along(going_left, "ctx", -1) + parts[step]
+    going_left = passed_along(going_left, "ctx", -1)
+    dkv = parts[reach] + going_left
+    if count - reach > 1:
+        going_right = parts[count - 1]
+        for step in range(1, count - reach - 1):
+            going_right = passed_along(going_right, "ctx", 1) + parts[count - 1 - step]
+        dkv = dkv + passed_along(going_right, "ctx", 1)
     dkey = dkv[:, :kv_width]
     dvalue = dkv[:, kv_width:]
     grad_query = (scale * dquery).reshape(rows, heads * head_dim).astype(jnp.bfloat16)[None]

time: 193 us -> 218 us (1.13)
  starting transfers between devices: 19.1 us -> 132 us
  waiting for transfers between devices: 129 us -> 17.5 us
  other arithmetic: 9.23 us -> 31 us
  local copies, waits for them, and re-layouts: 5.3 us -> 19.2 us
  between operations: 14.3 us -> 1.51 us
    ppermute x1 -> x31, starting transfers between devices: 5.38 us -> 127 us  [passed_along(): return lax.ppermute(value, axis, pairs)]
    reduce_scatter x1 -> x0, waiting for transfers between devices: 68.8 us -> none  [body(): dkv = lax.psum_scatter(dkv, 'ctx', scatter_dimension=0, tiled=True)]
    all_gather x1 -> x0, waiting for transfers between devices: 52.6 us -> none  [body(): kv_all = lax.all_gather(kv, 'ctx', axis=0, tiled=True)]
    add x0 -> x15, other arithmetic: none -> 16 us  [the longest x1 15.6 us: body(): k_pos_all = jnp.take(order, global_rows // half) * half + global_rows % half]
    ppermute x1 -> x31, waiting for transfers between devices: 2.16 us -> 17.5 us  [passed_along(): return lax.ppermute(value, axis, pairs)]
    all_to_all x1, starting transfers between devices: 13.7 us -> 4.78 us  [body(): lax.all_to_all(handed, 'tp', split_axis=1, concat_axis=0, tiled=True)]
    unnamed x15 -> x43, local copies, waits for them, and re-layouts: 3.07 us -> 10.7 us
    gather x0 -> x14, other arithmetic: none -> 6.38 us  [body(): k_pos_all = jnp.take(order, global_rows // half) * half + global_rows % half]
  transfers between devices with their start and end apart: 4 -> 32, of which waited for: 4 -> 14; matrix products, arithmetic and copies ran while one was open for 6% -> 21% of each run, Pallas kernels for 0% -> 0%
where the time goes in v2:
time: 218 us; the launch traced here: 215 us
  starting transfers between devices  132 us (61%)
  other arithmetic  31 us (14%)
  local copies, waits for them, and re-layouts  19.2 us (9%)
  waiting for transfers between devices  17.5 us (8%)
  matrix products  14.5 us (7%)
    ppermute x31, starting transfers between devices, passed_along(): return lax.ppermute(value, axis, pairs)  127 us
    ppermute x31, waiting for transfers between devices, passed_along(): return lax.ppermute(value, axis, pairs)  17.5 us
    add x1, other arithmetic, body(): k_pos_all = jnp.take(order, global_rows // half) * half + global_rows % half  15.6 us
    unnamed x43, local copies, waits for them, and re-layouts  10.7 us
    gather x14, other arithmetic, body(): k_pos_all = jnp.take(order, global_rows // half) * half + global_rows % half  6.38 us
    dot_general x4, matrix products, chunk_scores(): jnp.einsum('iged,jgd->geij', q_local, k_c, preferred_element_type=jnp.flo...  6.15 us
    all_to_all x1, starting transfers between devices, body(): lax.all_to_all(handed, 'tp', split_axis=1, concat_axis=0, tiled=True)  4.78 us
  transfers between devices with their start and end apart: 32, of which 14 were waited for; matrix products, arithmetic and copies ran while one was open for 21% of the time, Pallas kernels for 0%

profile of v2, /device:TPU:6, one launch (start us, length us, event | category | flops | bytes accessed | tf_op | source)
XLA Modules:
  0.0 215.4 jit_solution(1469387793564127651)
XLA Ops:
  0.7 0.8 pad_maximum_fusion.5
  1.5 18.2 %collective-permute-start.8 = (bf16[128,256]{1,0:T(8,128)(2,1)S(1)}, bf16[128,256]{1,0:T(8,128)(2,1)S(1)}, u32[]{:S(2)}, u32[]{:S(2)}) collective-permute-start(bf16[128,256]{1,0:T(8,128)(2,1)S(1)} %pad_maximum_fusion.5), channel_id=1, source_target_pairs={{0,120},{8,0},{16,8},{24,16},{32,24},{40,32},{48,40},{56,48},{64,5... | collective-permute-start | bytes 196616 | tf_op jit(solution)/shard_map/ppermute | solution.py:13
  19.7 1.9 collective-permute-start
  21.6 5.4 %collective-permute-start.15 = (bf16[16,8192]{1,0:T(8,128)(2,1)}, bf16[16,8192]{1,0:T(8,128)(2,1)S(1)}, u32[]{:S(2)}, u32[]{:S(2)}) collective-permute-start(bf16[16,8192]{1,0:T(8,128)(2,1)} %bitcast.342), channel_id=1, source_target_pairs={{0,896},{128,0},{256,128},{384,256},{512,384},{640,512},{768,640},... | collective-permute-start | bytes 786440 | tf_op jit(solution)/shard_map/ppermute | solution.py:13
  28.8 1.8 fusion.134
  30.7 2.1 fusion.133
  32.8 4.6 %compare_select_fusion.3 = s32[2048,1]{0,1:T(1,128)S(1)} fusion(s32[]{:T(128)} %bitcast.28, s32[]{:T(128)} %bitcast.29, s32[]{:T(128)} %bitcast.30, s32[]{:T(128)} %bitcast.31, s32[]{:T(128)} %bitcast.32, s32[]{:T(128)} %bitcast.34, s32[]{:T(128)} %bitcast.33, s32[]{:T(128)S(6)} %axis_index.15), kind=kLoop, calls=%fused_computation.201 | loop fusion | flops 116736 | bytes 8224 | tf_op jit(solution)/shard_map/jit(_take)/gather | solution.py:64
  37.4 15.6 %fusion.115 = s32[2048]{0:T(1024)S(1)} fusion(pred[2048]{0:T(1024)(128)(4,1)S(1)} %get-tuple-element.67, pred[2048]{0:T(1024)(128)(4,1)S(1)} %get-tuple-element.68, pred[2048]{0:T(1024)(128)(4,1)S(1)} %get-tuple-element.69, pred[2048]{0:T(1024)(128)(4,1)S(1)} %get-tuple-element.70, pred[2048]{0:T(1024)(128)(4,1)S(1)} %get-tuple-element.71, ...), kind=kLoop, calls=%fused_computation.256 | loop fusion | flops 163840 | bytes 67688 | tf_op jit(solution)/shard_map/add | solution.py:64
  53.0 1.0 convert_bitcast_fusion
  54.7 5.1 %collective-permute-start.9 = (bf16[128,256]{1,0:T(8,128)(2,1)S(1)}, bf16[128,256]{1,0:T(8,128)(2,1)S(1)}, u32[]{:S(2)}, u32[]{:S(2)}) collective-permute-start(bf16[128,256]{1,0:T(8,128)(2,1)S(1)} %collective-permute-done.8), channel_id=1, source_target_pairs={{0,120},{8,0},{16,8},{24,16},{32,24},{40,32},{48,40},{56,48},{64,5... | collective-permute-start | bytes 196616 | tf_op jit(solution)/shard_map/ppermute | solution.py:13
  59.9 1.9 collective-permute-start.1
  61.8 5.4 %collective-permute-start.10 = (bf16[128,256]{1,0:T(8,128)(2,1)S(1)}, bf16[128,256]{1,0:T(8,128)(2,1)}, u32[]{:S(2)}, u32[]{:S(2)}) collective-permute-start(bf16[128,256]{1,0:T(8,128)(2,1)S(1)} %collective-permute-done.9), channel_id=1, source_target_pairs={{0,120},{8,0},{16,8},{24,16},{32,24},{40,32},{48,40},{56,48},{64,5... | collective-permute-start | bytes 196616 | tf_op jit(solution)/shard_map/ppermute | solution.py:13
  67.3 1.9 collective-permute-start.2
  69.2 1.0 broadcast_compare_fusion.2
  70.2 1.1 copy.170
  71.4 3.3 %collective-permute-done.2 = bf16[128,256]{1,0:T(8,128)(2,1)} collective-permute-done((bf16[128,256]{1,0:T(8,128)(2,1)S(1)}, bf16[128,256]{1,0:T(8,128)(2,1)}, u32[]{:S(2)}, u32[]{:S(2)}) %collective-permute-start.2) | collective-permute-done | bytes 65568 | tf_op jit(solution)/shard_map/ppermute | solution.py:13
  74.7 1.9 collective-permute-start.3
  76.7 0.9 pad_maximum_fusion
  78.0 5.1 %collective-permute-start.11 = (bf16[128,256]{1,0:T(8,128)(2,1)}, bf16[128,256]{1,0:T(8,128)(2,1)}, u32[]{:S(2)}, u32[]{:S(2)}) collective-permute-start(bf16[128,256]{1,0:T(8,128)(2,1)} %collective-permute-done.10), channel_id=1, source_target_pairs={{0,120},{8,0},{16,8},{24,16},{32,24},{40,32},{48,40},{56,48},{64,5... | collective-permute-start | bytes 196616 | tf_op jit(solution)/shard_map/ppermute | solution.py:13
  83.9 4.8 %all-to-all-start = ((bf16[16,8,1024]{2,0,1:T(8,128)(2,1)}), bf16[16,8,1024]{2,0,1:T(8,128)(2,1)S(1)}, u32[]{:S(2)}, u32[]{:S(2)}) async-start(bf16[16,8,1024]{2,0,1:T(8,128)(2,1)} %bitcast.319), calls=%async_computation | async-start | bytes 524288 | tf_op jit(solution)/shard_map/all_to_all | solution.py:28
  88.7 0.8 constant_dynamic-update-slice_fusion.7
  89.5 0.8 constant_dynamic-update-slice_fusion.6
  90.3 0.8 constant_dynamic-update-slice_fusion.5
  91.2 0.8 constant_dynamic-update-slice_fusion.4
  92.0 2.7 %fusion.20 = (f32[8,128]{1,0:T(8,128)S(1)}, f32[512,128,8]{1,0,2:T(8,128)}) fusion(pred[128,512]{0,1:T(8,128)(4,1)} %get-tuple-element.23, bf16[128,8,128]{0,2,1:T(8,128)(2,1)S(1)} %bitcast.321, bf16[512,256]{1,0:T(8,128)(2,1)S(1)} %constant_dynamic-update-slice_fusion.4), kind=kOutput, calls=%fused_computation.33 | convolution fusion | flops 135789568 | bytes 2560000 | tf_op jit(solution)/shard_map/iged,jgd->geij/dot_general | solution.py:69
  94.7 1.9 collective-permute-start.4
  96.6 5.1 %collective-permute-start.12 = (bf16[128,256]{1,0:T(8,128)(2,1)}, bf16[128,256]{1,0:T(8,128)(2,1)S(1)}, u32[]{:S(2)}, u32[]{:S(2)}) collective-permute-start(bf16[128,256]{1,0:T(8,128)(2,1)} %collective-permute-done.11), channel_id=1, source_target_pairs={{0,120},{8,0},{16,8},{24,16},{32,24},{40,32},{48,40},{56,48},{64,5... | collective-permute-start | bytes 196616 | tf_op jit(solution)/shard_map/ppermute | solution.py:13
  101.8 0.9 constant_dynamic-update-slice_fusion.11
  102.6 1.3 collective-permute-done.12
  104.0 5.4 %collective-permute-start.13 = (bf16[128,256]{1,0:T(8,128)(2,1)S(1)}, bf16[128,256]{1,0:T(8,128)(2,1)S(1)}, u32[]{:S(2)}, u32[]{:S(2)}) collective-permute-start(bf16[128,256]{1,0:T(8,128)(2,1)S(1)} %collective-permute-done.12), channel_id=1, source_target_pairs={{0,120},{8,0},{16,8},{24,16},{32,24},{40,32},{48,40},{56,48},{64,5... | collective-permute-start | bytes 196616 | tf_op jit(solution)/shard_map/ppermute | solution.py:13
  109.4 1.9 collective-permute-start.5
  111.3 5.4 %collective-permute-start.14 = (bf16[128,256]{1,0:T(8,128)(2,1)S(1)}, bf16[128,256]{1,0:T(8,128)(2,1)S(1)}, u32[]{:S(2)}, u32[]{:S(2)}) collective-permute-start(bf16[128,256]{1,0:T(8,128)(2,1)S(1)} %collective-permute-done.13), channel_id=1, source_target_pairs={{0,120},{8,0},{16,8},{24,16},{32,24},{40,32},{48,40},{56,48},{64,5... | collective-permute-start | bytes 196616 | tf_op jit(solution)/shard_map/ppermute | solution.py:13
  116.7 1.9 collective-permute-start.6
  118.7 5.5 %collective-permute-done.6 = bf16[128,256]{1,0:T(8,128)(2,1)} collective-permute-done((bf16[128,256]{1,0:T(8,128)(2,1)S(1)}, bf16[128,256]{1,0:T(8,128)(2,1)}, u32[]{:S(2)}, u32[]{:S(2)}) %collective-permute-start.6) | collective-permute-done | bytes 65568 | tf_op jit(solution)/shard_map/ppermute | solution.py:13
  124.2 2.1 collective-permute-start.7
  127.0 1.7 fusion.8
  128.9 0.8 multiply_reduce_fusion
  130.1 0.9 copy.119
  131.0 0.9 collective-permute-done.7
  131.9 0.8 constant_dynamic-update-slice_fusion.3
  132.7 0.8 constant_dynamic-update-slice_fusion.2
  133.6 0.8 constant_dynamic-update-slice_fusion.1
  134.4 0.8 constant_dynamic-update-slice_fusion
  135.3 1.3 fusion.26
  136.6 3.3 %fusion.23 = (f32[8,128]{1,0:T(8,128)S(1)}, f32[8,128]{1,0:T(8,128)S(1)}, f32[8,128]{1,0:T(8,128)S(1)}, f32[8,128]{1,0:T(8,128)S(1)}) fusion(f32[512,128,8]{1,0,2:T(8,128)S(1)} %copy-done, f32[8,128]{1,0:T(8,128)S(1)} %maximum_maximum_fusion, pred[128,512]{0,1:T(8,128)(4,1)S(1)} %copy-done.2, f32[512,128,8]{1,0,2:T(8,128)S(1)} %get-tuple-element.62, ...), kind=kLoop, calls=%fused_computation.36 | loop fusion | flops 8384512 | bytes 8671232 | tf_op jit(solution)/shard_map/reduce_sum | solution.py:85
  144.8 0.9 copy-done.1
  147.9 4.4 %collective-permute-start.16 = (f32[128,256]{0,1:T(8,128)S(1)}, f32[128,256]{0,1:T(8,128)S(1)}, u32[]{:S(2)}, u32[]{:S(2)}) collective-permute-start(f32[128,256]{0,1:T(8,128)S(1)} %fusion.80), channel_id=1, source_target_pairs={{0,120},{8,0},{16,8},{24,16},{32,24},{40,32},{48,40},{56,48},{64,5... | collective-permute-start | bytes 393224 | tf_op jit(solution)/shard_map/ppermute | solution.py:13
  153.1 1.9 collective-permute-start.24
  156.0 5.1 %collective-permute-start.17 = (f32[128,256]{0,1:T(8,128)S(1)}, f32[128,256]{0,1:T(8,128)S(1)}, u32[]{:S(2)}, u32[]{:S(2)}) collective-permute-start(f32[128,256]{0,1:T(8,128)S(1)} %fusion.82), channel_id=1, source_target_pairs={{0,120},{8,0},{16,8},{24,16},{32,24},{40,32},{48,40},{56,48},{64,5... | collective-permute-start | bytes 393224 | tf_op jit(solution)/shard_map/ppermute | solution.py:13
  161.2 1.9 collective-permute-start.25
  163.6 5.6 %collective-permute-start.18 = (f32[128,256]{0,1:T(8,128)S(1)}, f32[128,256]{0,1:T(8,128)S(1)}, u32[]{:S(2)}, u32[]{:S(2)}) collective-permute-start(f32[128,256]{0,1:T(8,128)S(1)} %fusion.79), channel_id=1, source_target_pairs={{0,120},{8,0},{16,8},{24,16},{32,24},{40,32},{48,40},{56,48},{64,5... | collective-permute-start | bytes 393224 | tf_op jit(solution)/shard_map/ppermute | solution.py:13
  169.5 1.9 collective-permute-start.26
  171.5 1.2 collective-permute-done.18
  172.7 5.6 %collective-permute-start.19 = (f32[128,256]{0,1:T(8,128)S(1)}, f32[128,256]{0,1:T(8,128)S(1)}, u32[]{:S(2)}, u32[]{:S(2)}) collective-permute-start(f32[128,256]{0,1:T(8,128)S(1)} %fusion.93), channel_id=1, source_target_pairs={{0,120},{8,0},{16,8},{24,16},{32,24},{40,32},{48,40},{56,48},{64,5... | collective-permute-start | bytes 393224 | tf_op jit(solution)/shard_map/ppermute | solution.py:13
  179.0 1.9 collective-permute-start.27
  181.4 5.6 %collective-permute-start.20 = (f32[128,256]{0,1:T(8,128)S(1)}, f32[128,256]{0,1:T(8,128)S(1)}, u32[]{:S(2)}, u32[]{:S(2)}) collective-permute-start(f32[128,256]{0,1:T(8,128)S(1)} %fusion.75), channel_id=1, source_target_pairs={{0,120},{8,0},{16,8},{24,16},{32,24},{40,32},{48,40},{56,48},{64,5... | collective-permute-start | bytes 393224 | tf_op jit(solution)/shard_map/ppermute | solution.py:13
  187.7 1.9 collective-permute-start.28
  189.6 5.5 %collective-permute-start.21 = (f32[128,256]{0,1:T(8,128)S(1)}, f32[128,256]{0,1:T(8,128)S(1)}, u32[]{:S(2)}, u32[]{:S(2)}) collective-permute-start(f32[128,256]{0,1:T(8,128)S(1)} %fusion.77), channel_id=1, source_target_pairs={{0,120},{8,0},{16,8},{24,16},{32,24},{40,32},{48,40},{56,48},{64,5... | collective-permute-start | bytes 393224 | tf_op jit(solution)/shard_map/ppermute | solution.py:13
  195.8 1.9 collective-permute-start.29
  197.7 5.5 %collective-permute-start.22 = (f32[128,256]{0,1:T(8,128)S(1)}, f32[128,256]{0,1:T(8,128)S(1)}, u32[]{:S(2)}, u32[]{:S(2)}) collective-permute-start(f32[128,256]{0,1:T(8,128)S(1)} %fusion.73), channel_id=1, source_target_pairs={{0,120},{8,0},{16,8},{24,16},{32,24},{40,32},{48,40},{56,48},{64,5... | collective-permute-start | bytes 393224 | tf_op jit(solution)/shard_map/ppermute | solution.py:13
  203.9 1.9 collective-permute-start.30
  205.8 5.5 %collective-permute-start.23 = (f32[128,256]{0,1:T(8,128)S(1)}, f32[128,256]{0,1:T(8,128)S(1)}, u32[]{:S(2)}, u32[]{:S(2)}) collective-permute-start(f32[128,256]{0,1:T(8,128)S(1)} %fusion.92), channel_id=1, source_target_pairs={{0,120},{8,0},{16,8},{24,16},{32,24},{40,32},{48,40},{56,48},{64,5... | collective-permute-start | bytes 393224 | tf_op jit(solution)/shard_map/ppermute | solution.py:13
  211.7 0.9 copy.147
  212.6 1.3 collective-permute-done.23
  (118 shorter events, 19.7 us)
Async XLA Ops:
  0.6 76.0 %copy-start.8 = (bf16[1,128,128]{2,1,0:T(8,128)(2,1)S(1)}, bf16[1,128,128]{2,1,0:T(8,128)(2,1)}, u32[]{:S(2)}) copy-start(bf16[1,128,128]{2,1,0:T(8,128)(2,1)} %param.8) | copy-start | bytes 98308
  0.6 76.0 %copy-start.9 = (bf16[1,128,128]{2,1,0:T(8,128)(2,1)S(1)}, bf16[1,128,128]{2,1,0:T(8,128)(2,1)}, u32[]{:S(2)}) copy-start(bf16[1,128,128]{2,1,0:T(8,128)(2,1)} %param.7) | copy-start | bytes 98308
  1.5 53.2 %collective-permute-start.8 = (bf16[128,256]{1,0:T(8,128)(2,1)S(1)}, bf16[128,256]{1,0:T(8,128)(2,1)S(1)}, u32[]{:S(2)}, u32[]{:S(2)}) collective-permute-start(bf16[128,256]{1,0:T(8,128)(2,1)S(1)} %pad_maximum_fusion.5), channel_id=1, source_target_pairs={{0,120},{8,0},{16,8},{24,16},{32,24},{40,32},{48,40},{56,48},{64,5... | collective-permute-start | bytes 196616 | tf_op jit(solution)/shard_map/ppermute | solution.py:13
  19.7 40.2 %collective-permute-start = (bf16[128,256]{1,0:T(8,128)(2,1)S(1)}, bf16[128,256]{1,0:T(8,128)(2,1)S(1)}, u32[]{:S(2)}, u32[]{:S(2)}) collective-permute-start(bf16[128,256]{1,0:T(8,128)(2,1)S(1)} %pad_maximum_fusion.5), channel_id=1, source_target_pairs={{0,8},{8,16},{16,24},{24,32},{32,40},{40,48},{48,56},{56,64},{64,7... | collective-permute-start | bytes 196616 | tf_op jit(solution)/shard_map/ppermute | solution.py:13
  21.6 61.5 %collective-permute-start.15 = (bf16[16,8192]{1,0:T(8,128)(2,1)}, bf16[16,8192]{1,0:T(8,128)(2,1)S(1)}, u32[]{:S(2)}, u32[]{:S(2)}) collective-permute-start(bf16[16,8192]{1,0:T(8,128)(2,1)} %bitcast.342), channel_id=1, source_target_pairs={{0,896},{128,0},{256,128},{384,256},{512,384},{640,512},{768,640},... | collective-permute-start | bytes 786440 | tf_op jit(solution)/shard_map/ppermute | solution.py:13
  54.7 7.1 %collective-permute-start.9 = (bf16[128,256]{1,0:T(8,128)(2,1)S(1)}, bf16[128,256]{1,0:T(8,128)(2,1)S(1)}, u32[]{:S(2)}, u32[]{:S(2)}) collective-permute-start(bf16[128,256]{1,0:T(8,128)(2,1)S(1)} %collective-permute-done.8), channel_id=1, source_target_pairs={{0,120},{8,0},{16,8},{24,16},{32,24},{40,32},{48,40},{56,48},{64,5... | collective-permute-start | bytes 196616 | tf_op jit(solution)/shard_map/ppermute | solution.py:13
  59.9 9.3 %copy-start.10 = (bf16[128,256]{1,0:T(8,128)(2,1)}, bf16[128,256]{1,0:T(8,128)(2,1)S(1)}, u32[]{:S(2)}) copy-start(bf16[128,256]{1,0:T(8,128)(2,1)S(1)} %collective-permute-done) | copy-start | bytes 196612
  59.9 7.4 %collective-permute-start.1 = (bf16[128,256]{1,0:T(8,128)(2,1)S(1)}, bf16[128,256]{1,0:T(8,128)(2,1)S(1)}, u32[]{:S(2)}, u32[]{:S(2)}) collective-permute-start(bf16[128,256]{1,0:T(8,128)(2,1)S(1)} %collective-permute-done), channel_id=1, source_target_pairs={{0,8},{8,16},{16,24},{24,32},{32,40},{40,48},{48,56},{56,64},{64,7... | collective-permute-start | bytes 196616 | tf_op jit(solution)/shard_map/ppermute | solution.py:13
  61.8 14.8 %collective-permute-start.10 = (bf16[128,256]{1,0:T(8,128)(2,1)S(1)}, bf16[128,256]{1,0:T(8,128)(2,1)}, u32[]{:S(2)}, u32[]{:S(2)}) collective-permute-start(bf16[128,256]{1,0:T(8,128)(2,1)S(1)} %collective-permute-done.9), channel_id=1, source_target_pairs={{0,120},{8,0},{16,8},{24,16},{32,24},{40,32},{48,40},{56,48},{64,5... | collective-permute-start | bytes 196616 | tf_op jit(solution)/shard_map/ppermute | solution.py:13
  67.3 9.4 %copy-start.12 = (bf16[128,256]{1,0:T(8,128)(2,1)}, bf16[128,256]{1,0:T(8,128)(2,1)S(1)}, u32[]{:S(2)}) copy-start(bf16[128,256]{1,0:T(8,128)(2,1)S(1)} %collective-permute-done.1) | copy-start | bytes 196612
  67.3 7.5 %collective-permute-start.2 = (bf16[128,256]{1,0:T(8,128)(2,1)S(1)}, bf16[128,256]{1,0:T(8,128)(2,1)}, u32[]{:S(2)}, u32[]{:S(2)}) collective-permute-start(bf16[128,256]{1,0:T(8,128)(2,1)S(1)} %collective-permute-done.1), channel_id=1, source_target_pairs={{0,8},{8,16},{16,24},{24,32},{32,40},{40,48},{48,56},{56,64},{64,7... | collective-permute-start | bytes 196616 | tf_op jit(solution)/shard_map/ppermute | solution.py:13
  74.7 13.9 %collective-permute-start.3 = (bf16[128,256]{1,0:T(8,128)(2,1)}, bf16[128,256]{1,0:T(8,128)(2,1)}, u32[]{:S(2)}, u32[]{:S(2)}) collective-permute-start(bf16[128,256]{1,0:T(8,128)(2,1)} %collective-permute-done.2), channel_id=1, source_target_pairs={{0,8},{8,16},{16,24},{24,32},{32,40},{40,48},{48,56},{56,64},{64,7... | collective-permute-start | bytes 196616 | tf_op jit(solution)/shard_map/ppermute | solution.py:13
  78.0 18.6 %collective-permute-start.11 = (bf16[128,256]{1,0:T(8,128)(2,1)}, bf16[128,256]{1,0:T(8,128)(2,1)}, u32[]{:S(2)}, u32[]{:S(2)}) collective-permute-start(bf16[128,256]{1,0:T(8,128)(2,1)} %collective-permute-done.10), channel_id=1, source_target_pairs={{0,120},{8,0},{16,8},{24,16},{32,24},{40,32},{48,40},{56,48},{64,5... | collective-permute-start | bytes 196616 | tf_op jit(solution)/shard_map/ppermute | solution.py:13
  83.9 44.9 %all-to-all-start = ((bf16[16,8,1024]{2,0,1:T(8,128)(2,1)}), bf16[16,8,1024]{2,0,1:T(8,128)(2,1)S(1)}, u32[]{:S(2)}, u32[]{:S(2)}) async-start(bf16[16,8,1024]{2,0,1:T(8,128)(2,1)} %bitcast.319), calls=%async_computation | async-start | bytes 524288 | tf_op jit(solution)/shard_map/all_to_all | solution.py:28
  92.0 34.3 %copy-start.4 = (bf16[512,256]{1,0:T(8,128)(2,1)}, bf16[512,256]{1,0:T(8,128)(2,1)S(1)}, u32[]{:S(2)}) copy-start(bf16[512,256]{1,0:T(8,128)(2,1)S(1)} %constant_dynamic-update-slice_fusion.4) | copy-start | bytes 786436
  94.7 14.6 %collective-permute-start.4 = (bf16[128,256]{1,0:T(8,128)(2,1)}, bf16[128,256]{1,0:T(8,128)(2,1)S(1)}, u32[]{:S(2)}, u32[]{:S(2)}) collective-permute-start(bf16[128,256]{1,0:T(8,128)(2,1)} %collective-permute-done.3), channel_id=1, source_target_pairs={{0,8},{8,16},{16,24},{24,32},{32,40},{40,48},{48,56},{56,64},{64,7... | collective-permute-start | bytes 196616 | tf_op jit(solution)/shard_map/ppermute | solution.py:13
  96.6 7.3 %collective-permute-start.12 = (bf16[128,256]{1,0:T(8,128)(2,1)}, bf16[128,256]{1,0:T(8,128)(2,1)S(1)}, u32[]{:S(2)}, u32[]{:S(2)}) collective-permute-start(bf16[128,256]{1,0:T(8,128)(2,1)} %collective-permute-done.11), channel_id=1, source_target_pairs={{0,120},{8,0},{16,8},{24,16},{32,24},{40,32},{48,40},{56,48},{64,5... | collective-permute-start | bytes 196616 | tf_op jit(solution)/shard_map/ppermute | solution.py:13
  104.0 7.3 %collective-permute-start.13 = (bf16[128,256]{1,0:T(8,128)(2,1)S(1)}, bf16[128,256]{1,0:T(8,128)(2,1)S(1)}, u32[]{:S(2)}, u32[]{:S(2)}) collective-permute-start(bf16[128,256]{1,0:T(8,128)(2,1)S(1)} %collective-permute-done.12), channel_id=1, source_target_pairs={{0,120},{8,0},{16,8},{24,16},{32,24},{40,32},{48,40},{56,48},{64,5... | collective-permute-start | bytes 196616 | tf_op jit(solution)/shard_map/ppermute | solution.py:13
  109.4 17.0 %copy-start.11 = (bf16[128,256]{1,0:T(8,128)(2,1)}, bf16[128,256]{1,0:T(8,128)(2,1)S(1)}, u32[]{:S(2)}) copy-start(bf16[128,256]{1,0:T(8,128)(2,1)S(1)} %collective-permute-done.4) | copy-start | bytes 196612
  109.4 7.4 %collective-permute-start.5 = (bf16[128,256]{1,0:T(8,128)(2,1)S(1)}, bf16[128,256]{1,0:T(8,128)(2,1)S(1)}, u32[]{:S(2)}, u32[]{:S(2)}) collective-permute-start(bf16[128,256]{1,0:T(8,128)(2,1)S(1)} %collective-permute-done.4), channel_id=1, source_target_pairs={{0,8},{8,16},{16,24},{24,32},{32,40},{40,48},{48,56},{56,64},{64,7... | collective-permute-start | bytes 196616 | tf_op jit(solution)/shard_map/ppermute | solution.py:13
  111.3 15.0 %collective-permute-start.14 = (bf16[128,256]{1,0:T(8,128)(2,1)S(1)}, bf16[128,256]{1,0:T(8,128)(2,1)S(1)}, u32[]{:S(2)}, u32[]{:S(2)}) collective-permute-start(bf16[128,256]{1,0:T(8,128)(2,1)S(1)} %collective-permute-done.13), channel_id=1, source_target_pairs={{0,120},{8,0},{16,8},{24,16},{32,24},{40,32},{48,40},{56,48},{64,5... | collective-permute-start | bytes 196616 | tf_op jit(solution)/shard_map/ppermute | solution.py:13
  116.7 9.6 %copy-start.13 = (bf16[128,256]{1,0:T(8,128)(2,1)}, bf16[128,256]{1,0:T(8,128)(2,1)S(1)}, u32[]{:S(2)}) copy-start(bf16[128,256]{1,0:T(8,128)(2,1)S(1)} %collective-permute-done.5) | copy-start | bytes 196612
  116.7 7.5 %collective-permute-start.6 = (bf16[128,256]{1,0:T(8,128)(2,1)S(1)}, bf16[128,256]{1,0:T(8,128)(2,1)}, u32[]{:S(2)}, u32[]{:S(2)}) collective-permute-start(bf16[128,256]{1,0:T(8,128)(2,1)S(1)} %collective-permute-done.5), channel_id=1, source_target_pairs={{0,8},{8,16},{16,24},{24,32},{32,40},{40,48},{48,56},{56,64},{64,7... | collective-permute-start | bytes 196616 | tf_op jit(solution)/shard_map/ppermute | solution.py:13
  124.2 7.7 %collective-permute-start.7 = (bf16[128,256]{1,0:T(8,128)(2,1)}, bf16[128,256]{1,0:T(8,128)(2,1)}, u32[]{:S(2)}, u32[]{:S(2)}) collective-permute-start(bf16[128,256]{1,0:T(8,128)(2,1)} %collective-permute-done.6), channel_id=1, source_target_pairs={{0,8},{8,16},{16,24},{24,32},{32,40},{40,48},{48,56},{56,64},{64,7... | collective-permute-start | bytes 196616 | tf_op jit(solution)/shard_map/ppermute | solution.py:13
  126.3 0.7 copy-start.6
  129.8 6.8 %copy-start.2 = (pred[128,512]{0,1:T(8,128)(4,1)S(1)}, pred[128,512]{0,1:T(8,128)(4,1)}, u32[]{:S(2)}) copy-start(pred[128,512]{0,1:T(8,128)(4,1)} %get-tuple-element.23) | copy-start | bytes 196612
  129.8 6.8 %copy-start.3 = (pred[128,512]{0,1:T(8,128)(4,1)S(1)}, pred[128,512]{0,1:T(8,128)(4,1)}, u32[]{:S(2)}) copy-start(pred[128,512]{0,1:T(8,128)(4,1)} %get-tuple-element.26) | copy-start | bytes 196612
  131.0 5.6 %copy-start = (f32[512,128,8]{1,0,2:T(8,128)S(1)}, f32[512,128,8]{1,0,2:T(8,128)}, u32[]{:S(2)}) copy-start(f32[512,128,8]{1,0,2:T(8,128)} %get-tuple-element.66) | copy-start | bytes 6291460
  141.1 1.0 copy-start.5
  144.1 1.6 copy-start.1
  145.7 0.9 copy-start.7
  147.9 8.0 %collective-permute-start.16 = (f32[128,256]{0,1:T(8,128)S(1)}, f32[128,256]{0,1:T(8,128)S(1)}, u32[]{:S(2)}, u32[]{:S(2)}) collective-permute-start(f32[128,256]{0,1:T(8,128)S(1)} %fusion.80), channel_id=1, source_target_pairs={{0,120},{8,0},{16,8},{24,16},{32,24},{40,32},{48,40},{56,48},{64,5... | collective-permute-start | bytes 393224 | tf_op jit(solution)/shard_map/ppermute | solution.py:13
  153.1 8.1 %collective-permute-start.24 = (f32[128,256]{0,1:T(8,128)S(1)}, f32[128,256]{0,1:T(8,128)S(1)}, u32[]{:S(2)}, u32[]{:S(2)}) collective-permute-start(f32[128,256]{0,1:T(8,128)S(1)} %fusion.69), channel_id=1, source_target_pairs={{0,8},{8,16},{16,24},{24,32},{32,40},{40,48},{48,56},{56,64},{64,7... | collective-permute-start | bytes 393224 | tf_op jit(solution)/shard_map/ppermute | solution.py:13
  156.0 7.6 %collective-permute-start.17 = (f32[128,256]{0,1:T(8,128)S(1)}, f32[128,256]{0,1:T(8,128)S(1)}, u32[]{:S(2)}, u32[]{:S(2)}) collective-permute-start(f32[128,256]{0,1:T(8,128)S(1)} %fusion.82), channel_id=1, source_target_pairs={{0,120},{8,0},{16,8},{24,16},{32,24},{40,32},{48,40},{56,48},{64,5... | collective-permute-start | bytes 393224 | tf_op jit(solution)/shard_map/ppermute | solution.py:13
  161.2 8.3 %collective-permute-start.25 = (f32[128,256]{0,1:T(8,128)S(1)}, f32[128,256]{0,1:T(8,128)S(1)}, u32[]{:S(2)}, u32[]{:S(2)}) collective-permute-start(f32[128,256]{0,1:T(8,128)S(1)} %fusion.71), channel_id=1, source_target_pairs={{0,8},{8,16},{16,24},{24,32},{32,40},{40,48},{48,56},{56,64},{64,7... | collective-permute-start | bytes 393224 | tf_op jit(solution)/shard_map/ppermute | solution.py:13
  163.6 9.0 %collective-permute-start.18 = (f32[128,256]{0,1:T(8,128)S(1)}, f32[128,256]{0,1:T(8,128)S(1)}, u32[]{:S(2)}, u32[]{:S(2)}) collective-permute-start(f32[128,256]{0,1:T(8,128)S(1)} %fusion.79), channel_id=1, source_target_pairs={{0,120},{8,0},{16,8},{24,16},{32,24},{40,32},{48,40},{56,48},{64,5... | collective-permute-start | bytes 393224 | tf_op jit(solution)/shard_map/ppermute | solution.py:13
  169.5 9.4 %collective-permute-start.26 = (f32[128,256]{0,1:T(8,128)S(1)}, f32[128,256]{0,1:T(8,128)S(1)}, u32[]{:S(2)}, u32[]{:S(2)}) collective-permute-start(f32[128,256]{0,1:T(8,128)S(1)} %fusion.68), channel_id=1, source_target_pairs={{0,8},{8,16},{16,24},{24,32},{32,40},{40,48},{48,56},{56,64},{64,7... | collective-permute-start | bytes 393224 | tf_op jit(solution)/shard_map/ppermute | solution.py:13
  172.7 8.8 %collective-permute-start.19 = (f32[128,256]{0,1:T(8,128)S(1)}, f32[128,256]{0,1:T(8,128)S(1)}, u32[]{:S(2)}, u32[]{:S(2)}) collective-permute-start(f32[128,256]{0,1:T(8,128)S(1)} %fusion.93), channel_id=1, source_target_pairs={{0,120},{8,0},{16,8},{24,16},{32,24},{40,32},{48,40},{56,48},{64,5... | collective-permute-start | bytes 393224 | tf_op jit(solution)/shard_map/ppermute | solution.py:13
  179.0 8.6 %collective-permute-start.27 = (f32[128,256]{0,1:T(8,128)S(1)}, f32[128,256]{0,1:T(8,128)S(1)}, u32[]{:S(2)}, u32[]{:S(2)}) collective-permute-start(f32[128,256]{0,1:T(8,128)S(1)} %fusion.91), channel_id=1, source_target_pairs={{0,8},{8,16},{16,24},{24,32},{32,40},{40,48},{48,56},{56,64},{64,7... | collective-permute-start | bytes 393224 | tf_op jit(solution)/shard_map/ppermute | solution.py:13
  181.4 8.1 %collective-permute-start.20 = (f32[128,256]{0,1:T(8,128)S(1)}, f32[128,256]{0,1:T(8,128)S(1)}, u32[]{:S(2)}, u32[]{:S(2)}) collective-permute-start(f32[128,256]{0,1:T(8,128)S(1)} %fusion.75), channel_id=1, source_target_pairs={{0,120},{8,0},{16,8},{24,16},{32,24},{40,32},{48,40},{56,48},{64,5... | collective-permute-start | bytes 393224 | tf_op jit(solution)/shard_map/ppermute | solution.py:13
  187.7 8.1 %collective-permute-start.28 = (f32[128,256]{0,1:T(8,128)S(1)}, f32[128,256]{0,1:T(8,128)S(1)}, u32[]{:S(2)}, u32[]{:S(2)}) collective-permute-start(f32[128,256]{0,1:T(8,128)S(1)} %fusion.89), channel_id=1, source_target_pairs={{0,8},{8,16},{16,24},{24,32},{32,40},{40,48},{48,56},{56,64},{64,7... | collective-permute-start | bytes 393224 | tf_op jit(solution)/shard_map/ppermute | solution.py:13
  189.6 8.1 %collective-permute-start.21 = (f32[128,256]{0,1:T(8,128)S(1)}, f32[128,256]{0,1:T(8,128)S(1)}, u32[]{:S(2)}, u32[]{:S(2)}) collective-permute-start(f32[128,256]{0,1:T(8,128)S(1)} %fusion.77), channel_id=1, source_target_pairs={{0,120},{8,0},{16,8},{24,16},{32,24},{40,32},{48,40},{56,48},{64,5... | collective-permute-start | bytes 393224 | tf_op jit(solution)/shard_map/ppermute | solution.py:13
  195.8 8.1 %collective-permute-start.29 = (f32[128,256]{0,1:T(8,128)S(1)}, f32[128,256]{0,1:T(8,128)S(1)}, u32[]{:S(2)}, u32[]{:S(2)}) collective-permute-start(f32[128,256]{0,1:T(8,128)S(1)} %fusion.84), channel_id=1, source_target_pairs={{0,8},{8,16},{16,24},{24,32},{32,40},{40,48},{48,56},{56,64},{64,7... | collective-permute-start | bytes 393224 | tf_op jit(solution)/shard_map/ppermute | solution.py:13
  197.7 8.1 %collective-permute-start.22 = (f32[128,256]{0,1:T(8,128)S(1)}, f32[128,256]{0,1:T(8,128)S(1)}, u32[]{:S(2)}, u32[]{:S(2)}) collective-permute-start(f32[128,256]{0,1:T(8,128)S(1)} %fusion.73), channel_id=1, source_target_pairs={{0,120},{8,0},{16,8},{24,16},{32,24},{40,32},{48,40},{56,48},{64,5... | collective-permute-start | bytes 393224 | tf_op jit(solution)/shard_map/ppermute | solution.py:13
  203.9 8.7 %collective-permute-start.30 = (f32[128,256]{0,1:T(8,128)S(1)}, f32[128,256]{0,1:T(8,128)S(1)}, u32[]{:S(2)}, u32[]{:S(2)}) collective-permute-start(f32[128,256]{0,1:T(8,128)S(1)} %fusion.90), channel_id=1, source_target_pairs={{0,8},{8,16},{16,24},{24,32},{32,40},{40,48},{48,56},{56,64},{64,7... | collective-permute-start | bytes 393224 | tf_op jit(solution)/shard_map/ppermute | solution.py:13
  205.8 8.0 %collective-permute-start.23 = (f32[128,256]{0,1:T(8,128)S(1)}, f32[128,256]{0,1:T(8,128)S(1)}, u32[]{:S(2)}, u32[]{:S(2)}) collective-permute-start(f32[128,256]{0,1:T(8,128)S(1)} %fusion.92), channel_id=1, source_target_pairs={{0,120},{8,0},{16,8},{24,16},{32,24},{40,32},{48,40},{56,48},{64,5... | collective-permute-start | bytes 393224 | tf_op jit(solution)/shard_map/ppermute | solution.py:13

commit v3 on v1

--- a/solution.py
+++ b/solution.py
@@ -43,7 +43,10 @@
     q_pos = place(me * rows, rows)
 
     kv = jnp.concatenate([keys[0], values[0]], axis=1)
-    kv_all = lax.all_gather(kv, "ctx", axis=0, tiled=True)
+    count = lax.axis_size("ctx")
+    kv_all = lax.all_to_all(
+        jnp.broadcast_to(kv[None], (count,) + kv.shape), "ctx", 0, 0, tiled=True
+    ).reshape(count * rows, 2 * kv_width)
     seq = kv_all.shape[0]
     k_all = kv_all[:, :kv_width].reshape(seq, groups, head_dim)
     v_all = kv_all[:, kv_width:].reshape(seq, groups, head_dim)

time: 193 us -> 197 us (1.021)
  starting transfers between devices: 19.1 us -> 29.3 us
  waiting for transfers between devices: 129 us -> 126 us
  other arithmetic: 9.23 us -> 6.36 us
    all_gather x1 -> x0, waiting for transfers between devices: 52.6 us -> none  [body(): kv_all = lax.all_gather(kv, 'ctx', axis=0, tiled=True)]
    all_to_all x0 -> x1, waiting for transfers between devices: none -> 47.4 us  [body(): lax.all_to_all(jnp.broadcast_to(kv[None], (count,) + kv.shape), 'ctx', 0,...]
    all_to_all x0 -> x1, starting transfers between devices: none -> 10.1 us  [body(): lax.all_to_all(jnp.broadcast_to(kv[None], (count,) + kv.shape), 'ctx', 0,...]
    ppermute x1, waiting for transfers between devices: 2.16 us -> 5.86 us  [passed_along(): return lax.ppermute(value, axis, pairs)]
  transfers between devices with their start and end apart: 4 -> 4, of which waited for: 4 -> 4; matrix products, arithmetic and copies ran while one was open for 6% -> 4% of each run, Pallas kernels for 0% -> 0%
where the time goes in v3:
time: 197 us; the launch traced here: 196 us
  waiting for transfers between devices  126 us (64%)
  starting transfers between devices  29.3 us (15%)
  matrix products  15.4 us (8%)
  between operations  14.4 us (7%)
  other arithmetic  6.36 us (3%)
  local copies, waits for them, and re-layouts  5.28 us (3%)
    reduce_scatter x1, waiting for transfers between devices, body(): dkv = lax.psum_scatter(dkv, 'ctx', scatter_dimension=0, tiled=True)  67.8 us
    all_to_all x1, waiting for transfers between devices, body(): lax.all_to_all(jnp.broadcast_to(kv[None], (count,) + kv.shape), 'ctx', 0,...  47.4 us
    all_to_all x1, starting transfers between devices, body(): lax.all_to_all(handed, 'tp', split_axis=1, concat_axis=0, tiled=True)  13.8 us
    all_to_all x1, starting transfers between devices, body(): lax.all_to_all(jnp.broadcast_to(kv[None], (count,) + kv.shape), 'ctx', 0,...  10.1 us
    ppermute x1, waiting for transfers between devices, passed_along(): return lax.ppermute(value, axis, pairs)  5.86 us
    ppermute x1, starting transfers between devices, passed_along(): return lax.ppermute(value, axis, pairs)  5.38 us
    dot_general x4, matrix products, body(): jnp.einsum('geij,jgd->iged', dscore, k_c, preferred_element_type=jnp.floa...  5.04 us
    dot_general x4, matrix products, body(): jnp.einsum('iged,jgd->geij', do_local, v_c, preferred_element_type=jnp.fl...  4.78 us
  transfers between devices with their start and end apart: 4, of which 4 were waited for; matrix products, arithmetic and copies ran while one was open for 4% of the time, Pallas kernels for 0%

profile of v3, /device:TPU:6, one launch (start us, length us, event | category | flops | bytes accessed | tf_op | source)
XLA Modules:
  0.0 196.5 jit_solution(10496952004043365388)
XLA Ops:
  7.2 5.4 %collective-permute-start = (bf16[16,8192]{1,0:T(8,128)(2,1)}, bf16[16,8192]{1,0:T(8,128)(2,1)S(1)}, u32[]{:S(2)}, u32[]{:S(2)}) collective-permute-start(bf16[16,8192]{1,0:T(8,128)(2,1)} %bitcast.314), channel_id=1, source_target_pairs={{0,896},{128,0},{256,128},{384,256},{512,384},{640,512},{768,640},... | collective-permute-start | bytes 786440 | tf_op jit(solution)/shard_map/ppermute | solution.py:13
  12.5 5.9 %collective-permute-done = bf16[16,8192]{1,0:T(8,128)(2,1)S(1)} collective-permute-done((bf16[16,8192]{1,0:T(8,128)(2,1)}, bf16[16,8192]{1,0:T(8,128)(2,1)S(1)}, u32[]{:S(2)}, u32[]{:S(2)}) %collective-permute-start) | collective-permute-done | bytes 262176 | tf_op jit(solution)/shard_map/ppermute | solution.py:13
  18.4 0.0 copy-start.6
  18.4 0.7 copy.164
  19.1 0.0 copy-start.5
  19.1 13.8 %all-to-all-start.1 = ((bf16[16,8,1024]{2,0,1:T(8,128)(2,1)}), bf16[16,8,1024]{2,0,1:T(8,128)(2,1)S(1)}, u32[]{:S(2)}, u32[]{:S(2)}) async-start(bf16[16,8,1024]{2,0,1:T(8,128)(2,1)} %bitcast.273), calls=%async_computation.1 | async-start | bytes 524288 | tf_op jit(solution)/shard_map/all_to_all | solution.py:28
  32.9 0.8 pad_maximum_fusion
  33.7 4.6 %all-to-all-done.1 = bf16[16,8,1024]{2,0,1:T(8,128)(2,1)S(1)} async-done(((bf16[16,8,1024]{2,0,1:T(8,128)(2,1)}), bf16[16,8,1024]{2,0,1:T(8,128)(2,1)S(1)}, u32[]{:S(2)}, u32[]{:S(2)}) %all-to-all-start.1) | async-done | bytes 262176 | tf_op jit(solution)/shard_map/all_to_all | solution.py:28
  38.4 1.1 broadcast_in_dim.117
  39.5 0.0 copy-start.8
  39.5 10.1 %all-to-all-start = ((bf16[16,128,256]{2,1,0:T(8,128)(2,1)}), bf16[16,128,256]{2,1,0:T(8,128)(2,1)S(1)}, u32[]{:S(2)}, u32[]{:S(2)}) async-start(bf16[16,128,256]{2,1,0:T(8,128)(2,1)} %broadcast_in_dim.117), calls=%async_computation | async-start | bytes 2097152 | tf_op jit(solution)/shard_map/all_to_all | solution.py:47
  49.6 0.0 reduce-scatter.2.cloned.1.call-start
  49.6 0.0 copy-done.6
  49.7 0.0 copy-done.5
  49.8 0.1 copy.121
  49.9 0.0 copy-done.8
  49.9 0.1 select_reduce_fusion.1
  50.0 0.1 select_reduce_fusion
  50.1 0.3 broadcast_compare_fusion.2
  50.5 0.0 copy-start.3
  50.5 0.8 copy.120
  51.3 0.1 copy.122
  51.4 0.2 multiply_reduce_fusion
  51.7 47.4 %all-to-all-done = bf16[16,128,256]{2,1,0:T(8,128)(2,1)S(1)} async-done(((bf16[16,128,256]{2,1,0:T(8,128)(2,1)}), bf16[16,128,256]{2,1,0:T(8,128)(2,1)S(1)}, u32[]{:S(2)}, u32[]{:S(2)}) %all-to-all-start) | async-done | bytes 1048608 | tf_op jit(solution)/shard_map/all_to_all | solution.py:47
  99.1 0.0 copy-start.2
  99.1 0.5 fusion.26
  99.6 0.5 fusion.8
  100.0 0.5 fusion.14
  100.5 0.5 fusion.20
  101.0 0.0 copy-start.7
  101.0 1.7 fusion.23
  102.8 0.0 copy-done.7
  102.8 0.5 convolution_bitcast_fusion.3
  103.3 0.0 copy-done.3
  103.3 0.5 convolution_bitcast_fusion.2
  103.8 0.0 copy-start.4
  103.8 0.7 fusion.36
  104.6 0.0 copy-done.2
  104.6 0.1 copy-done.4
  104.6 0.7 fusion.37
  105.4 0.5 convolution_bitcast_fusion.1
  105.9 1.7 fusion.38
  107.6 0.5 convolution_bitcast_fusion
  108.1 1.6 fusion.39
  109.7 0.0 copy-start
  109.7 0.4 convolution_bitcast_fusion.7
  110.2 0.4 convolution_bitcast_fusion.6
  110.6 0.4 convolution_bitcast_fusion.5
  111.1 0.0 copy-done
  111.1 0.4 convolution_bitcast_fusion.4
  111.5 1.5 maximum_maximum_fusion
  113.0 0.0 reduce-scatter.2.cloned.1.call-update
  113.0 1.2 fusion.67
  114.3 0.0 copy-start.1
  114.3 1.3 convolution_add_fusion.2
  115.6 1.2 convolution_add_fusion.1
  116.8 0.0 copy-done.1
  116.9 1.2 fusion.41
  118.1 0.8 copy.105
  119.0 67.8 %reduce-scatter.2.cloned.1.call-done = f32[128,256]{1,0:T(8,128)} async-done(((f32[2048,256]{1,0:T(8,128)}), f32[128,256]{1,0:T(8,128)}) %reduce-scatter.2.cloned.1.call-update) | async-done | bytes 131088 | tf_op jit(solution)/shard_map/reduce_scatter | solution.py:94
  186.7 1.5 fusion.89
  188.2 1.5 fusion.88
  (11 shorter events, 0.2 us)
Async XLA Ops:
  7.2 11.2 %collective-permute-start = (bf16[16,8192]{1,0:T(8,128)(2,1)}, bf16[16,8192]{1,0:T(8,128)(2,1)S(1)}, u32[]{:S(2)}, u32[]{:S(2)}) collective-permute-start(bf16[16,8192]{1,0:T(8,128)(2,1)} %bitcast.314), channel_id=1, source_target_pairs={{0,896},{128,0},{256,128},{384,256},{512,384},{640,512},{768,640},... | collective-permute-start | bytes 786440 | tf_op jit(solution)/shard_map/ppermute | solution.py:13
  18.4 31.2 %copy-start.6 = (bf16[1,128,1024]{2,1,0:T(8,128)(2,1)S(1)}, bf16[1,128,1024]{2,1,0:T(8,128)(2,1)}, u32[]{:S(2)}) copy-start(bf16[1,128,1024]{2,1,0:T(8,128)(2,1)} %param.6) | copy-start | bytes 786436
  19.1 30.6 %copy-start.5 = (bf16[1,128,1024]{2,1,0:T(8,128)(2,1)S(1)}, bf16[1,128,1024]{2,1,0:T(8,128)(2,1)}, u32[]{:S(2)}) copy-start(bf16[1,128,1024]{2,1,0:T(8,128)(2,1)} %param.9) | copy-start | bytes 786436
  19.1 19.2 %all-to-all-start.1 = ((bf16[16,8,1024]{2,0,1:T(8,128)(2,1)}), bf16[16,8,1024]{2,0,1:T(8,128)(2,1)S(1)}, u32[]{:S(2)}, u32[]{:S(2)}) async-start(bf16[16,8,1024]{2,0,1:T(8,128)(2,1)} %bitcast.273), calls=%async_computation.1 | async-start | bytes 524288 | tf_op jit(solution)/shard_map/all_to_all | solution.py:28
  39.5 10.4 %copy-start.8 = (s32[1,32]{1,0:T(1,128)S(1)}, s32[1,32]{1,0:T(1,128)}, u32[]{:S(2)}) copy-start(s32[1,32]{1,0:T(1,128)} %param.11) | copy-start | bytes 388
  39.5 59.6 %all-to-all-start = ((bf16[16,128,256]{2,1,0:T(8,128)(2,1)}), bf16[16,128,256]{2,1,0:T(8,128)(2,1)S(1)}, u32[]{:S(2)}, u32[]{:S(2)}) async-start(bf16[16,128,256]{2,1,0:T(8,128)(2,1)} %broadcast_in_dim.117), calls=%async_computation | async-start | bytes 2097152 | tf_op jit(solution)/shard_map/all_to_all | solution.py:47
  49.6 137.2 %reduce-scatter.2.cloned.1.call-start = ((), (), s32[]{:S(2)}) async-start(), calls=%async_computation.3 | async-start | bytes 2228224 | tf_op jit(solution)/shard_map/reduce_scatter | solution.py:94
  50.5 52.8 %copy-start.3 = (pred[128,512]{0,1:T(8,128)(4,1)}, pred[128,512]{0,1:T(8,128)(4,1)S(1)}, u32[]{:S(2)}) copy-start(pred[128,512]{0,1:T(8,128)(4,1)S(1)} %get-tuple-element.23) | copy-start | bytes 196612
  99.1 5.5 %copy-start.2 = (bf16[16,128,256]{2,1,0:T(8,128)(2,1)}, bf16[16,128,256]{2,1,0:T(8,128)(2,1)S(1)}, u32[]{:S(2)}) copy-start(bf16[16,128,256]{2,1,0:T(8,128)(2,1)S(1)} %all-to-all-done) | copy-start | bytes 3145732
  101.0 1.8 copy-start.7
  103.8 0.8 copy-start.4
  109.7 1.3 copy-start
  114.3 2.6 %copy-start.1 = (bf16[8,128,512]{1,2,0:T(8,128)(2,1)S(1)}, bf16[8,128,512]{1,2,0:T(8,128)(2,1)}, u32[]{:S(2)}) copy-start(bf16[8,128,512]{1,2,0:T(8,128)(2,1)} %copy-done) | copy-start | bytes 3145732
Sparse Core Ops, SparseCore 0:
  113.1 73.5 reduce-scatter.1

commit v4 on v1

--- a/solution.py
+++ b/solution.py
@@ -88,7 +88,11 @@
         dks.append(dkey.reshape(width, kv_width))
         dvs.append(dvalue.reshape(width, kv_width))
     dkv = jnp.concatenate([jnp.concatenate(dks, axis=0), jnp.concatenate(dvs, axis=0)], axis=1)
-    dkv = lax.psum_scatter(dkv, "ctx", scatter_dimension=0, tiled=True)
+    count = lax.axis_size("ctx")
+    dkv = lax.all_to_all(
+        dkv.astype(jnp.bfloat16).reshape(count, rows, 2 * kv_width), "ctx", 0, 0, tiled=True
+    )
+    dkv = jnp.sum(dkv.astype(jnp.float32), axis=0)
     dkey = dkv[:, :kv_width]
     dvalue = dkv[:, kv_width:]
     grad_query = (scale * dquery).reshape(rows, heads * head_dim).astype(jnp.bfloat16)[None]

time: 193 us -> 161 us (0.83)
  waiting for transfers between devices: 129 us -> 91.9 us
  starting transfers between devices: 19.1 us -> 27 us
    reduce_scatter x1 -> x0, waiting for transfers between devices: 68.8 us -> none  [body(): dkv = lax.psum_scatter(dkv, 'ctx', scatter_dimension=0, tiled=True)]
    all_to_all x0 -> x1, waiting for transfers between devices: none -> 32.1 us  [body(): lax.all_to_all(dkv.astype(jnp.bfloat16).reshape(count, rows, 2 * kv_width...]
    all_to_all x0 -> x1, starting transfers between devices: none -> 7.87 us  [body(): lax.all_to_all(dkv.astype(jnp.bfloat16).reshape(count, rows, 2 * kv_width...]
  transfers between devices with their start and end apart: 4 -> 4, of which waited for: 4 -> 4; matrix products, arithmetic and copies ran while one was open for 6% -> 7% of each run, Pallas kernels for 0% -> 0%
where the time goes in v4:
time: 161 us
  waiting for transfers between devices  91.9 us (57%)
  starting transfers between devices  27 us (17%)
  matrix products  15 us (9%)
  between operations  14.4 us (9%)
  other arithmetic  8.3 us (5%)
  local copies, waits for them, and re-layouts  4.01 us (2%)
    all_gather x1, waiting for transfers between devices, body(): kv_all = lax.all_gather(kv, 'ctx', axis=0, tiled=True)  52.6 us
    all_to_all x1, waiting for transfers between devices, body(): lax.all_to_all(dkv.astype(jnp.bfloat16).reshape(count, rows, 2 * kv_width...  32.1 us
    all_to_all x1, starting transfers between devices, body(): lax.all_to_all(handed, 'tp', split_axis=1, concat_axis=0, tiled=True)  13.7 us
    all_to_all x1, starting transfers between devices, body(): lax.all_to_all(dkv.astype(jnp.bfloat16).reshape(count, rows, 2 * kv_width...  7.87 us
    dot_general x4, matrix products, body(): jnp.einsum('geij,jgd->iged', dscore, k_c, preferred_element_type=jnp.floa...  5.42 us
    ppermute x1, starting transfers between devices, passed_along(): return lax.ppermute(value, axis, pairs)  5.38 us
    all_to_all x1, waiting for transfers between devices, body(): lax.all_to_all(handed, 'tp', split_axis=1, concat_axis=0, tiled=True)  5.08 us
  transfers between devices with their start and end apart: 4, of which 4 were waited for; matrix products, arithmetic and copies ran while one was open for 7% of the time, Pallas kernels for 0%

profile of v4, /device:TPU:6, one launch (start us, length us, event | category | flops | bytes accessed | tf_op | source)
XLA Modules:
  0.0 160.5 jit_solution(11284917935885114850)
XLA Ops:
  7.2 0.0 all-gather.2.cloned.1.call-start
  7.2 1.4 pad_maximum_fusion.3
  8.6 0.0 all-gather.2.cloned.1.call-update
  8.6 5.4 %collective-permute-start = (bf16[16,8192]{1,0:T(8,128)(2,1)}, bf16[16,8192]{1,0:T(8,128)(2,1)S(1)}, u32[]{:S(2)}, u32[]{:S(2)}) collective-permute-start(bf16[16,8192]{1,0:T(8,128)(2,1)} %bitcast.321), channel_id=1, source_target_pairs={{0,896},{128,0},{256,128},{384,256},{512,384},{640,512},{768,640},... | collective-permute-start | bytes 786440 | tf_op jit(solution)/shard_map/ppermute | solution.py:13
  14.1 0.7 select_reduce_fusion.1
  14.8 0.8 select_reduce_fusion
  15.6 1.0 convert_bitcast_fusion
  16.6 1.0 copy.119
  17.6 0.1 copy.121
  17.7 2.2 %collective-permute-done = bf16[16,8192]{1,0:T(8,128)(2,1)S(1)} collective-permute-done((bf16[16,8192]{1,0:T(8,128)(2,1)}, bf16[16,8192]{1,0:T(8,128)(2,1)S(1)}, u32[]{:S(2)}, u32[]{:S(2)}) %collective-permute-start) | collective-permute-done | bytes 262176 | tf_op jit(solution)/shard_map/ppermute | solution.py:13
  19.9 0.7 copy.164
  20.6 13.7 %all-to-all-start = ((bf16[16,8,1024]{2,0,1:T(8,128)(2,1)}), bf16[16,8,1024]{2,0,1:T(8,128)(2,1)S(1)}, u32[]{:S(2)}, u32[]{:S(2)}) async-start(bf16[16,8,1024]{2,0,1:T(8,128)(2,1)} %bitcast.290), calls=%async_computation | async-start | bytes 524288 | tf_op jit(solution)/shard_map/all_to_all | solution.py:28
  34.3 0.3 broadcast_compare_fusion.2
  34.6 5.1 %all-to-all-done = bf16[16,8,1024]{2,0,1:T(8,128)(2,1)S(1)} async-done(((bf16[16,8,1024]{2,0,1:T(8,128)(2,1)}), bf16[16,8,1024]{2,0,1:T(8,128)(2,1)S(1)}, u32[]{:S(2)}, u32[]{:S(2)}) %all-to-all-start) | async-done | bytes 262176 | tf_op jit(solution)/shard_map/all_to_all | solution.py:28
  39.8 0.1 copy.122
  39.9 0.2 multiply_reduce_fusion
  40.2 52.6 %all-gather.2.cloned.1.call-done = bf16[2048,256]{1,0:T(8,128)(2,1)} async-done(((bf16[128,256]{1,0:T(8,128)(2,1)}), bf16[2048,256]{1,0:T(8,128)(2,1)}) %all-gather.2.cloned.1.call-update) | async-done | bytes 1048592 | tf_op jit(solution)/shard_map/all_gather | solution.py:46
  92.8 0.0 copy-start
  92.8 1.4 fusion.20
  94.2 0.0 copy-done
  94.2 0.5 fusion.14
  94.7 0.5 fusion.8
  95.2 0.5 fusion.26
  95.7 1.7 %fusion.23 = (f32[8,128]{1,0:T(8,128)S(1)}, f32[8,128]{1,0:T(8,128)S(1)}, f32[8,128]{1,0:T(8,128)S(1)}, f32[8,128]{1,0:T(8,128)S(1)}) fusion(f32[512,128,8]{1,0,2:T(8,128)S(1)} %get-tuple-element.34, f32[8,128]{1,0:T(8,128)S(1)} %maximum_maximum_fusion, pred[128,512]{0,1:T(8,128)(4,1)S(1)} %get-tuple-element.23, f32[512,128,8]{1,0,2:T(8,128)S(1)} %get-tuple-element.30, ...), kind=kLoop, calls=%fused_computation.36 | loop fusion | flops 8384512 | bytes 8671232 | tf_op jit(solution)/shard_map/reduce_sum | solution.py:71
  97.4 0.5 fusion.46
  97.9 0.5 fusion.47
  98.4 0.5 fusion.48
  98.9 0.5 fusion.49
  99.4 0.7 fusion.36
  100.2 0.0 copy-start.1
  100.2 0.4 fusion.42
  100.6 0.7 fusion.37
  101.4 0.0 copy-done.1
  101.4 0.4 fusion.43
  101.8 0.7 fusion.38
  102.6 0.4 fusion.44
  103.0 0.7 fusion.39
  103.8 0.0 copy-start.2
  103.8 0.4 fusion.45
  104.2 0.5 copy-done.2
  104.9 1.2 pad_maximum_fusion
  106.0 7.9 %all-to-all-start.1 = ((bf16[16,128,256]{2,1,0:T(8,128)(2,1)}), bf16[16,128,256]{2,1,0:T(8,128)(2,1)S(1)}, u32[]{:S(2)}, u32[]{:S(2)}) async-start(bf16[16,128,256]{2,1,0:T(8,128)(2,1)} %pad_maximum_fusion), calls=%async_computation.1 | async-start | bytes 2097152 | tf_op jit(solution)/shard_map/all_to_all | solution.py:92
  113.9 1.6 %fusion.75 = f32[128,8,128]{2,0,1:T(8,128)S(1)} fusion(bf16[8,128,512]{1,2,0:T(8,128)(2,1)} %copy-done.1, bf16[2048,256]{1,0:T(8,128)(2,1)} %all-gather.2.cloned.1.call-done), kind=kOutput, calls=%fused_computation.120 | convolution fusion | flops 134217728 | bytes 1703936 | tf_op jit(solution)/shard_map/geij,jgd->iged/dot_general | solution.py:86
  115.5 0.0 copy-start.3
  115.6 1.3 convolution_add_fusion.2
  116.9 1.2 convolution_add_fusion.1
  118.1 0.0 copy-done.3
  118.1 1.2 fusion.41
  119.4 0.9 copy.105
  120.2 32.1 %all-to-all-done.1 = bf16[16,128,256]{2,1,0:T(8,128)(2,1)S(1)} async-done(((bf16[16,128,256]{2,1,0:T(8,128)(2,1)}), bf16[16,128,256]{2,1,0:T(8,128)(2,1)S(1)}, u32[]{:S(2)}, u32[]{:S(2)}) %all-to-all-start.1) | async-done | bytes 1048608 | tf_op jit(solution)/shard_map/all_to_all | solution.py:92
  152.3 0.1 convert_reduce_fusion
  152.4 0.6 fusion.97
  153.1 0.6 fusion.96
  (12 shorter events, 0.3 us)
Async XLA Ops:
  7.2 85.6 %all-gather.2.cloned.1.call-start = ((), (), s32[]{:S(2)}) async-start(), calls=%async_computation.2 | async-start | bytes 1114112 | tf_op jit(solution)/shard_map/all_gather | solution.py:46
  8.6 11.2 %collective-permute-start = (bf16[16,8192]{1,0:T(8,128)(2,1)}, bf16[16,8192]{1,0:T(8,128)(2,1)S(1)}, u32[]{:S(2)}, u32[]{:S(2)}) collective-permute-start(bf16[16,8192]{1,0:T(8,128)(2,1)} %bitcast.321), channel_id=1, source_target_pairs={{0,896},{128,0},{256,128},{384,256},{512,384},{640,512},{768,640},... | collective-permute-start | bytes 786440 | tf_op jit(solution)/shard_map/ppermute | solution.py:13
  20.6 19.1 %all-to-all-start = ((bf16[16,8,1024]{2,0,1:T(8,128)(2,1)}), bf16[16,8,1024]{2,0,1:T(8,128)(2,1)S(1)}, u32[]{:S(2)}, u32[]{:S(2)}) async-start(bf16[16,8,1024]{2,0,1:T(8,128)(2,1)} %bitcast.290), calls=%async_computation | async-start | bytes 524288 | tf_op jit(solution)/shard_map/all_to_all | solution.py:28
  92.8 1.4 copy-start
  100.2 1.2 copy-start.1
  103.8 1.0 copy-start.2
  106.0 46.3 %all-to-all-start.1 = ((bf16[16,128,256]{2,1,0:T(8,128)(2,1)}), bf16[16,128,256]{2,1,0:T(8,128)(2,1)S(1)}, u32[]{:S(2)}, u32[]{:S(2)}) async-start(bf16[16,128,256]{2,1,0:T(8,128)(2,1)} %pad_maximum_fusion), calls=%async_computation.1 | async-start | bytes 2097152 | tf_op jit(solution)/shard_map/all_to_all | solution.py:92
  115.5 2.6 %copy-start.3 = (bf16[8,128,512]{1,2,0:T(8,128)(2,1)S(1)}, bf16[8,128,512]{1,2,0:T(8,128)(2,1)}, u32[]{:S(2)}) copy-start(bf16[8,128,512]{1,2,0:T(8,128)(2,1)} %copy-done.2) | copy-start | bytes 3145732
Sparse Core Ops, SparseCore 0:
  10.6 82.1 all-gather.1

commit v5 on v4

--- a/solution.py
+++ b/solution.py
@@ -2,6 +2,7 @@
 import jax.numpy as jnp
 from jax import lax
 from jax.sharding import PartitionSpec as P
+
 
 HEAD_DIM = 128
 CHUNKS = 4
@@ -13,7 +14,7 @@
     return lax.ppermute(value, axis, pairs)
 
 
-def body(query, keys, values, attn_out, grad_out, block_of):
+def section(query, keys, values, attn_out, grad_out, block_of):
     rows = query.shape[1]
     kv_width = keys.shape[2]
     head_dim = HEAD_DIM
@@ -25,7 +26,15 @@
     order = block_of[0]
     me = lax.axis_index("ctx")
     handed = passed_along(grad_out[0], "segment", -1)
-    incoming = lax.all_to_all(handed, "tp", split_axis=1, concat_axis=0, tiled=True)
+    ways = lax.axis_size("tp")
+    mine = lax.axis_index("tp")
+    width_tp = handed.shape[1] // ways
+    pieces = [lax.dynamic_slice_in_dim(handed, mine * width_tp, width_tp, axis=1)]
+    for shift in range(1, ways):
+        out = lax.dynamic_slice_in_dim(handed, ((mine + shift) % ways) * width_tp, width_tp, axis=1)
+        pieces.append(passed_along(out, "tp", shift))
+    stacked = jnp.stack(pieces[::-1], axis=0)
+    incoming = jnp.roll(stacked, mine + 1, axis=0).reshape(ways * handed.shape[0], width_tp)
     q_local = query[0].reshape(rows, groups, per, head_dim)
     do_local = incoming.reshape(rows, groups, per, head_dim)
     delta = jnp.sum(
@@ -43,7 +52,10 @@
     q_pos = place(me * rows, rows)
 
     kv = jnp.concatenate([keys[0], values[0]], axis=1)
-    kv_all = lax.all_gather(kv, "ctx", axis=0, tiled=True)
+    count = lax.axis_size("ctx")
+    kv_all = lax.all_to_all(
+        jnp.broadcast_to(kv[None], (count,) + kv.shape), "ctx", 0, 0, tiled=True
+    ).reshape(count * rows, 2 * kv_width)
     seq = kv_all.shape[0]
     k_all = kv_all[:, :kv_width].reshape(seq, groups, head_dim)
     v_all = kv_all[:, kv_width:].reshape(seq, groups, head_dim)
@@ -103,7 +115,7 @@
 
 def solution(mesh):
     return jax.shard_map(
-        body,
+        section,
         mesh=mesh,
         in_specs=(
             P("segment", "ctx", "tp"),

time: 161 us -> 170 us (1.056)
  starting transfers between devices: 27 us -> 47.8 us
  waiting for transfers between devices: 91.9 us -> 78.7 us
  between operations: 14.4 us -> 1.4 us
  local copies, waits for them, and re-layouts: 4.01 us -> 12.1 us
  matrix products: 15 us -> 20.3 us
    all_gather x1 -> x0, waiting for transfers between devices: 52.6 us -> none  [body(): kv_all = lax.all_gather(kv, 'ctx', axis=0, tiled=True)]
    all_to_all x2, waiting for transfers between devices: 37.1 us -> 69.1 us  [the longest x1 46 us: section(): lax.all_to_all(dkv.astype(jnp.bfloat16).reshape(count, rows, 2 * kv_width...]
    ppermute x1 -> x8, starting transfers between devices: 5.38 us -> 20.7 us  [passed_along(): return lax.ppermute(value, axis, pairs)]
    another operation x0 -> x4, local copies, waits for them, and re-layouts: none -> 8.26 us
    ppermute x1 -> x8, waiting for transfers between devices: 2.16 us -> 9.6 us  [passed_along(): return lax.ppermute(value, axis, pairs)]
    dot_general x16, matrix products: 12.1 us -> 18.5 us  [the longest x4 7.67 us: section(): jnp.einsum('iged,jgd->geij', do_local, v_c, preferred_element_type=jnp.fl...]
    all_to_all x2, starting transfers between devices: 21.6 us -> 27.1 us  [the longest x1 19 us: section(): lax.all_to_all(jnp.broadcast_to(kv[None], (count,) + kv.shape), 'ctx', 0,...]
    another operation x0 -> x1, other arithmetic: none -> 3.1 us
  transfers between devices with their start and end apart: 4 -> 10, of which waited for: 4 -> 4; matrix products, arithmetic and copies ran while one was open for 7% -> 4% of each run, Pallas kernels for 0% -> 0%
where the time goes in v5:
time: 170 us; the launch traced here: 169 us
  waiting for transfers between devices  78.7 us (46%)
  starting transfers between devices  47.8 us (28%)
  matrix products  20.3 us (12%)
  local copies, waits for them, and re-layouts  12.1 us (7%)
  other arithmetic  8.47 us (5%)
    all_to_all x1, waiting for transfers between devices, section(): lax.all_to_all(dkv.astype(jnp.bfloat16).reshape(count, rows, 2 * kv_width...  46 us
    all_to_all x1, waiting for transfers between devices, section(): lax.all_to_all(jnp.broadcast_to(kv[None], (count,) + kv.shape), 'ctx', 0,...  23.1 us
    ppermute x8, starting transfers between devices, passed_along(): return lax.ppermute(value, axis, pairs)  20.7 us
    all_to_all x1, starting transfers between devices, section(): lax.all_to_all(jnp.broadcast_to(kv[None], (count,) + kv.shape), 'ctx', 0,...  19 us
    ppermute x8, waiting for transfers between devices, passed_along(): return lax.ppermute(value, axis, pairs)  9.6 us
    another operation x4, local copies, waits for them, and re-layouts  8.26 us
    all_to_all x1, starting transfers between devices, section(): lax.all_to_all(dkv.astype(jnp.bfloat16).reshape(count, rows, 2 * kv_width...  8.11 us
    dot_general x4, matrix products, section(): jnp.einsum('iged,jgd->geij', do_local, v_c, preferred_element_type=jnp.fl...  7.67 us
  transfers between devices with their start and end apart: 10, of which 4 were waited for; matrix products, arithmetic and copies ran while one was open for 4% of the time, Pallas kernels for 0%

profile of v5, /device:TPU:6, one launch (start us, length us, event | category | flops | bytes accessed | tf_op | source)
XLA Modules:
  0.0 168.8 jit_solution(758204514891374918)
XLA Ops:
  0.7 5.5 %collective-permute-start = (bf16[16,8192]{1,0:T(8,128)(2,1)}, bf16[16,8192]{1,0:T(8,128)(2,1)S(1)}, u32[]{:S(2)}, u32[]{:S(2)}) collective-permute-start(bf16[16,8192]{1,0:T(8,128)(2,1)} %bitcast.384), channel_id=1, source_target_pairs={{0,896},{128,0},{256,128},{384,256},{512,384},{640,512},{768,640},... | collective-permute-start | bytes 786440 | tf_op jit(solution)/shard_map/ppermute | solution.py:14
  6.2 0.8 pad_maximum_fusion.3
  7.0 1.1 broadcast_in_dim.117
  8.0 19.0 %all-to-all-start = ((bf16[16,128,256]{2,1,0:T(8,128)(2,1)}), bf16[16,128,256]{2,1,0:T(8,128)(2,1)S(1)}, u32[]{:S(2)}, u32[]{:S(2)}) async-start(bf16[16,128,256]{2,1,0:T(8,128)(2,1)} %broadcast_in_dim.117), calls=%async_computation | async-start | bytes 2097152 | tf_op jit(solution)/shard_map/all_to_all | solution.py:56
  27.1 0.0 copy-done.10
  27.1 0.1 select_reduce_fusion.1
  27.2 0.1 select_reduce_fusion
  27.5 0.0 collective-permute-done
  27.6 0.0 collective-permute-start.1
  27.6 0.3 broadcast_compare_fusion.2
  28.0 0.1 copy.134
  28.1 0.5 collective-permute-start.7
  28.6 3.5 %collective-permute-start.6 = (bf16[16,1024]{1,0:T(8,128)(2,1)S(1)}, bf16[16,1024]{1,0:T(8,128)(2,1)S(1)}, u32[]{:S(2)}, u32[]{:S(2)}) collective-permute-start(bf16[16,1024]{1,0:T(8,128)(2,1)S(1)} %get-tuple-element.20), channel_id=1, source_target_pairs={{0,2},{1,3},{2,4},{3,5},{4,6},{5,7},{6,0},{7,1},{8,10},{9,11},{10,... | collective-permute-start | bytes 98312 | tf_op jit(solution)/shard_map/ppermute | solution.py:14
  32.2 2.7 %collective-permute-start.5 = (bf16[16,1024]{1,0:T(8,128)(2,1)S(1)}, bf16[16,1024]{1,0:T(8,128)(2,1)S(1)}, u32[]{:S(2)}, u32[]{:S(2)}) collective-permute-start(bf16[16,1024]{1,0:T(8,128)(2,1)S(1)} %get-tuple-element.21), channel_id=1, source_target_pairs={{0,3},{1,4},{2,5},{3,6},{4,7},{5,0},{6,1},{7,2},{8,11},{9,12},{10,... | collective-permute-start | bytes 98312 | tf_op jit(solution)/shard_map/ppermute | solution.py:14
  34.8 4.6 %collective-permute-start.4 = (bf16[16,1024]{1,0:T(8,128)(2,1)S(1)}, bf16[16,1024]{1,0:T(8,128)(2,1)S(1)}, u32[]{:S(2)}, u32[]{:S(2)}) collective-permute-start(bf16[16,1024]{1,0:T(8,128)(2,1)S(1)} %get-tuple-element.22), channel_id=1, source_target_pairs={{0,4},{1,5},{2,6},{3,7},{4,0},{5,1},{6,2},{7,3},{8,12},{9,13},{10,... | collective-permute-start | bytes 98312 | tf_op jit(solution)/shard_map/ppermute | solution.py:14
  39.5 0.0 collective-permute-done.1
  39.5 1.9 %collective-permute-start.2 = (bf16[16,1024]{1,0:T(8,128)(2,1)S(1)}, bf16[16,1024]{1,0:T(8,128)(2,1)S(1)}, u32[]{:S(2)}, u32[]{:S(2)}) collective-permute-start(bf16[16,1024]{1,0:T(8,128)(2,1)S(1)} %get-tuple-element.24), channel_id=1, source_target_pairs={{0,6},{1,7},{2,0},{3,1},{4,2},{5,3},{6,4},{7,5},{8,14},{9,15},{10,... | collective-permute-start | bytes 98312 | tf_op jit(solution)/shard_map/ppermute | solution.py:14
  41.4 5.1 %collective-permute-done.2 = bf16[16,1024]{1,0:T(8,128)(2,1)S(1)} collective-permute-done((bf16[16,1024]{1,0:T(8,128)(2,1)S(1)}, bf16[16,1024]{1,0:T(8,128)(2,1)S(1)}, u32[]{:S(2)}, u32[]{:S(2)}) %collective-permute-start.2) | collective-permute-done | bytes 32800 | tf_op jit(solution)/shard_map/ppermute | solution.py:14
  46.5 1.9 %collective-permute-start.3 = (bf16[16,1024]{1,0:T(8,128)(2,1)S(1)}, bf16[16,1024]{1,0:T(8,128)(2,1)S(1)}, u32[]{:S(2)}, u32[]{:S(2)}) collective-permute-start(bf16[16,1024]{1,0:T(8,128)(2,1)S(1)} %get-tuple-element.23), channel_id=1, source_target_pairs={{0,5},{1,6},{2,7},{3,0},{4,1},{5,2},{6,3},{7,4},{8,13},{9,14},{10,... | collective-permute-start | bytes 98312 | tf_op jit(solution)/shard_map/ppermute | solution.py:14
  48.5 4.5 %collective-permute-done.3 = bf16[16,1024]{1,0:T(8,128)(2,1)S(1)} collective-permute-done((bf16[16,1024]{1,0:T(8,128)(2,1)S(1)}, bf16[16,1024]{1,0:T(8,128)(2,1)S(1)}, u32[]{:S(2)}, u32[]{:S(2)}) %collective-permute-start.3) | collective-permute-done | bytes 32800 | tf_op jit(solution)/shard_map/ppermute | solution.py:14
  53.0 0.0 collective-permute-done.4
  53.0 0.0 collective-permute-done.5
  53.0 0.0 collective-permute-done.6
  53.0 0.0 collective-permute-done.7
  53.3 0.2 multiply_reduce_fusion
  53.6 23.1 %all-to-all-done = bf16[16,128,256]{2,1,0:T(8,128)(2,1)S(1)} async-done(((bf16[16,128,256]{2,1,0:T(8,128)(2,1)}), bf16[16,128,256]{2,1,0:T(8,128)(2,1)S(1)}, u32[]{:S(2)}, u32[]{:S(2)}) %all-to-all-start) | async-done | bytes 1048608 | tf_op jit(solution)/shard_map/all_to_all | solution.py:56
  76.7 0.5 fusion.26
  77.2 0.5 fusion.8
  77.6 0.5 fusion.14
  78.1 0.5 fusion.20
  78.6 1.7 %fusion.23 = (f32[8,128]{1,0:T(8,128)S(1)}, f32[8,128]{1,0:T(8,128)S(1)}, f32[8,128]{1,0:T(8,128)S(1)}, f32[8,128]{1,0:T(8,128)S(1)}) fusion(f32[512,128,8]{1,0,2:T(8,128)S(1)} %get-tuple-element.45, f32[8,128]{1,0:T(8,128)S(1)} %maximum_maximum_fusion, pred[128,512]{0,1:T(8,128)(4,1)S(1)} %get-tuple-element.34, f32[512,128,8]{1,0,2:T(8,128)S(1)} %get-tuple-element.41, ...), kind=kLoop, calls=%fused_computation.36 | loop fusion | flops 8384512 | bytes 8671232 | tf_op jit(solution)/shard_map/reduce_sum | solution.py:83
  80.3 0.7 fusion.37
  81.1 1.7 %fusion.38 = bf16[8,128,512]{1,2,0:T(8,128)(2,1)} fusion(f32[512,128,8]{1,0,2:T(8,128)S(1)} %get-tuple-element.41, f32[8,128]{1,0:T(8,128)S(1)} %copy.97, f32[8,128]{1,0:T(8,128)S(1)} %log_add_fusion, pred[128,512]{0,1:T(8,128)(4,1)S(1)} %get-tuple-element.35, bf16[128,8,128]{2,1,0:T(8,128)(2,1)S(1)} %bitcast.352, bf16[2048,256]{1,0:T(8,128)(2,1)S(1)} %bitcast.364), kind=kOutput, calls=%fused_computation.55 | convolution fusion | flops 137363456 | bytes 3612672 | tf_op jit(solution)/shard_map/iged,jgd->geij/dot_general | solution.py:96
  82.8 3.1 %fusion.57 = (bf16[8,128,512]{1,2,0:T(8,128)(2,1)}, bf16[8,128,512]{1,2,0:T(8,128)(2,1)}, bf16[8,128,512]{1,2,0:T(8,128)(2,1)S(1)}, bf16[8,128,512]{1,2,0:T(8,128)(2,1)S(1)}) fusion(f32[512,128,8]{1,0,2:T(8,128)S(1)} %get-tuple-element.43, f32[8,128]{1,0:T(8,128)S(1)} %log_add_fusion, pred[128,512]{0,1:T(8,128)(4,1)S(1)} %get-tuple-element.37, ...), kind=kLoop, calls=%fused_computation.85 | loop fusion | flops 8388608 | bytes 12849152 | tf_op jit(solution)/shard_map/reshape.79
  85.9 2.6 %fusion.39 = bf16[8,128,512]{1,2,0:T(8,128)(2,1)} fusion(f32[512,128,8]{1,0,2:T(8,128)S(1)} %get-tuple-element.39, f32[8,128]{1,0:T(8,128)S(1)} %copy.97, f32[8,128]{1,0:T(8,128)S(1)} %log_add_fusion, pred[128,512]{0,1:T(8,128)(4,1)S(1)} %get-tuple-element.36, bf16[128,8,128]{2,1,0:T(8,128)(2,1)S(1)} %bitcast.353, bf16[2048,256]{1,0:T(8,128)(2,1)} %bitcast.365), kind=kOutput, calls=%fused_computation.56 | convolution fusion | flops 137363456 | bytes 3612672 | tf_op jit(solution)/shard_map/iged,jgd->geij/dot_general | solution.py:96
  88.5 2.6 %fusion.36 = bf16[8,128,512]{1,2,0:T(8,128)(2,1)} fusion(f32[512,128,8]{1,0,2:T(8,128)S(1)} %get-tuple-element.43, f32[8,128]{1,0:T(8,128)S(1)} %copy.97, f32[8,128]{1,0:T(8,128)S(1)} %log_add_fusion, pred[128,512]{0,1:T(8,128)(4,1)S(1)} %get-tuple-element.37, bf16[128,8,128]{2,1,0:T(8,128)(2,1)S(1)} %bitcast.354, bf16[2048,256]{1,0:T(8,128)(2,1)} %bitcast.366), kind=kOutput, calls=%fused_computation.53 | convolution fusion | flops 137363456 | bytes 3612672 | tf_op jit(solution)/shard_map/iged,jgd->geij/dot_general | solution.py:96
  91.1 0.4 fusion.43
  91.6 2.9 %copy.113 = bf16[8,128,512]{2,0,1:T(8,128)(2,1)} copy(bf16[8,128,512]{1,2,0:T(8,128)(2,1)} %get-tuple-element.30) | data formatting | bytes 2097152 | tf_op jit(solution)/shard_map/reshape.79
  94.5 1.7 %fusion.53 = bf16[512,128]{0,1:T(8,128)(2,1)S(1)} fusion(bf16[128,8,128]{2,1,0:T(8,128)(2,1)S(1)} %bitcast.355, bf16[8,128,512]{2,0,1:T(8,128)(2,1)} %copy.113), kind=kOutput, calls=%fused_computation.81 | convolution fusion | flops 134283264 | bytes 1441792 | tf_op jit(solution)/shard_map/geij,iged->jgd/dot_general | solution.py:95
  96.2 1.7 fusion.42
  97.9 0.0 copy-done.6
  97.9 0.4 fusion.45
  98.3 0.0 copy-done.2
  98.3 0.4 fusion.44
  98.8 2.7 %copy.114 = bf16[8,128,512]{2,0,1:T(8,128)(2,1)} copy(bf16[8,128,512]{1,2,0:T(8,128)(2,1)} %get-tuple-element.31) | data formatting | bytes 2097152 | tf_op jit(solution)/shard_map/reshape.82
  101.5 1.6 fusion.52
  103.0 1.8 %copy.115 = bf16[8,128,512]{2,0,1:T(8,128)(2,1)} copy(bf16[8,128,512]{1,2,0:T(8,128)(2,1)S(1)} %get-tuple-element.32) | data formatting | bytes 2097152 | tf_op jit(solution)/shard_map/reshape.85
  104.8 1.6 fusion.51
  106.4 0.9 copy.116
  107.3 0.3 fusion.50
  107.7 0.3 copy.131
  108.0 1.2 pad_maximum_fusion
  109.2 8.1 %all-to-all-start.1 = ((bf16[16,128,256]{2,1,0:T(8,128)(2,1)}), bf16[16,128,256]{2,1,0:T(8,128)(2,1)S(1)}, u32[]{:S(2)}, u32[]{:S(2)}) async-start(bf16[16,128,256]{2,1,0:T(8,128)(2,1)} %pad_maximum_fusion), calls=%async_computation.1 | async-start | bytes 2097152 | tf_op jit(solution)/shard_map/all_to_all | solution.py:104
  117.3 0.0 copy-done.1
  117.3 1.6 fusion.63
  119.0 0.3 convolution_add_fusion.2
  119.3 0.3 convolution_add_fusion.1
  119.7 0.5 copy-done.7
  120.2 0.3 fusion.41
  120.6 0.9 copy.118
  121.4 46.0 %all-to-all-done.1 = bf16[16,128,256]{2,1,0:T(8,128)(2,1)S(1)} async-done(((bf16[16,128,256]{2,1,0:T(8,128)(2,1)}), bf16[16,128,256]{2,1,0:T(8,128)(2,1)S(1)}, u32[]{:S(2)}, u32[]{:S(2)}) %all-to-all-start.1) | async-done | bytes 1048608 | tf_op jit(solution)/shard_map/all_to_all | solution.py:104
  167.4 0.1 convert_reduce_fusion
  167.5 0.6 fusion.77
  168.1 0.6 fusion.76
  (49 shorter events, 0.6 us)
Async XLA Ops:
  0.6 26.5 %copy-start.10 = (s32[1,32]{1,0:T(1,128)S(1)}, s32[1,32]{1,0:T(1,128)}, u32[]{:S(2)}) copy-start(s32[1,32]{1,0:T(1,128)} %param.11) | copy-start | bytes 388
  0.6 26.8 %copy-start.8 = (bf16[1,128,1024]{2,1,0:T(8,128)(2,1)S(1)}, bf16[1,128,1024]{2,1,0:T(8,128)(2,1)}, u32[]{:S(2)}) copy-start(bf16[1,128,1024]{2,1,0:T(8,128)(2,1)} %param.9) | copy-start | bytes 786436
  0.7 26.9 %collective-permute-start = (bf16[16,8192]{1,0:T(8,128)(2,1)}, bf16[16,8192]{1,0:T(8,128)(2,1)S(1)}, u32[]{:S(2)}, u32[]{:S(2)}) collective-permute-start(bf16[16,8192]{1,0:T(8,128)(2,1)} %bitcast.384), channel_id=1, source_target_pairs={{0,896},{128,0},{256,128},{384,256},{512,384},{640,512},{768,640},... | collective-permute-start | bytes 786440 | tf_op jit(solution)/shard_map/ppermute | solution.py:14
  8.0 19.9 %copy-start.9 = (bf16[1,128,1024]{2,1,0:T(8,128)(2,1)S(1)}, bf16[1,128,1024]{2,1,0:T(8,128)(2,1)}, u32[]{:S(2)}) copy-start(bf16[1,128,1024]{2,1,0:T(8,128)(2,1)} %param.6) | copy-start | bytes 786436
  8.0 68.7 %all-to-all-start = ((bf16[16,128,256]{2,1,0:T(8,128)(2,1)}), bf16[16,128,256]{2,1,0:T(8,128)(2,1)S(1)}, u32[]{:S(2)}, u32[]{:S(2)}) async-start(bf16[16,128,256]{2,1,0:T(8,128)(2,1)} %broadcast_in_dim.117), calls=%async_computation | async-start | bytes 2097152 | tf_op jit(solution)/shard_map/all_to_all | solution.py:56
  27.6 11.9 %collective-permute-start.1 = (bf16[16,1024]{1,0:T(8,128)(2,1)S(1)}, bf16[16,1024]{1,0:T(8,128)(2,1)S(1)}, u32[]{:S(2)}, u32[]{:S(2)}) collective-permute-start(bf16[16,1024]{1,0:T(8,128)(2,1)S(1)} %get-tuple-element.25), channel_id=1, source_target_pairs={{0,7},{1,0},{2,1},{3,2},{4,3},{5,4},{6,5},{7,6},{8,15},{9,8},{10,9... | collective-permute-start | bytes 98312 | tf_op jit(solution)/shard_map/ppermute | solution.py:14
  28.1 24.9 %collective-permute-start.7 = (bf16[16,1024]{1,0:T(8,128)(2,1)S(1)}, bf16[16,1024]{1,0:T(8,128)(2,1)S(1)}, u32[]{:S(2)}, u32[]{:S(2)}) collective-permute-start(bf16[16,1024]{1,0:T(8,128)(2,1)S(1)} %get-tuple-element.19), channel_id=1, source_target_pairs={{0,1},{1,2},{2,3},{3,4},{4,5},{5,6},{6,7},{7,0},{8,9},{9,10},{10,1... | collective-permute-start | bytes 98312 | tf_op jit(solution)/shard_map/ppermute | solution.py:14
  28.6 24.4 %collective-permute-start.6 = (bf16[16,1024]{1,0:T(8,128)(2,1)S(1)}, bf16[16,1024]{1,0:T(8,128)(2,1)S(1)}, u32[]{:S(2)}, u32[]{:S(2)}) collective-permute-start(bf16[16,1024]{1,0:T(8,128)(2,1)S(1)} %get-tuple-element.20), channel_id=1, source_target_pairs={{0,2},{1,3},{2,4},{3,5},{4,6},{5,7},{6,0},{7,1},{8,10},{9,11},{10,... | collective-permute-start | bytes 98312 | tf_op jit(solution)/shard_map/ppermute | solution.py:14
  32.2 20.8 %collective-permute-start.5 = (bf16[16,1024]{1,0:T(8,128)(2,1)S(1)}, bf16[16,1024]{1,0:T(8,128)(2,1)S(1)}, u32[]{:S(2)}, u32[]{:S(2)}) collective-permute-start(bf16[16,1024]{1,0:T(8,128)(2,1)S(1)} %get-tuple-element.21), channel_id=1, source_target_pairs={{0,3},{1,4},{2,5},{3,6},{4,7},{5,0},{6,1},{7,2},{8,11},{9,12},{10,... | collective-permute-start | bytes 98312 | tf_op jit(solution)/shard_map/ppermute | solution.py:14
  34.8 18.1 %collective-permute-start.4 = (bf16[16,1024]{1,0:T(8,128)(2,1)S(1)}, bf16[16,1024]{1,0:T(8,128)(2,1)S(1)}, u32[]{:S(2)}, u32[]{:S(2)}) collective-permute-start(bf16[16,1024]{1,0:T(8,128)(2,1)S(1)} %get-tuple-element.22), channel_id=1, source_target_pairs={{0,4},{1,5},{2,6},{3,7},{4,0},{5,1},{6,2},{7,3},{8,12},{9,13},{10,... | collective-permute-start | bytes 98312 | tf_op jit(solution)/shard_map/ppermute | solution.py:14
  39.5 7.0 %collective-permute-start.2 = (bf16[16,1024]{1,0:T(8,128)(2,1)S(1)}, bf16[16,1024]{1,0:T(8,128)(2,1)S(1)}, u32[]{:S(2)}, u32[]{:S(2)}) collective-permute-start(bf16[16,1024]{1,0:T(8,128)(2,1)S(1)} %get-tuple-element.24), channel_id=1, source_target_pairs={{0,6},{1,7},{2,0},{3,1},{4,2},{5,3},{6,4},{7,5},{8,14},{9,15},{10,... | collective-permute-start | bytes 98312 | tf_op jit(solution)/shard_map/ppermute | solution.py:14
  46.5 6.4 %collective-permute-start.3 = (bf16[16,1024]{1,0:T(8,128)(2,1)S(1)}, bf16[16,1024]{1,0:T(8,128)(2,1)S(1)}, u32[]{:S(2)}, u32[]{:S(2)}) collective-permute-start(bf16[16,1024]{1,0:T(8,128)(2,1)S(1)} %get-tuple-element.23), channel_id=1, source_target_pairs={{0,5},{1,6},{2,7},{3,0},{4,1},{5,2},{6,3},{7,4},{8,13},{9,14},{10,... | collective-permute-start | bytes 98312 | tf_op jit(solution)/shard_map/ppermute | solution.py:14
  76.7 4.4 %copy-start = (bf16[16,128,256]{2,1,0:T(8,128)(2,1)}, bf16[16,128,256]{2,1,0:T(8,128)(2,1)S(1)}, u32[]{:S(2)}) copy-start(bf16[16,128,256]{2,1,0:T(8,128)(2,1)S(1)} %all-to-all-done) | copy-start | bytes 3145732
  81.1 10.1 %copy-start.4 = (bf16[8,128,512]{1,2,0:T(8,128)(2,1)}, bf16[8,128,512]{1,2,0:T(8,128)(2,1)S(1)}, u32[]{:S(2)}) copy-start(bf16[8,128,512]{1,2,0:T(8,128)(2,1)S(1)} %fusion.37) | copy-start | bytes 3145732
  94.5 3.4 %copy-start.6 = (bf16[8,128,512]{1,2,0:T(8,128)(2,1)S(1)}, bf16[8,128,512]{1,2,0:T(8,128)(2,1)}, u32[]{:S(2)}) copy-start(bf16[8,128,512]{1,2,0:T(8,128)(2,1)} %fusion.39) | copy-start | bytes 3145732
  94.5 3.8 %copy-start.2 = (bf16[8,128,512]{1,2,0:T(8,128)(2,1)S(1)}, bf16[8,128,512]{1,2,0:T(8,128)(2,1)}, u32[]{:S(2)}) copy-start(bf16[8,128,512]{1,2,0:T(8,128)(2,1)} %fusion.38) | copy-start | bytes 3145732
  108.0 9.3 %copy-start.1 = (bf16[16,128,256]{2,1,0:T(8,128)(2,1)S(1)}, bf16[16,128,256]{2,1,0:T(8,128)(2,1)}, u32[]{:S(2)}) copy-start(bf16[16,128,256]{2,1,0:T(8,128)(2,1)} %copy-done) | copy-start | bytes 3145732
  109.2 9.8 %copy-start.5 = (bf16[8,128,512]{1,2,0:T(8,128)(2,1)S(1)}, bf16[8,128,512]{1,2,0:T(8,128)(2,1)}, u32[]{:S(2)}) copy-start(bf16[8,128,512]{1,2,0:T(8,128)(2,1)} %copy-done.4) | copy-start | bytes 3145732
  109.2 58.2 %all-to-all-start.1 = ((bf16[16,128,256]{2,1,0:T(8,128)(2,1)}), bf16[16,128,256]{2,1,0:T(8,128)(2,1)S(1)}, u32[]{:S(2)}, u32[]{:S(2)}) async-start(bf16[16,128,256]{2,1,0:T(8,128)(2,1)} %pad_maximum_fusion), calls=%async_computation.1 | async-start | bytes 2097152 | tf_op jit(solution)/shard_map/all_to_all | solution.py:104
  117.3 2.0 %copy-start.3 = (bf16[8,128,512]{1,2,0:T(8,128)(2,1)S(1)}, bf16[8,128,512]{1,2,0:T(8,128)(2,1)}, u32[]{:S(2)}) copy-start(bf16[8,128,512]{1,2,0:T(8,128)(2,1)} %fusion.38) | copy-start | bytes 3145732
  119.0 1.2 copy-start.7

commit v6 on v5

--- a/solution.py
+++ b/solution.py
@@ -61,13 +61,15 @@
     v_all = kv_all[:, kv_width:].reshape(seq, groups, head_dim)
     k_pos_all = place(jnp.int32(0), seq)
     width = seq // CHUNKS
+    q_g = jnp.transpose(q_local, (1, 2, 0, 3)).reshape(groups, per * rows, head_dim)
+    do_g = jnp.transpose(do_local, (1, 2, 0, 3)).reshape(groups, per * rows, head_dim)
+    delta_g = delta.reshape(groups, per * rows)
+    q_pos_m = jnp.tile(q_pos, per)
 
     def chunk_scores(c):
         k_c = k_all[c * width:(c + 1) * width]
-        scores = scale * jnp.einsum(
-            "iged,jgd->geij", q_local, k_c, preferred_element_type=jnp.float32
-        )
-        allowed = k_pos_all[c * width:(c + 1) * width][None, :] <= q_pos[:, None]
+        scores = scale * jnp.einsum("gmd,jgd->gmj", q_g, k_c, preferred_element_type=jnp.float32)
+        allowed = k_pos_all[c * width:(c + 1) * width][None, :] <= q_pos_m[:, None]
         return scores, allowed
 
     tops = []
@@ -83,7 +85,7 @@
         total = total + jnp.sum(jnp.where(allowed, jnp.exp(scores - top[..., None]), 0.0), axis=-1)
     lse = top + jnp.log(total)
 
-    dquery = jnp.zeros((rows, groups, per, head_dim), jnp.float32)
+    dquery_g = jnp.zeros((groups, per * rows, head_dim), jnp.float32)
     dks = []
     dvs = []
     for c in range(CHUNKS):
@@ -92,13 +94,14 @@
         v_c = v_all[c * width:(c + 1) * width]
         prob = jnp.where(allowed, jnp.exp(scores - lse[..., None]), 0.0)
         prob_b = prob.astype(jnp.bfloat16)
-        dvalue = jnp.einsum("geij,iged->jgd", prob_b, do_local, preferred_element_type=jnp.float32)
-        dprob = jnp.einsum("iged,jgd->geij", do_local, v_c, preferred_element_type=jnp.float32)
-        dscore = (prob * (dprob - delta[..., None])).astype(jnp.bfloat16)
-        dquery = dquery + jnp.einsum("geij,jgd->iged", dscore, k_c, preferred_element_type=jnp.float32)
-        dkey = jnp.einsum("geij,iged->jgd", dscore, q_local, preferred_element_type=jnp.float32)
+        dvalue = jnp.einsum("gmj,gmd->jgd", prob_b, do_g, preferred_element_type=jnp.float32)
+        dprob = jnp.einsum("gmd,jgd->gmj", do_g, v_c, preferred_element_type=jnp.float32)
+        dscore = (prob * (dprob - delta_g[..., None])).astype(jnp.bfloat16)
+        dquery_g = dquery_g + jnp.einsum("gmj,jgd->gmd", dscore, k_c, preferred_element_type=jnp.float32)
+        dkey = jnp.einsum("gmj,gmd->jgd", dscore, q_g, preferred_element_type=jnp.float32)
         dks.append(dkey.reshape(width, kv_width))
         dvs.append(dvalue.reshape(width, kv_width))
+    dquery = jnp.transpose(dquery_g.reshape(groups, per, rows, head_dim), (2, 0, 1, 3))
     dkv = jnp.concatenate([jnp.concatenate(dks, axis=0), jnp.concatenate(dvs, axis=0)], axis=1)
     count = lax.axis_size("ctx")
     dkv = lax.all_to_all(

time: 170 us -> 156 us (0.918)
  local copies, waits for them, and re-layouts: 12.1 us -> 4.68 us
  waiting for transfers between devices: 78.7 us -> 75.6 us
  other arithmetic: 8.47 us -> 6.51 us
    another operation x4 -> x0, local copies, waits for them, and re-layouts: 8.26 us -> none
    another operation x1 -> x0, other arithmetic: 3.1 us -> none
    all_to_all x1, waiting for transfers between devices: 46 us -> 43.1 us  [section(): lax.all_to_all(dkv.astype(jnp.bfloat16).reshape(count, rows, 2 * kv_width...]
  transfers between devices with their start and end apart: 10 -> 10, of which waited for: 4 -> 4; matrix products, arithmetic and copies ran while one was open for 4% -> 7% of each run, Pallas kernels for 0% -> 0%
where the time goes in v6:
time: 156 us; the launch traced here: 155 us
  waiting for transfers between devices  75.6 us (48%)
  starting transfers between devices  47.8 us (31%)
  matrix products  18.9 us (12%)
  other arithmetic  6.51 us (4%)
  local copies, waits for them, and re-layouts  4.68 us (3%)
    all_to_all x1, waiting for transfers between devices, section(): lax.all_to_all(dkv.astype(jnp.bfloat16).reshape(count, rows, 2 * kv_width...  43.1 us
    all_to_all x1, waiting for transfers between devices, section(): lax.all_to_all(jnp.broadcast_to(kv[None], (count,) + kv.shape), 'ctx', 0,...  22.9 us
    ppermute x8, starting transfers between devices, passed_along(): return lax.ppermute(value, axis, pairs)  20.7 us
    all_to_all x1, starting transfers between devices, section(): lax.all_to_all(jnp.broadcast_to(kv[None], (count,) + kv.shape), 'ctx', 0,...  19 us
    ppermute x8, waiting for transfers between devices, passed_along(): return lax.ppermute(value, axis, pairs)  9.6 us
    all_to_all x1, starting transfers between devices, section(): lax.all_to_all(dkv.astype(jnp.bfloat16).reshape(count, rows, 2 * kv_width...  8.12 us
    dot_general x4, matrix products, section(): jnp.einsum('gmj,jgd->gmd', dscore, k_c, preferred_element_type=jnp.float32)  5.92 us
    dot_general x4, matrix products, section(): jnp.einsum('gmd,jgd->gmj', do_g, v_c, preferred_element_type=jnp.float32)  3.84 us
  transfers between devices with their start and end apart: 10, of which 4 were waited for; matrix products, arithmetic and copies ran while one was open for 7% of the time, Pallas kernels for 0%

profile of v6, /device:TPU:6, one launch (start us, length us, event | category | flops | bytes accessed | tf_op | source)
XLA Modules:
  0.0 154.9 jit_solution(8525347623621114097)
XLA Ops:
  0.7 5.5 %collective-permute-start = (bf16[16,8192]{1,0:T(8,128)(2,1)}, bf16[16,8192]{1,0:T(8,128)(2,1)S(1)}, u32[]{:S(2)}, u32[]{:S(2)}) collective-permute-start(bf16[16,8192]{1,0:T(8,128)(2,1)} %bitcast.223), channel_id=1, source_target_pairs={{0,896},{128,0},{256,128},{384,256},{512,384},{640,512},{768,640},... | collective-permute-start | bytes 786440 | tf_op jit(solution)/shard_map/ppermute | solution.py:14
  6.2 0.8 pad_maximum_fusion.3
  7.0 1.1 broadcast_in_dim.98
  8.0 19.0 %all-to-all-start = ((bf16[16,128,256]{2,1,0:T(8,128)(2,1)}), bf16[16,128,256]{2,1,0:T(8,128)(2,1)S(1)}, u32[]{:S(2)}, u32[]{:S(2)}) async-start(bf16[16,128,256]{2,1,0:T(8,128)(2,1)} %broadcast_in_dim.98), calls=%async_computation | async-start | bytes 2097152 | tf_op jit(solution)/shard_map/all_to_all | solution.py:56
  27.1 0.1 select_reduce_fusion.1
  27.2 0.1 select_reduce_fusion
  27.5 0.0 collective-permute-done
  27.5 0.0 collective-permute-start.1
  27.6 0.2 copy.44
  27.7 0.2 copy.45
  27.9 0.2 copy.47
  28.1 0.2 copy.48
  28.3 0.5 collective-permute-start.7
  28.8 3.5 %collective-permute-start.6 = (bf16[16,1024]{1,0:T(8,128)(2,1)S(1)}, bf16[16,1024]{1,0:T(8,128)(2,1)S(1)}, u32[]{:S(2)}, u32[]{:S(2)}) collective-permute-start(bf16[16,1024]{1,0:T(8,128)(2,1)S(1)} %get-tuple-element.12), channel_id=1, source_target_pairs={{0,2},{1,3},{2,4},{3,5},{4,6},{5,7},{6,0},{7,1},{8,10},{9,11},{10,... | collective-permute-start | bytes 98312 | tf_op jit(solution)/shard_map/ppermute | solution.py:14
  32.3 2.7 %collective-permute-start.5 = (bf16[16,1024]{1,0:T(8,128)(2,1)S(1)}, bf16[16,1024]{1,0:T(8,128)(2,1)S(1)}, u32[]{:S(2)}, u32[]{:S(2)}) collective-permute-start(bf16[16,1024]{1,0:T(8,128)(2,1)S(1)} %get-tuple-element.13), channel_id=1, source_target_pairs={{0,3},{1,4},{2,5},{3,6},{4,7},{5,0},{6,1},{7,2},{8,11},{9,12},{10,... | collective-permute-start | bytes 98312 | tf_op jit(solution)/shard_map/ppermute | solution.py:14
  35.1 4.6 %collective-permute-start.4 = (bf16[16,1024]{1,0:T(8,128)(2,1)S(1)}, bf16[16,1024]{1,0:T(8,128)(2,1)S(1)}, u32[]{:S(2)}, u32[]{:S(2)}) collective-permute-start(bf16[16,1024]{1,0:T(8,128)(2,1)S(1)} %get-tuple-element.14), channel_id=1, source_target_pairs={{0,4},{1,5},{2,6},{3,7},{4,0},{5,1},{6,2},{7,3},{8,12},{9,13},{10,... | collective-permute-start | bytes 98312 | tf_op jit(solution)/shard_map/ppermute | solution.py:14
  39.7 0.0 collective-permute-done.1
  39.7 1.9 %collective-permute-start.2 = (bf16[16,1024]{1,0:T(8,128)(2,1)S(1)}, bf16[16,1024]{1,0:T(8,128)(2,1)S(1)}, u32[]{:S(2)}, u32[]{:S(2)}) collective-permute-start(bf16[16,1024]{1,0:T(8,128)(2,1)S(1)} %get-tuple-element.16), channel_id=1, source_target_pairs={{0,6},{1,7},{2,0},{3,1},{4,2},{5,3},{6,4},{7,5},{8,14},{9,15},{10,... | collective-permute-start | bytes 98312 | tf_op jit(solution)/shard_map/ppermute | solution.py:14
  41.6 5.1 %collective-permute-done.2 = bf16[16,1024]{1,0:T(8,128)(2,1)S(1)} collective-permute-done((bf16[16,1024]{1,0:T(8,128)(2,1)S(1)}, bf16[16,1024]{1,0:T(8,128)(2,1)S(1)}, u32[]{:S(2)}, u32[]{:S(2)}) %collective-permute-start.2) | collective-permute-done | bytes 32800 | tf_op jit(solution)/shard_map/ppermute | solution.py:14
  46.7 1.9 %collective-permute-start.3 = (bf16[16,1024]{1,0:T(8,128)(2,1)S(1)}, bf16[16,1024]{1,0:T(8,128)(2,1)S(1)}, u32[]{:S(2)}, u32[]{:S(2)}) collective-permute-start(bf16[16,1024]{1,0:T(8,128)(2,1)S(1)} %get-tuple-element.15), channel_id=1, source_target_pairs={{0,5},{1,6},{2,7},{3,0},{4,1},{5,2},{6,3},{7,4},{8,13},{9,14},{10,... | collective-permute-start | bytes 98312 | tf_op jit(solution)/shard_map/ppermute | solution.py:14
  48.6 4.5 %collective-permute-done.3 = bf16[16,1024]{1,0:T(8,128)(2,1)S(1)} collective-permute-done((bf16[16,1024]{1,0:T(8,128)(2,1)S(1)}, bf16[16,1024]{1,0:T(8,128)(2,1)S(1)}, u32[]{:S(2)}, u32[]{:S(2)}) %collective-permute-start.3) | collective-permute-done | bytes 32800 | tf_op jit(solution)/shard_map/ppermute | solution.py:14
  53.2 0.0 collective-permute-done.4
  53.2 0.0 collective-permute-done.5
  53.2 0.0 collective-permute-done.6
  53.2 0.0 collective-permute-done.7
  53.4 0.2 multiply_reduce_fusion
  53.7 0.1 copy.46
  53.8 0.0 copy-start.8
  53.8 22.9 %all-to-all-done = bf16[16,128,256]{2,1,0:T(8,128)(2,1)S(1)} async-done(((bf16[16,128,256]{2,1,0:T(8,128)(2,1)}), bf16[16,128,256]{2,1,0:T(8,128)(2,1)S(1)}, u32[]{:S(2)}, u32[]{:S(2)}) %all-to-all-start) | async-done | bytes 1048608 | tf_op jit(solution)/shard_map/all_to_all | solution.py:56
  76.7 0.4 fusion.51
  77.1 0.4 fusion.54
  77.6 0.4 fusion.61
  78.0 1.6 %fusion.2 = (f32[1024]{0:T(1024)S(1)}, f32[1024]{0:T(1024)S(1)}, f32[1024]{0:T(1024)S(1)}, f32[1024]{0:T(1024)S(1)}, f32[512,1024]{1,0:T(8,128)S(1)}) fusion(s32[1024]{0:T(1024)S(1)} %broadcast_bitcast_fusion, s32[512]{0:T(512)S(1)} %get-tuple-element.21, f32[512,1024]{1,0:T(8,128)S(1)} %fusion.54, s32[512]{0:T(512)S(1)} %get-tuple-element.20, ...), kind=kOutput, calls=%fused_computation.14 | convolution fusion | flops 142602240 | bytes 8810496 | tf_op jit(solution)/shard_map/gmd,jgd->gmj/dot_general | solution.py:71
  79.6 2.4 %fusion.3 = (f32[1024]{0:T(1024)S(1)}, f32[1024]{0:T(1024)S(1)}, f32[1024]{0:T(1024)S(1)}, f32[1024]{0:T(1024)S(1)}) fusion(f32[512,1024]{1,0:T(8,128)S(1)} %get-tuple-element.22, f32[1024]{0:T(1024)S(1)} %maximum_maximum_fusion, s32[1024]{0:T(1024)S(1)} %broadcast_bitcast_fusion, s32[512]{0:T(512)S(1)} %get-tuple-element.21, f32[512,1024]{1,0:T(8,128)S(1)} %fusion.54, ...), kind=kLoop, calls=%fused_computation.15 | loop fusion | flops 10481664 | bytes 8421376 | tf_op jit(solution)/shard_map/reduce_sum | solution.py:85
  82.0 0.6 fusion.22
  82.6 0.6 fusion.23
  83.3 0.7 multiply_convert_fusion.3
  84.0 0.7 multiply_convert_fusion.2
  84.7 0.6 fusion.24
  85.4 0.0 copy-start.9
  85.4 1.7 %multiply_convert_fusion.1 = bf16[1024,512]{0,1:T(8,128)(2,1)S(1)} fusion(bf16[1024,128]{1,0:T(8,128)(2,1)} %bitcast.211, f32[512,1024]{1,0:T(8,128)S(1)} %fusion.54, f32[1024]{0:T(1024)S(1)} %bitcast.219, f32[1024]{0:T(1024)S(1)} %log_add_fusion, s32[1024]{0:T(1024)S(1)} %broadcast_bitcast_fusion, s32[512]{0:T(512)S(1)} %get-tuple-element.20, ...), kind=kOutput, calls=%fused_computation.38 | convolution fusion | flops 137887744 | bytes 3553280 | tf_op jit(solution)/shard_map/gmd,jgd->gmj/dot_general | solution.py:98
  87.1 0.0 copy-done.9
  87.1 0.6 fusion.25
  87.8 0.7 multiply_convert_fusion
  88.5 0.4 convolution_convert_fusion.7
  89.0 1.1 convolution_convert_fusion.6
  90.1 1.1 convolution_convert_fusion.5
  91.1 1.1 convolution_convert_fusion.4
  92.3 0.3 copy.60
  92.6 0.6 copy-done.4
  93.1 0.1 copy-done.5
  93.2 0.9 pad_maximum_fusion.1
  94.1 1.1 pad_maximum_fusion
  95.3 8.1 %all-to-all-start.1 = ((bf16[16,128,256]{2,1,0:T(8,128)(2,1)}), bf16[16,128,256]{2,1,0:T(8,128)(2,1)S(1)}, u32[]{:S(2)}, u32[]{:S(2)}) async-start(bf16[16,128,256]{2,1,0:T(8,128)(2,1)} %pad_maximum_fusion), calls=%async_computation.1 | async-start | bytes 2097152 | tf_op jit(solution)/shard_map/all_to_all | solution.py:107
  103.4 1.7 %fusion.59 = f32[1024,128]{1,0:T(8,128)S(1)} fusion(bf16[1024,512]{0,1:T(8,128)(2,1)} %copy-done, bf16[2048,256]{1,0:T(8,128)(2,1)} %bitcast.194), kind=kOutput, calls=%fused_computation.97 | convolution fusion | flops 134217728 | bytes 1703936 | tf_op jit(solution)/shard_map/gmj,jgd->gmd/dot_general | solution.py:100
  105.1 1.5 convolution_add_fusion.2
  106.6 1.4 convolution_add_fusion.1
  108.0 1.4 fusion.21
  109.4 0.2 copy.54
  109.5 0.8 convert_element_type.103
  110.4 43.1 %all-to-all-done.1 = bf16[16,128,256]{2,1,0:T(8,128)(2,1)S(1)} async-done(((bf16[16,128,256]{2,1,0:T(8,128)(2,1)}), bf16[16,128,256]{2,1,0:T(8,128)(2,1)S(1)}, u32[]{:S(2)}, u32[]{:S(2)}) %all-to-all-start.1) | async-done | bytes 1048608 | tf_op jit(solution)/shard_map/all_to_all | solution.py:107
  153.5 0.1 convert_reduce_fusion
  153.7 0.6 fusion.65
  154.3 0.6 fusion.64
  (46 shorter events, 0.4 us)
Async XLA Ops:
  0.6 26.5 %copy-start.10 = (s32[1,32]{1,0:T(1,128)S(1)}, s32[1,32]{1,0:T(1,128)}, u32[]{:S(2)}) copy-start(s32[1,32]{1,0:T(1,128)} %param.11) | copy-start | bytes 388
  0.6 26.9 %copy-start.6 = (bf16[1,128,1024]{2,1,0:T(8,128)(2,1)S(1)}, bf16[1,128,1024]{2,1,0:T(8,128)(2,1)}, u32[]{:S(2)}) copy-start(bf16[1,128,1024]{2,1,0:T(8,128)(2,1)} %param.6) | copy-start | bytes 786436
  0.7 26.8 %collective-permute-start = (bf16[16,8192]{1,0:T(8,128)(2,1)}, bf16[16,8192]{1,0:T(8,128)(2,1)S(1)}, u32[]{:S(2)}, u32[]{:S(2)}) collective-permute-start(bf16[16,8192]{1,0:T(8,128)(2,1)} %bitcast.223), channel_id=1, source_target_pairs={{0,896},{128,0},{256,128},{384,256},{512,384},{640,512},{768,640},... | collective-permute-start | bytes 786440 | tf_op jit(solution)/shard_map/ppermute | solution.py:14
  8.0 19.9 %copy-start.7 = (bf16[1,128,1024]{2,1,0:T(8,128)(2,1)S(1)}, bf16[1,128,1024]{2,1,0:T(8,128)(2,1)}, u32[]{:S(2)}) copy-start(bf16[1,128,1024]{2,1,0:T(8,128)(2,1)} %param.9) | copy-start | bytes 786436
  8.0 68.7 %all-to-all-start = ((bf16[16,128,256]{2,1,0:T(8,128)(2,1)}), bf16[16,128,256]{2,1,0:T(8,128)(2,1)S(1)}, u32[]{:S(2)}, u32[]{:S(2)}) async-start(bf16[16,128,256]{2,1,0:T(8,128)(2,1)} %broadcast_in_dim.98), calls=%async_computation | async-start | bytes 2097152 | tf_op jit(solution)/shard_map/all_to_all | solution.py:56
  27.5 12.2 %collective-permute-start.1 = (bf16[16,1024]{1,0:T(8,128)(2,1)S(1)}, bf16[16,1024]{1,0:T(8,128)(2,1)S(1)}, u32[]{:S(2)}, u32[]{:S(2)}) collective-permute-start(bf16[16,1024]{1,0:T(8,128)(2,1)S(1)} %get-tuple-element.17), channel_id=1, source_target_pairs={{0,7},{1,0},{2,1},{3,2},{4,3},{5,4},{6,5},{7,6},{8,15},{9,8},{10,9... | collective-permute-start | bytes 98312 | tf_op jit(solution)/shard_map/ppermute | solution.py:14
  28.3 24.9 %collective-permute-start.7 = (bf16[16,1024]{1,0:T(8,128)(2,1)S(1)}, bf16[16,1024]{1,0:T(8,128)(2,1)S(1)}, u32[]{:S(2)}, u32[]{:S(2)}) collective-permute-start(bf16[16,1024]{1,0:T(8,128)(2,1)S(1)} %get-tuple-element.11), channel_id=1, source_target_pairs={{0,1},{1,2},{2,3},{3,4},{4,5},{5,6},{6,7},{7,0},{8,9},{9,10},{10,1... | collective-permute-start | bytes 98312 | tf_op jit(solution)/shard_map/ppermute | solution.py:14
  28.8 24.4 %collective-permute-start.6 = (bf16[16,1024]{1,0:T(8,128)(2,1)S(1)}, bf16[16,1024]{1,0:T(8,128)(2,1)S(1)}, u32[]{:S(2)}, u32[]{:S(2)}) collective-permute-start(bf16[16,1024]{1,0:T(8,128)(2,1)S(1)} %get-tuple-element.12), channel_id=1, source_target_pairs={{0,2},{1,3},{2,4},{3,5},{4,6},{5,7},{6,0},{7,1},{8,10},{9,11},{10,... | collective-permute-start | bytes 98312 | tf_op jit(solution)/shard_map/ppermute | solution.py:14
  32.3 20.8 %collective-permute-start.5 = (bf16[16,1024]{1,0:T(8,128)(2,1)S(1)}, bf16[16,1024]{1,0:T(8,128)(2,1)S(1)}, u32[]{:S(2)}, u32[]{:S(2)}) collective-permute-start(bf16[16,1024]{1,0:T(8,128)(2,1)S(1)} %get-tuple-element.13), channel_id=1, source_target_pairs={{0,3},{1,4},{2,5},{3,6},{4,7},{5,0},{6,1},{7,2},{8,11},{9,12},{10,... | collective-permute-start | bytes 98312 | tf_op jit(solution)/shard_map/ppermute | solution.py:14
  35.1 18.1 %collective-permute-start.4 = (bf16[16,1024]{1,0:T(8,128)(2,1)S(1)}, bf16[16,1024]{1,0:T(8,128)(2,1)S(1)}, u32[]{:S(2)}, u32[]{:S(2)}) collective-permute-start(bf16[16,1024]{1,0:T(8,128)(2,1)S(1)} %get-tuple-element.14), channel_id=1, source_target_pairs={{0,4},{1,5},{2,6},{3,7},{4,0},{5,1},{6,2},{7,3},{8,12},{9,13},{10,... | collective-permute-start | bytes 98312 | tf_op jit(solution)/shard_map/ppermute | solution.py:14
  39.7 7.0 %collective-permute-start.2 = (bf16[16,1024]{1,0:T(8,128)(2,1)S(1)}, bf16[16,1024]{1,0:T(8,128)(2,1)S(1)}, u32[]{:S(2)}, u32[]{:S(2)}) collective-permute-start(bf16[16,1024]{1,0:T(8,128)(2,1)S(1)} %get-tuple-element.16), channel_id=1, source_target_pairs={{0,6},{1,7},{2,0},{3,1},{4,2},{5,3},{6,4},{7,5},{8,14},{9,15},{10,... | collective-permute-start | bytes 98312 | tf_op jit(solution)/shard_map/ppermute | solution.py:14
  46.7 6.4 %collective-permute-start.3 = (bf16[16,1024]{1,0:T(8,128)(2,1)S(1)}, bf16[16,1024]{1,0:T(8,128)(2,1)S(1)}, u32[]{:S(2)}, u32[]{:S(2)}) collective-permute-start(bf16[16,1024]{1,0:T(8,128)(2,1)S(1)} %get-tuple-element.15), channel_id=1, source_target_pairs={{0,5},{1,6},{2,7},{3,0},{4,1},{5,2},{6,3},{7,4},{8,13},{9,14},{10,... | collective-permute-start | bytes 98312 | tf_op jit(solution)/shard_map/ppermute | solution.py:14
  53.8 30.9 %copy-start.8 = (bf16[1,8,128,128]{3,2,1,0:T(8,128)(2,1)}, bf16[1,8,128,128]{3,2,1,0:T(8,128)(2,1)S(1)}, u32[]{:S(2)}) copy-start(bf16[1,8,128,128]{3,2,1,0:T(8,128)(2,1)S(1)} %copy.46) | copy-start | bytes 786436
  76.7 11.1 %copy-start.3 = (bf16[16,128,256]{2,1,0:T(8,128)(2,1)}, bf16[16,128,256]{2,1,0:T(8,128)(2,1)S(1)}, u32[]{:S(2)}) copy-start(bf16[16,128,256]{2,1,0:T(8,128)(2,1)S(1)} %all-to-all-done) | copy-start | bytes 3145732
  84.0 4.5 %copy-start = (bf16[1024,512]{0,1:T(8,128)(2,1)}, bf16[1024,512]{0,1:T(8,128)(2,1)S(1)}, u32[]{:S(2)}) copy-start(bf16[1024,512]{0,1:T(8,128)(2,1)S(1)} %multiply_convert_fusion.3) | copy-start | bytes 3145732
  85.4 1.7 %copy-start.9 = (bf16[1,8,128,128]{3,2,1,0:T(8,128)(2,1)S(1)}, bf16[1,8,128,128]{3,2,1,0:T(8,128)(2,1)}, u32[]{:S(2)}) copy-start(bf16[1,8,128,128]{3,2,1,0:T(8,128)(2,1)} %copy-done.8) | copy-start | bytes 786436
  88.5 2.6 %copy-start.1 = (bf16[1024,512]{0,1:T(8,128)(2,1)}, bf16[1024,512]{0,1:T(8,128)(2,1)S(1)}, u32[]{:S(2)}) copy-start(bf16[1024,512]{0,1:T(8,128)(2,1)S(1)} %multiply_convert_fusion) | copy-start | bytes 3145732
  92.2 0.9 copy-start.4
  92.2 1.0 copy-start.5
  95.3 58.2 %all-to-all-start.1 = ((bf16[16,128,256]{2,1,0:T(8,128)(2,1)}), bf16[16,128,256]{2,1,0:T(8,128)(2,1)S(1)}, u32[]{:S(2)}, u32[]{:S(2)}) async-start(bf16[16,128,256]{2,1,0:T(8,128)(2,1)} %pad_maximum_fusion), calls=%async_computation.1 | async-start | bytes 2097152 | tf_op jit(solution)/shard_map/all_to_all | solution.py:107
  105.1 2.9 %copy-start.2 = (bf16[1024,512]{0,1:T(8,128)(2,1)S(1)}, bf16[1024,512]{0,1:T(8,128)(2,1)}, u32[]{:S(2)}) copy-start(bf16[1024,512]{0,1:T(8,128)(2,1)} %copy-done.1) | copy-start | bytes 3145732

commit v7 on v6

--- a/solution.py
+++ b/solution.py
@@ -5,7 +5,7 @@
 
 
 HEAD_DIM = 128
-CHUNKS = 4
+CHUNKS = 1
 
 
 def passed_along(value, axis, steps):
@@ -73,16 +73,18 @@
         return scores, allowed
 
     tops = []
+    sums = []
     for c in range(CHUNKS):
         scores, allowed = chunk_scores(c)
-        tops.append(jnp.max(jnp.where(allowed, scores, -1e30), axis=-1))
+        chunk_top = jnp.max(jnp.where(allowed, scores, -1e30), axis=-1)
+        tops.append(chunk_top)
+        sums.append(jnp.sum(jnp.where(allowed, jnp.exp(scores - chunk_top[..., None]), 0.0), axis=-1))
     top = tops[0]
     for t in tops[1:]:
         top = jnp.maximum(top, t)
     total = jnp.zeros_like(top)
-    for c in range(CHUNKS):
-        scores, allowed = chunk_scores(c)
-        total = total + jnp.sum(jnp.where(allowed, jnp.exp(scores - top[..., None]), 0.0), axis=-1)
+    for chunk_top, chunk_sum in zip(tops, sums):
+        total = total + chunk_sum * jnp.exp(chunk_top - top)
     lse = top + jnp.log(total)
 
     dquery_g = jnp.zeros((groups, per * rows, head_dim), jnp.float32)

time: 156 us -> 157 us (level)
  local copies, waits for them, and re-layouts: 4.68 us -> 13.8 us
  waiting for transfers between devices: 75.6 us -> 66.7 us
  other arithmetic: 6.51 us -> 9.7 us
  matrix products: 18.9 us -> 15.8 us
    ppermute x8, waiting for transfers between devices: 9.6 us -> 2.67 us  [passed_along(): return lax.ppermute(value, axis, pairs)]
    another operation x0 -> x1, local copies, waits for them, and re-layouts: none -> 6.53 us
    all_to_all x1, waiting for transfers between devices: 43.1 us -> 39 us  [section(): lax.all_to_all(dkv.astype(jnp.bfloat16).reshape(count, rows, 2 * kv_width...]
    convert_element_type x0 -> x1, other arithmetic: none -> 3.85 us  [section(): dscore = (prob * (dprob - delta_g[..., None])).astype(jnp.bfloat16)]
    unnamed x40 -> x21, local copies, waits for them, and re-layouts: 1.13 us -> 4.51 us
    dot_general x4 -> x1, matrix products: 5.92 us -> 3.7 us  [section(): jnp.einsum('gmj,jgd->gmd', dscore, k_c, preferred_element_type=jnp.float32)]
    all_to_all x1, waiting for transfers between devices: 22.9 us -> 25.1 us  [section(): lax.all_to_all(jnp.broadcast_to(kv[None], (count,) + kv.shape), 'ctx', 0,...]
    dot_general x4 -> x1, matrix products: 3.84 us -> 4.51 us  [section(): jnp.einsum('gmd,jgd->gmj', do_g, v_c, preferred_element_type=jnp.float32)]
  transfers between devices with their start and end apart: 10 -> 10, of which waited for: 4 -> 4; matrix products, arithmetic and copies ran while one was open for 7% -> 11% of each run, Pallas kernels for 0% -> 0%
where the time goes in v7:
time: 157 us; the launch traced here: 156 us
  waiting for transfers between devices  66.7 us (42%)
  starting transfers between devices  49 us (31%)
  matrix products  15.8 us (10%)
  local copies, waits for them, and re-layouts  13.8 us (9%)
  other arithmetic  9.7 us (6%)
    all_to_all x1, waiting for transfers between devices, section(): lax.all_to_all(dkv.astype(jnp.bfloat16).reshape(count, rows, 2 * kv_width...  39 us
    all_to_all x1, waiting for transfers between devices, section(): lax.all_to_all(jnp.broadcast_to(kv[None], (count,) + kv.shape), 'ctx', 0,...  25.1 us
    ppermute x8, starting transfers between devices, passed_along(): return lax.ppermute(value, axis, pairs)  22.2 us
    all_to_all x1, starting transfers between devices, section(): lax.all_to_all(jnp.broadcast_to(kv[None], (count,) + kv.shape), 'ctx', 0,...  18.9 us
    all_to_all x1, starting transfers between devices, section(): lax.all_to_all(dkv.astype(jnp.bfloat16).reshape(count, rows, 2 * kv_width...  7.95 us
    another operation x1, local copies, waits for them, and re-layouts  6.53 us
    unnamed x21, local copies, waits for them, and re-layouts  4.51 us
    dot_general x1, matrix products, section(): jnp.einsum('gmd,jgd->gmj', do_g, v_c, preferred_element_type=jnp.float32)  4.51 us
  transfers between devices with their start and end apart: 10, of which 4 were waited for; matrix products, arithmetic and copies ran while one was open for 11% of the time, Pallas kernels for 0%

profile of v7, /device:TPU:6, one launch (start us, length us, event | category | flops | bytes accessed | tf_op | source)
XLA Modules:
  0.0 156.1 jit_solution(14099537644654491159)
XLA Ops:
  0.6 5.4 %collective-permute-start = (bf16[16,8192]{1,0:T(8,128)(2,1)}, bf16[16,8192]{1,0:T(8,128)(2,1)S(1)}, u32[]{:S(2)}, u32[]{:S(2)}) collective-permute-start(bf16[16,8192]{1,0:T(8,128)(2,1)} %bitcast.138), channel_id=1, source_target_pairs={{0,896},{128,0},{256,128},{384,256},{512,384},{640,512},{768,640},... | collective-permute-start | bytes 786440 | tf_op jit(solution)/shard_map/ppermute | solution.py:14
  6.0 0.8 pad_maximum_fusion.1
  6.8 0.1 copy.45
  6.9 1.2 broadcast_in_dim.66
  8.1 18.9 %all-to-all-start = ((bf16[16,128,256]{1,2,0:T(8,128)(2,1)}), bf16[16,128,256]{1,2,0:T(8,128)(2,1)S(1)}, u32[]{:S(2)}, u32[]{:S(2)}) async-start(bf16[16,128,256]{1,2,0:T(8,128)(2,1)} %broadcast_in_dim.66), calls=%async_computation | async-start | bytes 2097152 | tf_op jit(solution)/shard_map/all_to_all | solution.py:56
  27.0 0.7 select_reduce_fusion.1
  27.8 0.8 select_reduce_fusion
  28.7 0.0 collective-permute-done
  28.7 0.0 collective-permute-start.1
  28.8 1.1 copy.49
  29.9 0.2 copy.50
  30.1 1.0 copy.62
  31.1 0.2 copy.47
  31.4 0.1 reshape.224
  31.5 2.7 %collective-permute-start.2 = (bf16[16,1024]{1,0:T(8,128)(2,1)S(1)}, bf16[16,1024]{1,0:T(8,128)(2,1)S(1)}, u32[]{:S(2)}, u32[]{:S(2)}) collective-permute-start(bf16[16,1024]{1,0:T(8,128)(2,1)S(1)} %get-tuple-element.23), channel_id=1, source_target_pairs={{0,6},{1,7},{2,0},{3,1},{4,2},{5,3},{6,4},{7,5},{8,14},{9,15},{10,... | collective-permute-start | bytes 98312 | tf_op jit(solution)/shard_map/ppermute | solution.py:14
  34.2 2.8 %collective-permute-start.3 = (bf16[16,1024]{1,0:T(8,128)(2,1)S(1)}, bf16[16,1024]{1,0:T(8,128)(2,1)S(1)}, u32[]{:S(2)}, u32[]{:S(2)}) collective-permute-start(bf16[16,1024]{1,0:T(8,128)(2,1)S(1)} %get-tuple-element.22), channel_id=1, source_target_pairs={{0,5},{1,6},{2,7},{3,0},{4,1},{5,2},{6,3},{7,4},{8,13},{9,14},{10,... | collective-permute-start | bytes 98312 | tf_op jit(solution)/shard_map/ppermute | solution.py:14
  37.1 4.3 %collective-permute-start.4 = (bf16[16,1024]{1,0:T(8,128)(2,1)S(1)}, bf16[16,1024]{1,0:T(8,128)(2,1)S(1)}, u32[]{:S(2)}, u32[]{:S(2)}) collective-permute-start(bf16[16,1024]{1,0:T(8,128)(2,1)S(1)} %get-tuple-element.21), channel_id=1, source_target_pairs={{0,4},{1,5},{2,6},{3,7},{4,0},{5,1},{6,2},{7,3},{8,12},{9,13},{10,... | collective-permute-start | bytes 98312 | tf_op jit(solution)/shard_map/ppermute | solution.py:14
  41.4 3.4 %collective-permute-start.5 = (bf16[16,1024]{1,0:T(8,128)(2,1)S(1)}, bf16[16,1024]{1,0:T(8,128)(2,1)S(1)}, u32[]{:S(2)}, u32[]{:S(2)}) collective-permute-start(bf16[16,1024]{1,0:T(8,128)(2,1)S(1)} %get-tuple-element.20), channel_id=1, source_target_pairs={{0,3},{1,4},{2,5},{3,6},{4,7},{5,0},{6,1},{7,2},{8,11},{9,12},{10,... | collective-permute-start | bytes 98312 | tf_op jit(solution)/shard_map/ppermute | solution.py:14
  44.8 0.0 collective-permute-done.1
  44.8 2.9 %collective-permute-start.6 = (bf16[16,1024]{1,0:T(8,128)(2,1)S(1)}, bf16[16,1024]{1,0:T(8,128)(2,1)S(1)}, u32[]{:S(2)}, u32[]{:S(2)}) collective-permute-start(bf16[16,1024]{1,0:T(8,128)(2,1)S(1)} %get-tuple-element.19), channel_id=1, source_target_pairs={{0,2},{1,3},{2,4},{3,5},{4,6},{5,7},{6,0},{7,1},{8,10},{9,11},{10,... | collective-permute-start | bytes 98312 | tf_op jit(solution)/shard_map/ppermute | solution.py:14
  47.7 0.0 collective-permute-done.2
  47.7 0.6 collective-permute-start.7
  48.3 0.0 collective-permute-done.3
  48.3 0.0 collective-permute-done.4
  48.3 0.0 collective-permute-done.5
  48.4 2.2 %collective-permute-done.6 = bf16[16,1024]{1,0:T(8,128)(2,1)S(1)} collective-permute-done((bf16[16,1024]{1,0:T(8,128)(2,1)S(1)}, bf16[16,1024]{1,0:T(8,128)(2,1)S(1)}, u32[]{:S(2)}, u32[]{:S(2)}) %collective-permute-start.6) | collective-permute-done | bytes 32800 | tf_op jit(solution)/shard_map/ppermute | solution.py:14
  50.6 0.4 collective-permute-done.7
  51.3 0.2 multiply_reduce_fusion
  51.5 25.1 %all-to-all-done = bf16[16,128,256]{1,2,0:T(8,128)(2,1)S(1)} async-done(((bf16[16,128,256]{1,2,0:T(8,128)(2,1)}), bf16[16,128,256]{1,2,0:T(8,128)(2,1)S(1)}, u32[]{:S(2)}, u32[]{:S(2)}) %all-to-all-start) | async-done | bytes 1048608 | tf_op jit(solution)/shard_map/all_to_all | solution.py:56
  76.6 0.2 copy_bitcast_fusion
  76.8 1.6 %fusion = (f32[1024]{0:T(1024)S(1)}, f32[2048,1024]{1,0:T(8,128)S(1)}) fusion(s32[1024]{0:T(1024)S(1)} %broadcast_bitcast_fusion, s32[2048]{0:T(1024)S(1)} %fusion.33, bf16[16,8,8,128]{3,2,1,0:T(8,128)(2,1)S(1)} %bitcast.127, bf16[2048,256]{0,1:T(8,128)(2,1)S(1)} %copy_bitcast_fusion), kind=kOutput, calls=%fused_computation.3 | convolution fusion | flops 545258496 | bytes 9191424 | tf_op jit(solution)/shard_map/gmd,jgd->gmj/dot_general | solution.py:71
  78.4 2.0 %fusion.1 = f32[1024]{0:T(1024)S(1)} fusion(f32[2048,1024]{1,0:T(8,128)S(1)} %get-tuple-element.26, f32[1024]{0:T(1024)S(1)} %get-tuple-element.25, s32[1024]{0:T(1024)S(1)} %broadcast_bitcast_fusion, s32[2048]{0:T(1024)S(1)} %fusion.33), kind=kLoop, calls=%fused_computation.4 | loop fusion | flops 10484736 | bytes 8409088 | tf_op jit(solution)/shard_map/reduce_sum | solution.py:81
  80.4 2.3 %fusion.12 = bf16[2048,1,128]{0,2,1:T(8,128)(2,1)S(1)} fusion(bf16[1024,128]{1,0:T(8,128)(2,1)S(1)} %bitcast.123, f32[2048,1024]{1,0:T(8,128)S(1)} %get-tuple-element.26, f32[1024]{0:T(1024)S(1)} %log_add_fusion, s32[1024]{0:T(1024)S(1)} %broadcast_bitcast_fusion, s32[2048]{0:T(1024)S(1)} %fusion.33), kind=kOutput, calls=%fused_computation.16 | convolution fusion | flops 547618816 | bytes 9191424 | tf_op jit(solution)/shard_map/gmj,gmd->jgd/dot_general | solution.py:99
  82.7 4.5 %multiply_convert_fusion = (bf16[1024,2048]{0,1:T(8,128)(2,1)}, f32[1024,2048]{0,1:T(8,128)S(1)}) fusion(f32[2048,1024]{1,0:T(8,128)S(1)} %get-tuple-element.26, f32[1024]{0:T(1024)S(1)} %bitcast.132, f32[1024]{0:T(1024)S(1)} %log_add_fusion, s32[1024]{0:T(1024)S(1)} %broadcast_bitcast_fusion, s32[2048]{0:T(1024)S(1)} %fusion.33, ...), kind=kOutput, calls=%fused_computation.11 | convolution fusion | flops 551550976 | bytes 21778432 | tf_op jit(solution)/shard_map/gmd,jgd->gmj/dot_general | solution.py:100
  87.2 3.9 %fusion.2 = bf16[2048,1024]{1,0:T(8,128)(2,1)} fusion(f32[1024,2048]{0,1:T(8,128)S(1)} %get-tuple-element.28, f32[2048,1024]{1,0:T(8,128)S(1)} %get-tuple-element.26, f32[1024]{0:T(1024)S(1)} %log_add_fusion, s32[1024]{0:T(1024)S(1)} %broadcast_bitcast_fusion, f32[1024]{0:T(1024)S(1)} %bitcast.133, s32[2048]{0:T(1024)S(1)} %fusion.33), kind=kLoop, calls=%fused_computation.6 | loop fusion | flops 14680064 | bytes 20992000 | tf_op jit(solution)/shard_map/convert_element_type | solution.py:101
  91.1 0.3 copy.54
  91.3 0.3 copy.55
  91.6 3.7 %convolution_convert_fusion = bf16[16,128,128]{1,2,0:T(8,128)(2,1)S(1)} fusion(bf16[16,128,1024]{2,1,0:T(8,128)(2,1)} %bitcast.118, bf16[1024,128,1]{0,1,2:T(8,128)(2,1)S(1)} %reshape.224), kind=kOutput, calls=%fused_computation.18 | convolution fusion | flops 537133056 | bytes 4980736 | tf_op jit(solution)/shard_map/gmj,gmd->jgd/dot_general | solution.py:103
  95.3 1.2 pad_maximum_fusion
  96.5 8.0 %all-to-all-start.1 = ((bf16[16,128,256]{1,2,0:T(8,128)(2,1)}), bf16[16,128,256]{1,2,0:T(8,128)(2,1)S(1)}, u32[]{:S(2)}, u32[]{:S(2)}) async-start(bf16[16,128,256]{1,2,0:T(8,128)(2,1)} %pad_maximum_fusion), calls=%async_computation.1 | async-start | bytes 2097152 | tf_op jit(solution)/shard_map/all_to_all | solution.py:109
  104.4 6.5 %copy.60 = bf16[1024,2048]{1,0:T(8,128)(2,1)} copy(bf16[1024,2048]{0,1:T(8,128)(2,1)} %get-tuple-element.27) | data formatting | bytes 8388608 | tf_op jit(solution)/shard_map/reshape.92
  111.0 3.7 %fusion.15 = bf16[8,128,128]{1,2,0:T(8,128)(2,1)S(1)} fusion(bf16[8,128,2048]{2,1,0:T(8,128)(2,1)} %bitcast.119, bf16[2048,256]{0,1:T(8,128)(2,1)S(1)} %copy_bitcast_fusion), kind=kOutput, calls=%fused_computation.20 | convolution fusion | flops 537133056 | bytes 4980736 | tf_op jit(solution)/shard_map/gmj,jgd->gmd/dot_general | solution.py:102
  114.7 0.9 copy.56
  115.5 39.0 %all-to-all-done.1 = bf16[16,128,256]{1,2,0:T(8,128)(2,1)S(1)} async-done(((bf16[16,128,256]{1,2,0:T(8,128)(2,1)}), bf16[16,128,256]{1,2,0:T(8,128)(2,1)S(1)}, u32[]{:S(2)}, u32[]{:S(2)}) %all-to-all-start.1) | async-done | bytes 1048608 | tf_op jit(solution)/shard_map/all_to_all | solution.py:109
  154.5 0.1 convert_reduce_fusion
  154.7 0.7 copy.57
  155.4 0.7 copy.58
  (29 shorter events, 0.3 us)
Async XLA Ops:
  0.6 28.0 %collective-permute-start = (bf16[16,8192]{1,0:T(8,128)(2,1)}, bf16[16,8192]{1,0:T(8,128)(2,1)S(1)}, u32[]{:S(2)}, u32[]{:S(2)}) collective-permute-start(bf16[16,8192]{1,0:T(8,128)(2,1)} %bitcast.138), channel_id=1, source_target_pairs={{0,896},{128,0},{256,128},{384,256},{512,384},{640,512},{768,640},... | collective-permute-start | bytes 786440 | tf_op jit(solution)/shard_map/ppermute | solution.py:14
  8.1 68.5 %all-to-all-start = ((bf16[16,128,256]{1,2,0:T(8,128)(2,1)}), bf16[16,128,256]{1,2,0:T(8,128)(2,1)S(1)}, u32[]{:S(2)}, u32[]{:S(2)}) async-start(bf16[16,128,256]{1,2,0:T(8,128)(2,1)} %broadcast_in_dim.66), calls=%async_computation | async-start | bytes 2097152 | tf_op jit(solution)/shard_map/all_to_all | solution.py:56
  28.7 16.0 %collective-permute-start.1 = (bf16[16,1024]{1,0:T(8,128)(2,1)S(1)}, bf16[16,1024]{1,0:T(8,128)(2,1)S(1)}, u32[]{:S(2)}, u32[]{:S(2)}) collective-permute-start(bf16[16,1024]{1,0:T(8,128)(2,1)S(1)} %get-tuple-element.24), channel_id=1, source_target_pairs={{0,7},{1,0},{2,1},{3,2},{4,3},{5,4},{6,5},{7,6},{8,15},{9,8},{10,9... | collective-permute-start | bytes 98312 | tf_op jit(solution)/shard_map/ppermute | solution.py:14
  31.5 16.2 %collective-permute-start.2 = (bf16[16,1024]{1,0:T(8,128)(2,1)S(1)}, bf16[16,1024]{1,0:T(8,128)(2,1)S(1)}, u32[]{:S(2)}, u32[]{:S(2)}) collective-permute-start(bf16[16,1024]{1,0:T(8,128)(2,1)S(1)} %get-tuple-element.23), channel_id=1, source_target_pairs={{0,6},{1,7},{2,0},{3,1},{4,2},{5,3},{6,4},{7,5},{8,14},{9,15},{10,... | collective-permute-start | bytes 98312 | tf_op jit(solution)/shard_map/ppermute | solution.py:14
  34.2 14.1 %collective-permute-start.3 = (bf16[16,1024]{1,0:T(8,128)(2,1)S(1)}, bf16[16,1024]{1,0:T(8,128)(2,1)S(1)}, u32[]{:S(2)}, u32[]{:S(2)}) collective-permute-start(bf16[16,1024]{1,0:T(8,128)(2,1)S(1)} %get-tuple-element.22), channel_id=1, source_target_pairs={{0,5},{1,6},{2,7},{3,0},{4,1},{5,2},{6,3},{7,4},{8,13},{9,14},{10,... | collective-permute-start | bytes 98312 | tf_op jit(solution)/shard_map/ppermute | solution.py:14
  37.1 11.3 %collective-permute-start.4 = (bf16[16,1024]{1,0:T(8,128)(2,1)S(1)}, bf16[16,1024]{1,0:T(8,128)(2,1)S(1)}, u32[]{:S(2)}, u32[]{:S(2)}) collective-permute-start(bf16[16,1024]{1,0:T(8,128)(2,1)S(1)} %get-tuple-element.21), channel_id=1, source_target_pairs={{0,4},{1,5},{2,6},{3,7},{4,0},{5,1},{6,2},{7,3},{8,12},{9,13},{10,... | collective-permute-start | bytes 98312 | tf_op jit(solution)/shard_map/ppermute | solution.py:14
  41.4 7.0 %collective-permute-start.5 = (bf16[16,1024]{1,0:T(8,128)(2,1)S(1)}, bf16[16,1024]{1,0:T(8,128)(2,1)S(1)}, u32[]{:S(2)}, u32[]{:S(2)}) collective-permute-start(bf16[16,1024]{1,0:T(8,128)(2,1)S(1)} %get-tuple-element.20), channel_id=1, source_target_pairs={{0,3},{1,4},{2,5},{3,6},{4,7},{5,0},{6,1},{7,2},{8,11},{9,12},{10,... | collective-permute-start | bytes 98312 | tf_op jit(solution)/shard_map/ppermute | solution.py:14
  44.8 5.8 %collective-permute-start.6 = (bf16[16,1024]{1,0:T(8,128)(2,1)S(1)}, bf16[16,1024]{1,0:T(8,128)(2,1)S(1)}, u32[]{:S(2)}, u32[]{:S(2)}) collective-permute-start(bf16[16,1024]{1,0:T(8,128)(2,1)S(1)} %get-tuple-element.19), channel_id=1, source_target_pairs={{0,2},{1,3},{2,4},{3,5},{4,6},{5,7},{6,0},{7,1},{8,10},{9,11},{10,... | collective-permute-start | bytes 98312 | tf_op jit(solution)/shard_map/ppermute | solution.py:14
  47.7 3.4 %collective-permute-start.7 = (bf16[16,1024]{1,0:T(8,128)(2,1)S(1)}, bf16[16,1024]{1,0:T(8,128)(2,1)S(1)}, u32[]{:S(2)}, u32[]{:S(2)}) collective-permute-start(bf16[16,1024]{1,0:T(8,128)(2,1)S(1)} %get-tuple-element.18), channel_id=1, source_target_pairs={{0,1},{1,2},{2,3},{3,4},{4,5},{5,6},{6,7},{7,0},{8,9},{9,10},{10,1... | collective-permute-start | bytes 98312 | tf_op jit(solution)/shard_map/ppermute | solution.py:14
  96.5 58.0 %all-to-all-start.1 = ((bf16[16,128,256]{1,2,0:T(8,128)(2,1)}), bf16[16,128,256]{1,2,0:T(8,128)(2,1)S(1)}, u32[]{:S(2)}, u32[]{:S(2)}) async-start(bf16[16,128,256]{1,2,0:T(8,128)(2,1)} %pad_maximum_fusion), calls=%async_computation.1 | async-start | bytes 2097152 | tf_op jit(solution)/shard_map/all_to_all | solution.py:109

commit v8 on v7

--- a/solution.py
+++ b/solution.py
@@ -5,7 +5,7 @@
 
 
 HEAD_DIM = 128
-CHUNKS = 1
+CHUNKS = 2
 
 
 def passed_along(value, axis, steps):
@@ -74,11 +74,14 @@
 
     tops = []
     sums = []
+    terms = []
     for c in range(CHUNKS):
         scores, allowed = chunk_scores(c)
         chunk_top = jnp.max(jnp.where(allowed, scores, -1e30), axis=-1)
         tops.append(chunk_top)
-        sums.append(jnp.sum(jnp.where(allowed, jnp.exp(scores - chunk_top[..., None]), 0.0), axis=-1))
+        term = jnp.where(allowed, jnp.exp(scores - chunk_top[..., None]), 0.0)
+        terms.append(term)
+        sums.append(jnp.sum(term, axis=-1))
     top = tops[0]
     for t in tops[1:]:
         top = jnp.maximum(top, t)
@@ -91,10 +94,9 @@
     dks = []
     dvs = []
     for c in range(CHUNKS):
-        scores, allowed = chunk_scores(c)
         k_c = k_all[c * width:(c + 1) * width]
         v_c = v_all[c * width:(c + 1) * width]
-        prob = jnp.where(allowed, jnp.exp(scores - lse[..., None]), 0.0)
+        prob = terms[c] * jnp.exp(tops[c] - lse)[..., None]
         prob_b = prob.astype(jnp.bfloat16)
         dvalue = jnp.einsum("gmj,gmd->jgd", prob_b, do_g, preferred_element_type=jnp.float32)
         dprob = jnp.einsum("gmd,jgd->gmj", do_g, v_c, preferred_element_type=jnp.float32)

time: 157 us -> 153 us (0.975)
  local copies, waits for them, and re-layouts: 13.8 us -> 4.03 us
  waiting for transfers between devices: 66.7 us -> 76.3 us
  other arithmetic: 9.7 us -> 6.53 us
    ppermute x8, waiting for transfers between devices: 2.67 us -> 9.6 us  [passed_along(): return lax.ppermute(value, axis, pairs)]
    another operation x1 -> x0, local copies, waits for them, and re-layouts: 6.53 us -> none
    all_to_all x1, waiting for transfers between devices: 39 us -> 45.1 us  [section(): lax.all_to_all(dkv.astype(jnp.bfloat16).reshape(count, rows, 2 * kv_width...]
    unnamed x21 -> x30, local copies, waits for them, and re-layouts: 4.51 us -> 0.49 us
    convert_element_type x1 -> x0, other arithmetic: 3.85 us -> none  [section(): dscore = (prob * (dprob - delta_g[..., None])).astype(jnp.bfloat16)]
    all_to_all x1, waiting for transfers between devices: 25.1 us -> 21.6 us  [section(): lax.all_to_all(jnp.broadcast_to(kv[None], (count,) + kv.shape), 'ctx', 0,...]
    dot_general x1 -> x2, matrix products: 3.7 us -> 2.85 us  [section(): jnp.einsum('gmj,gmd->jgd', dscore, q_g, preferred_element_type=jnp.float32)]
    dot_general x1 -> x2, matrix products: 3.7 us -> 4.02 us  [section(): jnp.einsum('gmj,jgd->gmd', dscore, k_c, preferred_element_type=jnp.float32)]
  transfers between devices with their start and end apart: 10 -> 10, of which waited for: 4 -> 4; matrix products, arithmetic and copies ran while one was open for 11% -> 6% of each run, Pallas kernels for 0% -> 0%
where the time goes in v8:
time: 153 us; the launch traced here: 152 us
  waiting for transfers between devices  76.3 us (50%)
  starting transfers between devices  47.5 us (31%)
  matrix products  16.5 us (11%)
  other arithmetic  6.53 us (4%)
  local copies, waits for them, and re-layouts  4.03 us (3%)
    all_to_all x1, waiting for transfers between devices, section(): lax.all_to_all(dkv.astype(jnp.bfloat16).reshape(count, rows, 2 * kv_width...  45.1 us
    all_to_all x1, waiting for transfers between devices, section(): lax.all_to_all(jnp.broadcast_to(kv[None], (count,) + kv.shape), 'ctx', 0,...  21.6 us
    ppermute x8, starting transfers between devices, passed_along(): return lax.ppermute(value, axis, pairs)  20.7 us
    all_to_all x1, starting transfers between devices, section(): lax.all_to_all(jnp.broadcast_to(kv[None], (count,) + kv.shape), 'ctx', 0,...  18.9 us
    ppermute x8, waiting for transfers between devices, passed_along(): return lax.ppermute(value, axis, pairs)  9.6 us
    all_to_all x1, starting transfers between devices, section(): lax.all_to_all(dkv.astype(jnp.bfloat16).reshape(count, rows, 2 * kv_width...  7.94 us
    dot_general x2, matrix products, section(): jnp.einsum('gmd,jgd->gmj', do_g, v_c, preferred_element_type=jnp.float32)  4.4 us
    dot_general x2, matrix products, section(): jnp.einsum('gmj,jgd->gmd', dscore, k_c, preferred_element_type=jnp.float32)  4.02 us
  transfers between devices with their start and end apart: 10, of which 4 were waited for; matrix products, arithmetic and copies ran while one was open for 6% of the time, Pallas kernels for 0%

profile of v8, /device:TPU:6, one launch (start us, length us, event | category | flops | bytes accessed | tf_op | source)
XLA Modules:
  0.0 152.1 jit_solution(11059279033169888045)
XLA Ops:
  0.6 0.0 copy-start.2
  0.6 0.0 copy-start.3
  0.7 5.5 %collective-permute-start = (bf16[16,8192]{1,0:T(8,128)(2,1)}, bf16[16,8192]{1,0:T(8,128)(2,1)S(1)}, u32[]{:S(2)}, u32[]{:S(2)}) collective-permute-start(bf16[16,8192]{1,0:T(8,128)(2,1)} %bitcast.143), channel_id=1, source_target_pairs={{0,896},{128,0},{256,128},{384,256},{512,384},{640,512},{768,640},... | collective-permute-start | bytes 786440 | tf_op jit(solution)/shard_map/ppermute | solution.py:14
  6.2 0.8 pad_maximum_fusion.3
  7.0 1.1 broadcast_in_dim.68
  8.0 18.9 %all-to-all-start = ((bf16[16,128,256]{2,1,0:T(8,128)(2,1)}), bf16[16,128,256]{2,1,0:T(8,128)(2,1)S(1)}, u32[]{:S(2)}, u32[]{:S(2)}) async-start(bf16[16,128,256]{2,1,0:T(8,128)(2,1)} %broadcast_in_dim.68), calls=%async_computation | async-start | bytes 2097152 | tf_op jit(solution)/shard_map/all_to_all | solution.py:56
  27.0 0.7 select_reduce_fusion.1
  27.7 0.8 select_reduce_fusion
  28.6 0.0 collective-permute-done
  28.7 0.0 collective-permute-start.1
  28.7 0.0 copy-done.2
  28.7 0.2 copy.36
  28.9 0.2 copy.37
  29.1 0.0 copy-done.3
  29.1 0.2 copy.39
  29.3 0.2 copy.40
  29.5 0.5 collective-permute-start.7
  30.0 3.5 %collective-permute-start.6 = (bf16[16,1024]{1,0:T(8,128)(2,1)S(1)}, bf16[16,1024]{1,0:T(8,128)(2,1)S(1)}, u32[]{:S(2)}, u32[]{:S(2)}) collective-permute-start(bf16[16,1024]{1,0:T(8,128)(2,1)S(1)} %get-tuple-element.6), channel_id=1, source_target_pairs={{0,2},{1,3},{2,4},{3,5},{4,6},{5,7},{6,0},{7,1},{8,10},{9,11},{10,... | collective-permute-start | bytes 98312 | tf_op jit(solution)/shard_map/ppermute | solution.py:14
  33.5 2.7 %collective-permute-start.5 = (bf16[16,1024]{1,0:T(8,128)(2,1)S(1)}, bf16[16,1024]{1,0:T(8,128)(2,1)S(1)}, u32[]{:S(2)}, u32[]{:S(2)}) collective-permute-start(bf16[16,1024]{1,0:T(8,128)(2,1)S(1)} %get-tuple-element.7), channel_id=1, source_target_pairs={{0,3},{1,4},{2,5},{3,6},{4,7},{5,0},{6,1},{7,2},{8,11},{9,12},{10,... | collective-permute-start | bytes 98312 | tf_op jit(solution)/shard_map/ppermute | solution.py:14
  36.2 4.6 %collective-permute-start.4 = (bf16[16,1024]{1,0:T(8,128)(2,1)S(1)}, bf16[16,1024]{1,0:T(8,128)(2,1)S(1)}, u32[]{:S(2)}, u32[]{:S(2)}) collective-permute-start(bf16[16,1024]{1,0:T(8,128)(2,1)S(1)} %get-tuple-element.8), channel_id=1, source_target_pairs={{0,4},{1,5},{2,6},{3,7},{4,0},{5,1},{6,2},{7,3},{8,12},{9,13},{10,... | collective-permute-start | bytes 98312 | tf_op jit(solution)/shard_map/ppermute | solution.py:14
  40.8 0.0 collective-permute-done.1
  40.9 1.9 %collective-permute-start.2 = (bf16[16,1024]{1,0:T(8,128)(2,1)S(1)}, bf16[16,1024]{1,0:T(8,128)(2,1)S(1)}, u32[]{:S(2)}, u32[]{:S(2)}) collective-permute-start(bf16[16,1024]{1,0:T(8,128)(2,1)S(1)} %get-tuple-element.10), channel_id=1, source_target_pairs={{0,6},{1,7},{2,0},{3,1},{4,2},{5,3},{6,4},{7,5},{8,14},{9,15},{10,... | collective-permute-start | bytes 98312 | tf_op jit(solution)/shard_map/ppermute | solution.py:14
  42.8 5.1 %collective-permute-done.2 = bf16[16,1024]{1,0:T(8,128)(2,1)S(1)} collective-permute-done((bf16[16,1024]{1,0:T(8,128)(2,1)S(1)}, bf16[16,1024]{1,0:T(8,128)(2,1)S(1)}, u32[]{:S(2)}, u32[]{:S(2)}) %collective-permute-start.2) | collective-permute-done | bytes 32800 | tf_op jit(solution)/shard_map/ppermute | solution.py:14
  47.9 1.9 %collective-permute-start.3 = (bf16[16,1024]{1,0:T(8,128)(2,1)S(1)}, bf16[16,1024]{1,0:T(8,128)(2,1)S(1)}, u32[]{:S(2)}, u32[]{:S(2)}) collective-permute-start(bf16[16,1024]{1,0:T(8,128)(2,1)S(1)} %get-tuple-element.9), channel_id=1, source_target_pairs={{0,5},{1,6},{2,7},{3,0},{4,1},{5,2},{6,3},{7,4},{8,13},{9,14},{10,... | collective-permute-start | bytes 98312 | tf_op jit(solution)/shard_map/ppermute | solution.py:14
  49.8 4.5 %collective-permute-done.3 = bf16[16,1024]{1,0:T(8,128)(2,1)S(1)} collective-permute-done((bf16[16,1024]{1,0:T(8,128)(2,1)S(1)}, bf16[16,1024]{1,0:T(8,128)(2,1)S(1)}, u32[]{:S(2)}, u32[]{:S(2)}) %collective-permute-start.3) | collective-permute-done | bytes 32800 | tf_op jit(solution)/shard_map/ppermute | solution.py:14
  54.3 0.0 collective-permute-done.4
  54.3 0.0 collective-permute-done.5
  54.3 0.0 collective-permute-done.6
  54.4 0.0 collective-permute-done.7
  54.6 0.2 multiply_reduce_fusion
  54.9 0.1 copy.38
  54.9 0.0 copy-start.4
  55.0 21.6 %all-to-all-done = bf16[16,128,256]{2,1,0:T(8,128)(2,1)S(1)} async-done(((bf16[16,128,256]{2,1,0:T(8,128)(2,1)}), bf16[16,128,256]{2,1,0:T(8,128)(2,1)S(1)}, u32[]{:S(2)}, u32[]{:S(2)}) %all-to-all-start) | async-done | bytes 1048608 | tf_op jit(solution)/shard_map/all_to_all | solution.py:56
  76.6 0.0 copy-start.1
  76.6 0.8 fusion
  77.3 1.8 %fusion.37 = (f32[1024]{0:T(1024)S(1)}, f32[1024]{0:T(1024)S(1)}, f32[1024,1024]{1,0:T(8,128)S(1)}) fusion(f32[1024]{0:T(1024)S(1)} %get-tuple-element.16, f32[1024,1024]{1,0:T(8,128)S(1)} %get-tuple-element.17, s32[1024]{0:T(1024)S(1)} %broadcast_bitcast_fusion, s32[1024]{0:T(1024)S(1)} %get-tuple-element.15, s32[1024]{0:T(1024)S(1)} %get-tuple-element.14, ...), kind=kOutput, calls=%fused_computation.101 | convolution fusion | flops 277870592 | bytes 8937472 | tf_op jit(solution)/shard_map/gmd,jgd->gmj/dot_general | solution.py:71
  79.1 1.0 fusion.38
  80.1 0.0 copy-done.4
  80.1 1.4 fusion.13
  81.5 0.0 copy-start.5
  81.5 2.7 %multiply_convert_fusion = bf16[1024,1024]{0,1:T(8,128)(2,1)S(1)} fusion(bf16[1024,128]{1,0:T(8,128)(2,1)} %bitcast.133, f32[1024]{0:T(1024)S(1)} %get-tuple-element.12, f32[1024]{0:T(1024)S(1)} %bitcast.139, bf16[2048,256]{1,0:T(8,128)(2,1)S(1)} %bitcast.122, f32[1024]{0:T(1024)S(1)} %get-tuple-element.4, f32[1024,1024]{1,0:T(8,128)S(1)} %get-tuple-element.18, ...), kind=kOutput, calls=%fused_computation.10 | convolution fusion | flops 276824064 | bytes 6836224 | tf_op jit(solution)/shard_map/gmd,jgd->gmj/dot_general | solution.py:102
  84.2 0.0 copy-done.5
  84.2 1.3 fusion.12
  85.6 0.0 copy-done.1
  85.6 1.7 %multiply_convert_fusion.1 = bf16[1024,1024]{0,1:T(8,128)(2,1)S(1)} fusion(bf16[1024,128]{1,0:T(8,128)(2,1)S(1)} %bitcast.135, f32[1024]{0:T(1024)S(1)} %bitcast.140, f32[1024]{0:T(1024)S(1)} %get-tuple-element.13, bf16[2048,256]{1,0:T(8,128)(2,1)S(1)} %bitcast.123, f32[1024]{0:T(1024)S(1)} %get-tuple-element.16, f32[1024,1024]{1,0:T(8,128)S(1)} %get-tuple-element.17, ...), kind=kOutput, calls=%fused_computation.11 | convolution fusion | flops 276824064 | bytes 6836224 | tf_op jit(solution)/shard_map/gmd,jgd->gmj/dot_general | solution.py:102
  87.3 0.0 copy-start
  87.3 1.4 convolution_convert_fusion
  88.7 0.0 copy-done
  88.7 1.4 convolution_convert_fusion.1
  90.2 0.3 copy.48
  90.5 1.1 pad_maximum_fusion.1
  91.5 1.1 pad_maximum_fusion
  92.7 7.9 %all-to-all-start.1 = ((bf16[16,128,256]{2,1,0:T(8,128)(2,1)}), bf16[16,128,256]{2,1,0:T(8,128)(2,1)S(1)}, u32[]{:S(2)}, u32[]{:S(2)}) async-start(bf16[16,128,256]{2,1,0:T(8,128)(2,1)} %pad_maximum_fusion), calls=%async_computation.1 | async-start | bytes 2097152 | tf_op jit(solution)/shard_map/all_to_all | solution.py:111
  100.6 2.3 %fusion.19 = f32[1024,128]{1,0:T(8,128)S(1)} fusion(bf16[1024,1024]{0,1:T(8,128)(2,1)} %copy-done, bf16[2048,256]{1,0:T(8,128)(2,1)} %bitcast.124), kind=kOutput, calls=%fused_computation.39 | convolution fusion | flops 268435456 | bytes 2883584 | tf_op jit(solution)/shard_map/gmj,jgd->gmd/dot_general | solution.py:104
  102.9 1.7 %fusion.9 = bf16[1024,128]{1,0:T(8,128)(2,1)S(1)} fusion(f32[1024,128]{1,0:T(8,128)S(1)} %fusion.19, bf16[1024,1024]{0,1:T(8,128)(2,1)S(1)} %multiply_convert_fusion, bf16[2048,256]{1,0:T(8,128)(2,1)} %bitcast.125), kind=kOutput, calls=%fused_computation.21 | convolution fusion | flops 268828672 | bytes 3145728 | tf_op jit(solution)/shard_map/gmj,jgd->gmd/dot_general | solution.py:104
  104.6 0.2 copy.44
  104.8 0.8 convert_element_type.85
  105.6 45.1 %all-to-all-done.1 = bf16[16,128,256]{2,1,0:T(8,128)(2,1)S(1)} async-done(((bf16[16,128,256]{2,1,0:T(8,128)(2,1)}), bf16[16,128,256]{2,1,0:T(8,128)(2,1)S(1)}, u32[]{:S(2)}, u32[]{:S(2)}) %all-to-all-start.1) | async-done | bytes 1048608 | tf_op jit(solution)/shard_map/all_to_all | solution.py:111
  150.7 0.1 convert_reduce_fusion
  150.9 0.6 fusion.25
  151.5 0.6 fusion.24
  (28 shorter events, 0.3 us)
Async XLA Ops:
  0.6 28.1 %copy-start.2 = (bf16[1,128,1024]{2,1,0:T(8,128)(2,1)S(1)}, bf16[1,128,1024]{2,1,0:T(8,128)(2,1)}, u32[]{:S(2)}) copy-start(bf16[1,128,1024]{2,1,0:T(8,128)(2,1)} %param.6) | copy-start | bytes 786436
  0.6 28.4 %copy-start.3 = (bf16[1,128,1024]{2,1,0:T(8,128)(2,1)S(1)}, bf16[1,128,1024]{2,1,0:T(8,128)(2,1)}, u32[]{:S(2)}) copy-start(bf16[1,128,1024]{2,1,0:T(8,128)(2,1)} %param.9) | copy-start | bytes 786436
  0.7 28.0 %collective-permute-start = (bf16[16,8192]{1,0:T(8,128)(2,1)}, bf16[16,8192]{1,0:T(8,128)(2,1)S(1)}, u32[]{:S(2)}, u32[]{:S(2)}) collective-permute-start(bf16[16,8192]{1,0:T(8,128)(2,1)} %bitcast.143), channel_id=1, source_target_pairs={{0,896},{128,0},{256,128},{384,256},{512,384},{640,512},{768,640},... | collective-permute-start | bytes 786440 | tf_op jit(solution)/shard_map/ppermute | solution.py:14
  8.0 68.5 %all-to-all-start = ((bf16[16,128,256]{2,1,0:T(8,128)(2,1)}), bf16[16,128,256]{2,1,0:T(8,128)(2,1)S(1)}, u32[]{:S(2)}, u32[]{:S(2)}) async-start(bf16[16,128,256]{2,1,0:T(8,128)(2,1)} %broadcast_in_dim.68), calls=%async_computation | async-start | bytes 2097152 | tf_op jit(solution)/shard_map/all_to_all | solution.py:56
  28.7 12.2 %collective-permute-start.1 = (bf16[16,1024]{1,0:T(8,128)(2,1)S(1)}, bf16[16,1024]{1,0:T(8,128)(2,1)S(1)}, u32[]{:S(2)}, u32[]{:S(2)}) collective-permute-start(bf16[16,1024]{1,0:T(8,128)(2,1)S(1)} %get-tuple-element.11), channel_id=1, source_target_pairs={{0,7},{1,0},{2,1},{3,2},{4,3},{5,4},{6,5},{7,6},{8,15},{9,8},{10,9... | collective-permute-start | bytes 98312 | tf_op jit(solution)/shard_map/ppermute | solution.py:14
  29.5 24.9 %collective-permute-start.7 = (bf16[16,1024]{1,0:T(8,128)(2,1)S(1)}, bf16[16,1024]{1,0:T(8,128)(2,1)S(1)}, u32[]{:S(2)}, u32[]{:S(2)}) collective-permute-start(bf16[16,1024]{1,0:T(8,128)(2,1)S(1)} %get-tuple-element.5), channel_id=1, source_target_pairs={{0,1},{1,2},{2,3},{3,4},{4,5},{5,6},{6,7},{7,0},{8,9},{9,10},{10,1... | collective-permute-start | bytes 98312 | tf_op jit(solution)/shard_map/ppermute | solution.py:14
  30.0 24.4 %collective-permute-start.6 = (bf16[16,1024]{1,0:T(8,128)(2,1)S(1)}, bf16[16,1024]{1,0:T(8,128)(2,1)S(1)}, u32[]{:S(2)}, u32[]{:S(2)}) collective-permute-start(bf16[16,1024]{1,0:T(8,128)(2,1)S(1)} %get-tuple-element.6), channel_id=1, source_target_pairs={{0,2},{1,3},{2,4},{3,5},{4,6},{5,7},{6,0},{7,1},{8,10},{9,11},{10,... | collective-permute-start | bytes 98312 | tf_op jit(solution)/shard_map/ppermute | solution.py:14
  33.5 20.8 %collective-permute-start.5 = (bf16[16,1024]{1,0:T(8,128)(2,1)S(1)}, bf16[16,1024]{1,0:T(8,128)(2,1)S(1)}, u32[]{:S(2)}, u32[]{:S(2)}) collective-permute-start(bf16[16,1024]{1,0:T(8,128)(2,1)S(1)} %get-tuple-element.7), channel_id=1, source_target_pairs={{0,3},{1,4},{2,5},{3,6},{4,7},{5,0},{6,1},{7,2},{8,11},{9,12},{10,... | collective-permute-start | bytes 98312 | tf_op jit(solution)/shard_map/ppermute | solution.py:14
  36.2 18.1 %collective-permute-start.4 = (bf16[16,1024]{1,0:T(8,128)(2,1)S(1)}, bf16[16,1024]{1,0:T(8,128)(2,1)S(1)}, u32[]{:S(2)}, u32[]{:S(2)}) collective-permute-start(bf16[16,1024]{1,0:T(8,128)(2,1)S(1)} %get-tuple-element.8), channel_id=1, source_target_pairs={{0,4},{1,5},{2,6},{3,7},{4,0},{5,1},{6,2},{7,3},{8,12},{9,13},{10,... | collective-permute-start | bytes 98312 | tf_op jit(solution)/shard_map/ppermute | solution.py:14
  40.9 7.0 %collective-permute-start.2 = (bf16[16,1024]{1,0:T(8,128)(2,1)S(1)}, bf16[16,1024]{1,0:T(8,128)(2,1)S(1)}, u32[]{:S(2)}, u32[]{:S(2)}) collective-permute-start(bf16[16,1024]{1,0:T(8,128)(2,1)S(1)} %get-tuple-element.10), channel_id=1, source_target_pairs={{0,6},{1,7},{2,0},{3,1},{4,2},{5,3},{6,4},{7,5},{8,14},{9,15},{10,... | collective-permute-start | bytes 98312 | tf_op jit(solution)/shard_map/ppermute | solution.py:14
  47.9 6.4 %collective-permute-start.3 = (bf16[16,1024]{1,0:T(8,128)(2,1)S(1)}, bf16[16,1024]{1,0:T(8,128)(2,1)S(1)}, u32[]{:S(2)}, u32[]{:S(2)}) collective-permute-start(bf16[16,1024]{1,0:T(8,128)(2,1)S(1)} %get-tuple-element.9), channel_id=1, source_target_pairs={{0,5},{1,6},{2,7},{3,0},{4,1},{5,2},{6,3},{7,4},{8,13},{9,14},{10,... | collective-permute-start | bytes 98312 | tf_op jit(solution)/shard_map/ppermute | solution.py:14
  54.9 25.2 %copy-start.4 = (bf16[1,8,128,128]{3,2,1,0:T(8,128)(2,1)}, bf16[1,8,128,128]{3,2,1,0:T(8,128)(2,1)S(1)}, u32[]{:S(2)}) copy-start(bf16[1,8,128,128]{3,2,1,0:T(8,128)(2,1)S(1)} %copy.38) | copy-start | bytes 786436
  76.6 9.0 %copy-start.1 = (bf16[16,128,256]{2,1,0:T(8,128)(2,1)}, bf16[16,128,256]{2,1,0:T(8,128)(2,1)S(1)}, u32[]{:S(2)}) copy-start(bf16[16,128,256]{2,1,0:T(8,128)(2,1)S(1)} %all-to-all-done) | copy-start | bytes 3145732
  81.5 2.7 %copy-start.5 = (bf16[1,8,128,128]{3,2,1,0:T(8,128)(2,1)S(1)}, bf16[1,8,128,128]{3,2,1,0:T(8,128)(2,1)}, u32[]{:S(2)}) copy-start(bf16[1,8,128,128]{3,2,1,0:T(8,128)(2,1)} %copy-done.4) | copy-start | bytes 786436
  87.3 1.4 copy-start
  92.7 58.0 %all-to-all-start.1 = ((bf16[16,128,256]{2,1,0:T(8,128)(2,1)}), bf16[16,128,256]{2,1,0:T(8,128)(2,1)S(1)}, u32[]{:S(2)}, u32[]{:S(2)}) async-start(bf16[16,128,256]{2,1,0:T(8,128)(2,1)} %pad_maximum_fusion), calls=%async_computation.1 | async-start | bytes 2097152 | tf_op jit(solution)/shard_map/all_to_all | solution.py:111
